TPU v7x, 512 devices: a whole 4x8x8 slice. The times are simulated.
512 devices in a mesh: gx: 32 (over y, x), ga: 16 (over z, core).
Axes of the slice: x: 4, y: 8, z: 8, core: 2. Of those that a mesh axis runs over, the one named last changes fastest.
Arguments:
- velocity: float32 [3, 128, 384, 768], P(None, 'gx', 'ga'), may hold values from -6 to 6
- accumulated: float32 [3, 128, 384, 768], P(None, 'gx', 'ga'), may hold values from -6 to 6
- wall_first: float32 [384, 384], replicated, may hold values from -0.3125 to 0.3125
- wall_second: float32 [384, 384], replicated, may hold values from -0.3125 to 0.3125
- recycle_rows: int32 [384], replicated, may hold values from 0 to 382
- weight_index: int32 [384], replicated, may hold values from 0 to 63
- weight_table: float32 [64], replicated, may hold values from 0 to 1
Outputs:
- velocity_next: float32 [3, 128, 384, 768], P(None, 'gx', 'ga')
- accumulated_next: float32 [3, 128, 384, 768], P(None, 'gx', 'ga')
Inputs may be any that keep to these rules, and one draw needn't show every extreme that they name: `recycle_rows`: each entry names the lower of two adjacent recycle-plane rows. `weight_index`: each entry names one entry of weight_table.
All inputs are finite; a program needn't handle non-finite values.
Results may differ from a plain program's by a relative error of at most 0.0001.
Values sent between devices are 32-bit elements; how exact they have to be, the bound alone decides.
No kernel may reach another device: no remote copies, remote signals or barrier semaphores. Data moves between devices by JAX's collectives and lax.ppermute only.
A program may use at most 64 MiB of HBM per device.

v0:
```python
import math

import numpy as np
import jax
import jax.numpy as jnp
from jax import lax
from jax.sharding import PartitionSpec as P

HALO = 4
RECYCLE_PLANE = 124


first_coef = (0.8, -0.2, 4.0 / 105.0, -1.0 / 280.0)
second_coef = (1.6, -0.2, 8.0 / 315.0, -1.0 / 560.0)
center_coef = -205.0 / 72.0
step_size = 0.2
viscosity = 0.2
keep_rate = -5.0 / 9.0
update_rate = 15.0 / 16.0
HIGHEST = lax.Precision.HIGHEST


def spanwise_table(length):
    places = np.arange(length)
    apart = places[None, :] - places[:, None]
    apart = np.remainder(apart + length // 2, length) - length // 2
    parity = 1.0 - 2.0 * np.remainder(apart, 2)
    spacing = 2.0 * math.pi / length
    angle = apart * (0.5 * spacing)
    same = apart == 0
    safe_sine = np.where(same, 1.0, np.sin(angle))
    first = np.where(same, 0.0, 0.5 * spacing * parity * np.cos(angle) / safe_sine)
    second = np.where(
        same,
        -math.pi * math.pi / 3.0 - spacing * spacing / 6.0,
        -0.5 * spacing * spacing * parity / (safe_sine * safe_sine),
    )
    return np.concatenate([first, second], 1).astype(np.float32)


def ghost_weights(planes):
    lower = [sum(first_coef[m - 1] for m in range(x + 1, HALO + 1)) for x in range(planes)]
    upper = [sum(second_coef[m - 1] for m in range(x + 1, HALO + 1)) for x in range(planes)]
    return np.asarray(lower, np.float32), np.asarray(upper, np.float32)


def streamwise(field):
    count = lax.axis_size("gx")
    extent = field.shape[1]
    behind = lax.ppermute(field, "gx", [(i, i + 1) for i in range(count - 1)])
    ahead = lax.ppermute(field, "gx", [(i + 1, i) for i in range(count - 1)])
    at_outlet = lax.axis_index("gx") == count - 1
    ahead = jnp.where(at_outlet, jnp.broadcast_to(field[:, -1:], ahead.shape), ahead)
    padded = jnp.concatenate([behind[:, extent - HALO :], field, ahead[:, :HALO]], 1)
    first = jnp.zeros_like(field)
    second = center_coef * field
    for offset in range(1, HALO + 1):
        up = padded[:, HALO + offset : HALO + offset + extent]
        down = padded[:, HALO - offset : HALO - offset + extent]
        first = first + first_coef[offset - 1] * (up - down)
        second = second + second_coef[offset - 1] * (up + down)
    return -(field[0:1] * first) + viscosity * second


def interpolation_matrix(recycle_rows, weight_index, weight_table, rows):
    levels = jnp.arange(weight_table.shape[0], dtype=jnp.int32)
    frac = jnp.sum(
        jnp.where(weight_index[:, None] == levels[None, :], weight_table[None, :], 0.0), axis=1
    )[:, None]
    places = jnp.arange(rows, dtype=jnp.int32)[None, :]
    lower = jnp.where(places == recycle_rows[:, None], 1.0 - frac, 0.0)
    upper = jnp.where(places == recycle_rows[:, None] + 1, frac, 0.0)
    return lower + upper


def shards(
    velocity, accumulated, wall_first, wall_second, recycle_rows, weight_index, weight_table
):
    comps, planes, rows_here, span = velocity.shape
    parts = lax.axis_size("ga")
    slabs = lax.axis_size("gx")
    share = span // parts
    rows = rows_here * parts
    width = comps * planes * share

    send = velocity.reshape(comps, planes, rows_here, parts, share)
    send = send.transpose(3, 2, 0, 1, 4).reshape(parts, rows_here, width)
    cols = lax.all_to_all(send, "ga", 0, 0, tiled=True).reshape(rows, width)
    grid = cols.reshape(rows, comps, planes, share)

    source_slab, source_plane = divmod(RECYCLE_PLANE, planes)
    mix = interpolation_matrix(recycle_rows, weight_index, weight_table, rows)
    plane = grid[:, :, source_plane, :].reshape(rows, comps * share)
    inflow = jnp.dot(mix, plane, precision=HIGHEST, preferred_element_type=jnp.float32)
    inflow = lax.ppermute(inflow, "gx", [(source_slab, 0)]).reshape(rows, comps, 1, share)

    both = jnp.concatenate([wall_first, wall_second], 0)
    derived = jnp.dot(both, cols, precision=HIGHEST, preferred_element_type=jnp.float32)
    normal_first = derived[:rows].reshape(rows, comps, planes, share)
    normal_second = derived[rows:].reshape(rows, comps, planes, share)
    wall = -(grid[:, 1:2] * normal_first) + viscosity * normal_second

    lower, upper = ghost_weights(planes)
    ghost = inflow * (grid[:, 0:1] * lower[None, None, :, None] + viscosity * upper[None, None, :, None])
    wall = wall + jnp.where(lax.axis_index("gx") == 0, ghost, 0.0)

    back = lax.all_to_all(wall.reshape(parts, rows_here, width), "ga", 0, 0, tiled=True)
    back = back.reshape(parts, rows_here, comps, planes, share).transpose(2, 3, 1, 0, 4)
    back = back.reshape(comps, planes, rows_here, span)

    lines = velocity.reshape(-1, span)
    spectral = jnp.dot(
        lines,
        jnp.asarray(spanwise_table(span)),
        precision=HIGHEST,
        preferred_element_type=jnp.float32,
    )
    span_first = spectral[:, :span].reshape(velocity.shape)
    span_second = spectral[:, span:].reshape(velocity.shape)

    tendency = -(velocity[2:3] * span_first) + viscosity * span_second
    tendency = tendency + streamwise(velocity)
    tendency = tendency + back
    accumulated_next = keep_rate * accumulated + step_size * tendency
    return (velocity + update_rate * accumulated_next, accumulated_next)


def solution(mesh):
    in_specs = (P(None, "gx", "ga", None), P(None, "gx", "ga", None), P(), P(), P(), P(), P())
    out_specs = (P(None, "gx", "ga", None), P(None, "gx", "ga", None))
    return jax.shard_map(shards, mesh=mesh, in_specs=in_specs, out_specs=out_specs, check_vma=False)
```

profile of v0, /device:TPU:1, one launch (start us, length us, event | category | flops | bytes accessed | tf_op | source)
XLA Modules:
  0.0 121.5 jit_solution(13695308662174063801)
XLA Ops:
  0.6 3.3 %reshape.62 = f32[3,4,24,16,48]{4,3,2,1,0:T(8,128)} reshape(f32[3,4,24,768]{3,2,1,0:T(8,128)} %param.10) | data formatting | bytes 1769472 | tf_op jit(solution)/shard_map/reshape | solution.py:86
  3.9 3.2 %copy.31 = f32[3,4,24,16,48]{4,1,0,2,3:T(4,128)S(1)} copy(f32[3,4,24,16,48]{4,3,2,1,0:T(8,128)} %reshape.62) | data formatting | bytes 1769472 | tf_op jit(solution)/shard_map/reshape | solution.py:86
  7.1 2.1 %reshape.63 = f32[16,24,576]{2,1,0:T(8,128)} reshape(f32[16,24,3,4,48]{4,3,2,1,0:T(4,128)S(1)} %bitcast.33) | data formatting | bytes 1769472 | tf_op jit(solution)/shard_map/reshape | solution.py:87
  9.2 12.0 %all-to-all-start = ((f32[16,24,576]{2,1,0:T(8,128)}), f32[16,24,576]{2,1,0:T(8,128)S(1)}, u32[]{:S(2)}, u32[]{:S(2)}) async-start(f32[16,24,576]{2,1,0:T(8,128)} %reshape.63), calls=%async_computation | async-start | bytes 1966080 | tf_op jit(solution)/shard_map/all_to_all | solution.py:88
  21.2 4.1 %collective-permute-start.1 = (f32[3,4,24,768]{3,2,1,0:T(8,128)S(1)}, f32[3,4,24,768]{3,2,1,0:T(8,128)}, u32[]{:S(2)}, u32[]{:S(2)}) collective-permute-start(f32[3,4,24,768]{3,2,1,0:T(8,128)S(1)} %copy-done), channel_id=1, source_target_pairs={{0,16},{16,32},{32,48},{48,64},{64,80},{80,96},{96,112},{112,128},... | collective-permute-start | bytes 2654216 | tf_op jit(solution)/shard_map/ppermute | solution.py:50
  26.8 21.1 %all-to-all-done = f32[16,24,576]{2,1,0:T(8,128)S(1)} async-done(((f32[16,24,576]{2,1,0:T(8,128)}), f32[16,24,576]{2,1,0:T(8,128)S(1)}, u32[]{:S(2)}, u32[]{:S(2)}) %all-to-all-start) | async-done | bytes 884768 | tf_op jit(solution)/shard_map/all_to_all | solution.py:88
  47.8 2.7 %reshape_reshape.3 = f32[384,3,4,48]{3,2,1,0:T(4,128)} reshape(f32[16,24,576]{2,1,0:T(8,128)S(1)} %all-to-all-done) | data formatting | bytes 1769472 | tf_op jit(solution)/shard_map/reshape;reshape | solution.py:89
  50.6 2.1 %slice.82 = f32[384,3,1,48]{3,2,1,0:T(1,128)S(1)} slice(f32[384,3,4,48]{3,2,1,0:T(4,128)} %reshape_reshape.3), slice={[0:384], [0:3], [0:1], [0:48]} | slice | bytes 442368 | tf_op jit(solution)/shard_map/slice | solution.py:93
  53.5 1.6 %fusion.8 = f32[384,144]{0,1:T(8,128)} fusion(f32[384,144]{0,1:T(8,128)S(1)} %bitcast.40, f32[384]{0:T(512)S(1)} %select_reduce_fusion, s32[384]{0:T(512)S(1)} %broadcast_add_fusion, f32[384]{0:T(512)S(1)} %broadcast_subtract_fusion, s32[384]{0:T(512)S(1)} %copy-done.6), kind=kOutput, calls=%fused_computation.23 | convolution fusion | flops 255541248 | bytes 448512 | tf_op jit(solution)/shard_map/dot_general | solution.py:94
  55.1 1.5 %collective-permute-start.2 = (f32[384,144]{0,1:T(8,128)}, f32[384,144]{0,1:T(8,128)S(1)}, u32[]{:S(2)}, u32[]{:S(2)}) collective-permute-start(f32[384,144]{0,1:T(8,128)} %fusion.8), channel_id=1, source_target_pairs={{496,0},{497,1},{498,2},{499,3},{500,4},{501,5},{502,6},{503,7},{5... | collective-permute-start | bytes 663560 | tf_op jit(solution)/shard_map/ppermute | solution.py:95
  56.6 2.5 %slice_bitcast_fusion = (f32[384,4,48]{2,1,0:T(4,128)S(1)}, f32[384,4,48]{2,1,0:T(4,128)}) fusion(f32[384,3,4,48]{3,2,1,0:T(4,128)} %reshape_reshape.3, f32[4]{0:T(128)S(1)} %copy-done.8, f32[4]{0:T(128)S(1)} %copy-done.7), kind=kLoop, calls=%fused_computation.22 | loop fusion | flops 147456 | bytes 1179680 | tf_op jit(solution)/shard_map/mul | solution.py:101
  59.4 2.1 %mul.173 = f32[16,24,576]{2,1,0:T(8,128)} reshape(f32[384,3,4,48]{3,2,1,0:T(4,128)S(1)} %mul.172) | data formatting | bytes 1769472 | tf_op jit(solution)/shard_map/mul | solution.py:101
  61.5 4.7 %fusion = f32[768,576]{0,1:T(8,128)S(1)} fusion(f32[384,576]{1,0:T(8,128)} %bitcast.35, f32[384,384]{1,0:T(8,128)} %param.13, f32[384,384]{1,0:T(8,128)} %param.12), kind=kOutput, calls=%fused_computation.7 | convolution fusion | flops 2038726656 | bytes 3833856 | tf_op jit(solution)/shard_map/dot_general | solution.py:98
  70.1 2.1 %multiply_select_fusion = f32[384,3,4,48]{3,2,1,0:T(4,128)S(1)} fusion(f32[384,4,48]{2,1,0:T(4,128)} %get-tuple-element.5, f32[384,3,48]{2,1,0:T(4,128)} %copy.28, pred[]{:T(512)S(6)} %eq.46), kind=kLoop, calls=%fused_computation.2 | loop fusion | flops 442368 | bytes 1400833 | tf_op jit(solution)/shard_map/jit(_where)/select_n | solution.py:105
  72.2 2.1 %select_n.38 = f32[16,24,576]{2,1,0:T(8,128)} reshape(f32[384,3,4,48]{3,2,1,0:T(4,128)S(1)} %multiply_select_fusion) | data formatting | bytes 1769472 | tf_op jit(solution)/shard_map/jit(_where)/select_n | solution.py:105
  74.3 3.2 %add_add_fusion = f32[16,24,576]{2,1,0:T(8,128)} fusion(f32[16,24,576]{2,1,0:T(8,128)} %select_n.38, f32[16,24,576]{2,1,0:T(8,128)} %bitcast.37, f32[16,24,576]{2,1,0:T(8,128)} %mul.173, f32[16,24,576]{2,1,0:T(8,128)} %bitcast.36), kind=kLoop, calls=%fused_computation.11 | loop fusion | flops 884736 | bytes 4423680 | tf_op jit(solution)/shard_map/add | solution.py:105
  77.5 4.4 %all-to-all-start.1 = ((f32[16,24,576]{2,1,0:T(8,128)}), f32[16,24,576]{2,1,0:T(8,128)}, u32[]{:S(2)}, u32[]{:S(2)}) async-start(f32[16,24,576]{2,1,0:T(8,128)} %add_add_fusion), calls=%async_computation.1 | async-start | bytes 1966080 | tf_op jit(solution)/shard_map/all_to_all | solution.py:107
  81.9 6.7 %convolution_bitcast_fusion = f32[288,1536]{1,0:T(8,128)S(1)} fusion(f32[768,1536]{1,0:T(8,128)} %constant.47.clone, f32[288,768]{1,0:T(8,128)S(1)} %bitcast.32), kind=kOutput, calls=%fused_computation | convolution fusion | flops 4076863488 | bytes 7372800 | tf_op jit(solution)/shard_map/dot_general | solution.py:112
  93.4 2.2 %broadcast_select_fusion = f32[3,4,24,768]{3,2,1,0:T(8,128)} fusion(f32[3,4,24,768]{3,2,1,0:T(8,128)} %collective-permute-done, f32[3,24,768]{2,1,0:T(8,128)S(1)} %slice_bitcast_fusion.3, pred[]{:T(512)S(6)} %eq.22), kind=kLoop, calls=%fused_computation.29 | loop fusion | flops 221184 | bytes 1990657 | tf_op jit(solution)/shard_map/jit(_where)/select_n | solution.py:53
  95.6 12.0 %all-to-all-done.1 = f32[16,24,576]{2,1,0:T(8,128)} async-done(((f32[16,24,576]{2,1,0:T(8,128)}), f32[16,24,576]{2,1,0:T(8,128)}, u32[]{:S(2)}, u32[]{:S(2)}) %all-to-all-start.1) | async-done | bytes 884768 | tf_op jit(solution)/shard_map/all_to_all | solution.py:107
  107.6 2.5 %reshape.66 = f32[16,24,3,4,48]{4,3,2,1,0:T(4,128)S(1)} reshape(f32[16,24,576]{2,1,0:T(8,128)} %all-to-all-done.1) | data formatting | bytes 1769472 | tf_op jit(solution)/shard_map/reshape | solution.py:108
  110.2 2.8 %copy.29 = f32[3,4,24,16,48]{4,3,2,1,0:T(8,128)} copy(f32[3,4,24,16,48]{4,1,0,2,3:T(4,128)S(1)} %bitcast.34) | data formatting | bytes 1769472 | tf_op jit(solution)/shard_map/transpose | solution.py:108
  113.0 3.3 %reshape.67 = f32[3,4,24,768]{3,2,1,0:T(8,128)} reshape(f32[3,4,24,16,48]{4,3,2,1,0:T(8,128)} %copy.29) | data formatting | bytes 1769472 | tf_op jit(solution)/shard_map/reshape | solution.py:109
  116.3 5.2 %multiply_add_fusion = (f32[3,4,24,768]{3,2,1,0:T(8,128)}, f32[3,4,24,768]{3,2,1,0:T(8,128)}) fusion(f32[3,4,24,768]{3,2,1,0:T(8,128)S(1)} %copy-done, f32[3,4,24,768]{3,2,1,0:T(8,128)} %reshape.67, f32[3,4,24,768]{3,2,1,0:T(8,128)} %broadcast_select_fusion, f32[3,4,24,768]{3,2,1,0:T(8,128)} %collective-permute-done.1, f32[3,8,24,768]{3,2,1,0:T(8,128)S(1)} %copy-done.3, ...), kind=kLoop, calls=%fused_computation.17 | loop fusion | flops 9068544 | bytes 11206656 | tf_op jit(solution)/shard_map/add | solution.py:125
  (38 shorter events, 11.1 us)
Async XLA Ops:
  9.2 12.0 %copy-start = (f32[3,4,24,768]{3,2,1,0:T(8,128)S(1)}, f32[3,4,24,768]{3,2,1,0:T(8,128)}, u32[]{:S(2)}) copy-start(f32[3,4,24,768]{3,2,1,0:T(8,128)} %param.10) | copy-start | bytes 2654212
  9.2 17.4 %copy-start.5 = (s32[384]{0:T(512)S(1)}, s32[384]{0:T(512)}, u32[]{:S(2)}) copy-start(s32[384]{0:T(512)} %param.15) | copy-start | bytes 4612
  9.2 17.4 %copy-start.9 = (f32[64]{0:T(128)S(1)}, f32[64]{0:T(128)}, u32[]{:S(2)}) copy-start(f32[64]{0:T(128)} %param.16) | copy-start | bytes 772
  9.2 17.5 %copy-start.6 = (s32[384]{0:T(512)S(1)}, s32[384]{0:T(512)}, u32[]{:S(2)}) copy-start(s32[384]{0:T(512)} %param.14) | copy-start | bytes 4612
  9.2 38.6 %all-to-all-start = ((f32[16,24,576]{2,1,0:T(8,128)}), f32[16,24,576]{2,1,0:T(8,128)S(1)}, u32[]{:S(2)}, u32[]{:S(2)}) async-start(f32[16,24,576]{2,1,0:T(8,128)} %reshape.63), calls=%async_computation | async-start | bytes 1966080 | tf_op jit(solution)/shard_map/all_to_all | solution.py:88
  21.2 69.7 %collective-permute-start.1 = (f32[3,4,24,768]{3,2,1,0:T(8,128)S(1)}, f32[3,4,24,768]{3,2,1,0:T(8,128)}, u32[]{:S(2)}, u32[]{:S(2)}) collective-permute-start(f32[3,4,24,768]{3,2,1,0:T(8,128)S(1)} %copy-done), channel_id=1, source_target_pairs={{0,16},{16,32},{32,48},{48,64},{64,80},{80,96},{96,112},{112,128},... | collective-permute-start | bytes 2654216 | tf_op jit(solution)/shard_map/ppermute | solution.py:50
  25.3 66.9 %collective-permute-start = (f32[3,4,24,768]{3,2,1,0:T(8,128)S(1)}, f32[3,4,24,768]{3,2,1,0:T(8,128)}, u32[]{:S(2)}, u32[]{:S(2)}) collective-permute-start(f32[3,4,24,768]{3,2,1,0:T(8,128)S(1)} %copy-done), channel_id=1, source_target_pairs={{16,0},{32,16},{48,32},{64,48},{80,64},{96,80},{112,96},{128,112},... | collective-permute-start | bytes 2654216 | tf_op jit(solution)/shard_map/ppermute | solution.py:51
  47.8 4.9 %copy-start.1 = (f32[16,24,576]{2,1,0:T(8,128)}, f32[16,24,576]{2,1,0:T(8,128)S(1)}, u32[]{:S(2)}) copy-start(f32[16,24,576]{2,1,0:T(8,128)S(1)} %all-to-all-done) | copy-start | bytes 2654212
  50.6 6.0 %copy-start.7 = (f32[4]{0:T(128)S(1)}, f32[4]{0:T(128)}, u32[]{:S(2)}) copy-start(f32[4]{0:T(128)} %constant.50) | copy-start | bytes 52
  50.6 6.0 %copy-start.8 = (f32[4]{0:T(128)S(1)}, f32[4]{0:T(128)}, u32[]{:S(2)}) copy-start(f32[4]{0:T(128)} %constant.51) | copy-start | bytes 52
  55.1 13.8 %collective-permute-start.2 = (f32[384,144]{0,1:T(8,128)}, f32[384,144]{0,1:T(8,128)S(1)}, u32[]{:S(2)}, u32[]{:S(2)}) collective-permute-start(f32[384,144]{0,1:T(8,128)} %fusion.8), channel_id=1, source_target_pairs={{496,0},{497,1},{498,2},{499,3},{500,4},{501,5},{502,6},{503,7},{5... | collective-permute-start | bytes 663560 | tf_op jit(solution)/shard_map/ppermute | solution.py:95
  77.5 30.2 %all-to-all-start.1 = ((f32[16,24,576]{2,1,0:T(8,128)}), f32[16,24,576]{2,1,0:T(8,128)}, u32[]{:S(2)}, u32[]{:S(2)}) async-start(f32[16,24,576]{2,1,0:T(8,128)} %add_add_fusion), calls=%async_computation.1 | async-start | bytes 1966080 | tf_op jit(solution)/shard_map/all_to_all | solution.py:107
  92.2 1.2 %copy-start.2 = (f32[3,8,24,768]{3,2,1,0:T(8,128)}, f32[3,8,24,768]{3,2,1,0:T(8,128)S(1)}, u32[]{:S(2)}) copy-start(f32[3,8,24,768]{3,2,1,0:T(8,128)S(1)} %constant_dynamic-update-slice_fusion) | copy-start | bytes 5308420
  113.0 3.3 %copy-start.3 = (f32[3,8,24,768]{3,2,1,0:T(8,128)S(1)}, f32[3,8,24,768]{3,2,1,0:T(8,128)}, u32[]{:S(2)}) copy-start(f32[3,8,24,768]{3,2,1,0:T(8,128)} %copy-done.2) | copy-start | bytes 5308420
  113.0 3.3 %copy-start.4 = (f32[288,768]{1,0:T(8,128)S(1)}, f32[288,768]{1,0:T(8,128)}, u32[]{:S(2)}) copy-start(f32[288,768]{1,0:T(8,128)} %get-tuple-element.6) | copy-start | bytes 2654212
where the time goes:
time: 122 us; the launch traced here: 121 us
  local copies, waits for them, and re-layouts  34.6 us (28%)
  waiting for transfers between devices  33.1 us (27%)
  starting transfers between devices  23.3 us (19%)
  other arithmetic  16.7 us (14%)
  matrix products  13 us (11%)
    all_to_all x1, waiting for transfers between devices, shards(): cols = lax.all_to_all(send, 'ga', 0, 0, tiled=True).reshape(rows, width)  21.1 us
    all_to_all x1, waiting for transfers between devices, shards(): lax.all_to_all(wall.reshape(parts, rows_here, width), 'ga', 0, 0, tiled=T...  12 us
    all_to_all x1, starting transfers between devices, shards(): cols = lax.all_to_all(send, 'ga', 0, 0, tiled=True).reshape(rows, width)  12 us
    dot_general x1, matrix products, shards(): jnp.dot(lines, jnp.asarray(spanwise_table(span)), precision=HIGHEST, pref...  6.65 us
    reshape x2, local copies, waits for them, and re-layouts, shards(): send = velocity.reshape(comps, planes, rows_here, parts, share)  6.48 us
    add x1, other arithmetic, shards(): return (velocity + update_rate * accumulated_next, accumulated_next)  5.15 us
    dot_general x1, matrix products, shards(): jnp.dot(both, cols, precision=HIGHEST, preferred_element_type=jnp.float32)  4.69 us
    all_to_all x1, starting transfers between devices, shards(): lax.all_to_all(wall.reshape(parts, rows_here, width), 'ga', 0, 0, tiled=T...  4.45 us
  transfers between devices with their start and end apart: 5, of which 2 were waited for; matrix products, arithmetic and copies ran while one was open for 33% of the time, Pallas kernels for 0%

commit v1 on v0

--- a/solution.py
+++ b/solution.py
@@ -44,11 +44,16 @@
     return np.asarray(lower, np.float32), np.asarray(upper, np.float32)
 
 
-def streamwise(field):
+def halo_planes(field):
+    count = lax.axis_size("gx")
+    behind = lax.ppermute(field, "gx", [(i, i + 1) for i in range(count - 1)])
+    ahead = lax.ppermute(field, "gx", [(i + 1, i) for i in range(count - 1)])
+    return behind, ahead
+
+
+def streamwise(field, behind, ahead):
     count = lax.axis_size("gx")
     extent = field.shape[1]
-    behind = lax.ppermute(field, "gx", [(i, i + 1) for i in range(count - 1)])
-    ahead = lax.ppermute(field, "gx", [(i + 1, i) for i in range(count - 1)])
     at_outlet = lax.axis_index("gx") == count - 1
     ahead = jnp.where(at_outlet, jnp.broadcast_to(field[:, -1:], ahead.shape), ahead)
     padded = jnp.concatenate([behind[:, extent - HALO :], field, ahead[:, :HALO]], 1)
@@ -73,40 +78,34 @@
     return lower + upper
 
 
+def columns_of(field, parts):
+    planes, rows_here, span = field.shape
+    share = span // parts
+    send = field.reshape(planes, rows_here, parts, share).transpose(2, 1, 0, 3)
+    send = send.reshape(parts, rows_here, planes * share)
+    return lax.all_to_all(send, "ga", 0, 0, tiled=True).reshape(rows_here * parts, planes * share)
+
+
+def rows_of(block, parts, planes):
+    rows, width = block.shape
+    share = width // planes
+    back = lax.all_to_all(block.reshape(parts, rows // parts, width), "ga", 0, 0, tiled=True)
+    back = back.reshape(parts, rows // parts, planes, share).transpose(2, 1, 0, 3)
+    return back.reshape(planes, rows // parts, parts * share)
+
+
 def shards(
     velocity, accumulated, wall_first, wall_second, recycle_rows, weight_index, weight_table
 ):
     comps, planes, rows_here, span = velocity.shape
     parts = lax.axis_size("ga")
-    slabs = lax.axis_size("gx")
     share = span // parts
     rows = rows_here * parts
-    width = comps * planes * share
+    contract_rows = (((0,), (1,)), ((), ()))
+    contract_lead = (((0,), (0,)), ((), ()))
 
-    send = velocity.reshape(comps, planes, rows_here, parts, share)
-    send = send.transpose(3, 2, 0, 1, 4).reshape(parts, rows_here, width)
-    cols = lax.all_to_all(send, "ga", 0, 0, tiled=True).reshape(rows, width)
-    grid = cols.reshape(rows, comps, planes, share)
-
-    source_slab, source_plane = divmod(RECYCLE_PLANE, planes)
-    mix = interpolation_matrix(recycle_rows, weight_index, weight_table, rows)
-    plane = grid[:, :, source_plane, :].reshape(rows, comps * share)
-    inflow = jnp.dot(mix, plane, precision=HIGHEST, preferred_element_type=jnp.float32)
-    inflow = lax.ppermute(inflow, "gx", [(source_slab, 0)]).reshape(rows, comps, 1, share)
-
-    both = jnp.concatenate([wall_first, wall_second], 0)
-    derived = jnp.dot(both, cols, precision=HIGHEST, preferred_element_type=jnp.float32)
-    normal_first = derived[:rows].reshape(rows, comps, planes, share)
-    normal_second = derived[rows:].reshape(rows, comps, planes, share)
-    wall = -(grid[:, 1:2] * normal_first) + viscosity * normal_second
-
-    lower, upper = ghost_weights(planes)
-    ghost = inflow * (grid[:, 0:1] * lower[None, None, :, None] + viscosity * upper[None, None, :, None])
-    wall = wall + jnp.where(lax.axis_index("gx") == 0, ghost, 0.0)
-
-    back = lax.all_to_all(wall.reshape(parts, rows_here, width), "ga", 0, 0, tiled=True)
-    back = back.reshape(parts, rows_here, comps, planes, share).transpose(2, 3, 1, 0, 4)
-    back = back.reshape(comps, planes, rows_here, span)
+    behind, ahead = halo_planes(velocity)
+    cols = [columns_of(velocity[c], parts) for c in range(comps)]
 
     lines = velocity.reshape(-1, span)
     spectral = jnp.dot(
@@ -117,9 +116,49 @@
     )
     span_first = spectral[:, :span].reshape(velocity.shape)
     span_second = spectral[:, span:].reshape(velocity.shape)
+    span_terms = -(velocity[2:3] * span_first) + viscosity * span_second
+    cols, span_terms, behind, ahead = lax.optimization_barrier((cols, span_terms, behind, ahead))
 
-    tendency = -(velocity[2:3] * span_first) + viscosity * span_second
-    tendency = tendency + streamwise(velocity)
+    source_slab, source_plane = divmod(RECYCLE_PLANE, planes)
+    mix = interpolation_matrix(recycle_rows, weight_index, weight_table, rows)
+    inflow = jnp.concatenate(
+        [
+            lax.dot_general(
+                cols[c][:, source_plane * share : (source_plane + 1) * share],
+                mix,
+                contract_rows,
+                precision=HIGHEST,
+                preferred_element_type=jnp.float32,
+            )
+            for c in range(comps)
+        ],
+        0,
+    )
+    inflow = lax.ppermute(inflow, "gx", [(source_slab, 0)])
+
+    lower, upper = ghost_weights(planes)
+    lower = jnp.asarray(np.repeat(lower, share))
+    upper = jnp.asarray(np.repeat(upper, share))
+    spread = jnp.asarray(np.tile(np.eye(share, dtype=np.float32), (1, planes)))
+    at_inlet = lax.axis_index("gx") == 0
+    both = jnp.concatenate([wall_first, wall_second], 0)
+    backs = []
+    for c in range(comps):
+        derived = jnp.dot(both, cols[c], precision=HIGHEST, preferred_element_type=jnp.float32)
+        wall = -(cols[1] * derived[:rows]) + viscosity * derived[rows:]
+        spread_inflow = lax.dot_general(
+            inflow[c * share : (c + 1) * share],
+            spread,
+            contract_lead,
+            precision=HIGHEST,
+            preferred_element_type=jnp.float32,
+        )
+        ghost = spread_inflow * (cols[0] * lower + viscosity * upper)
+        wall = wall + jnp.where(at_inlet, ghost, 0.0)
+        backs.append(rows_of(wall, parts, planes))
+    back = jnp.stack(backs)
+
+    tendency = span_terms + streamwise(velocity, behind, ahead)
     tendency = tendency + back
     accumulated_next = keep_rate * accumulated + step_size * tendency
     return (velocity + update_rate * accumulated_next, accumulated_next)

time: 122 us -> 166 us (1.36)
  starting transfers between devices: 23.3 us -> 41.5 us
  waiting for transfers between devices: 33.1 us -> 48 us
  matrix products: 13 us -> 23.2 us
  other arithmetic: 16.7 us -> 9.68 us
  local copies, waits for them, and re-layouts: 34.6 us -> 40.8 us
    all_to_all x2 -> x6, starting transfers between devices: 16.4 us -> 34.7 us  [the longest x3 22.3 us: columns_of(): lax.all_to_all(send, 'ga', 0, 0, tiled=True)]
    dot_general x2 -> x9, matrix products: 6.32 us -> 16.5 us  [the longest x3 6.18 us: shards(): jnp.dot(both, cols[c], precision=HIGHEST, preferred_element_type=jnp.floa...]
    ppermute x3, waiting for transfers between devices: 0.01 us -> 10.1 us  [the longest x1 10.1 us: shards(): inflow = lax.ppermute(inflow, 'gx', [(source_slab, 0)])]
    another operation x1 -> x7, local copies, waits for them, and re-layouts: 2.75 us -> 9.98 us  [the longest x3 6.41 us: shards(): back = jnp.stack(backs)]
    transpose x1 -> x5, local copies, waits for them, and re-layouts: 2.8 us -> 8.43 us  [the longest x3 7.41 us: rows_of(): back.reshape(parts, rows // parts, planes, share).transpose(2, 1, 0, 3)]
    all_to_all x2 -> x6, waiting for transfers between devices: 33.1 us -> 37.9 us  [the longest x3 20.6 us: columns_of(): lax.all_to_all(send, 'ga', 0, 0, tiled=True)]
    add x0 -> x3, local copies, waits for them, and re-layouts: none -> 4.68 us  [shards(): wall = wall + jnp.where(at_inlet, ghost, 0.0)]
    slice x3 -> x0, local copies, waits for them, and re-layouts: 4.16 us -> none  [the longest x2 2.86 us: shards(): plane = grid[:, :, source_plane, :].reshape(rows, comps * share)]
  transfers between devices with their start and end apart: 5 -> 9, of which waited for: 2 -> 6; matrix products, arithmetic and copies ran while one was open for 33% -> 28% of each run, Pallas kernels for 0% -> 0%
where the time goes in v1:
time: 166 us; the launch traced here: 164 us
  waiting for transfers between devices  48 us (29%)
  starting transfers between devices  41.5 us (25%)
  local copies, waits for them, and re-layouts  40.8 us (25%)
  matrix products  23.2 us (14%)
  other arithmetic  9.68 us (6%)
    all_to_all x3, starting transfers between devices, columns_of(): lax.all_to_all(send, 'ga', 0, 0, tiled=True)  22.3 us
    all_to_all x3, waiting for transfers between devices, columns_of(): lax.all_to_all(send, 'ga', 0, 0, tiled=True)  20.6 us
    all_to_all x3, waiting for transfers between devices, rows_of(): lax.all_to_all(block.reshape(parts, rows // parts, width), 'ga', 0, 0, ti...  17.3 us
    all_to_all x3, starting transfers between devices, rows_of(): lax.all_to_all(block.reshape(parts, rows // parts, width), 'ga', 0, 0, ti...  12.4 us
    ppermute x1, waiting for transfers between devices, shards(): inflow = lax.ppermute(inflow, 'gx', [(source_slab, 0)])  10.1 us
    transpose x3, local copies, waits for them, and re-layouts, rows_of(): back.reshape(parts, rows // parts, planes, share).transpose(2, 1, 0, 3)  7.41 us
    reshape x3, local copies, waits for them, and re-layouts, rows_of(): back.reshape(parts, rows // parts, planes, share).transpose(2, 1, 0, 3)  6.86 us
    dot_general x1, matrix products, shards(): jnp.dot(lines, jnp.asarray(spanwise_table(span)), precision=HIGHEST, pref...  6.64 us
  transfers between devices with their start and end apart: 9, of which 6 were waited for; matrix products, arithmetic and copies ran while one was open for 28% of the time, Pallas kernels for 0%

profile of v1, /device:TPU:1, one launch (start us, length us, event | category | flops | bytes accessed | tf_op | source)
XLA Modules:
  0.0 164.2 jit_solution(3909612740501265352)
XLA Ops:
  4.8 11.8 %all-to-all-start = ((f32[16,24,192]{2,1,0:T(8,128)}), f32[16,24,192]{2,1,0:T(8,128)S(1)}, u32[]{:S(2)}, u32[]{:S(2)}) async-start(f32[16,24,192]{2,1,0:T(8,128)} %reshape.61), calls=%async_computation | async-start | bytes 786432 | tf_op jit(solution)/shard_map/all_to_all | solution.py:86
  16.6 4.1 %collective-permute-start = (f32[3,4,24,768]{3,2,1,0:T(8,128)S(1)}, f32[3,4,24,768]{3,2,1,0:T(8,128)}, u32[]{:S(2)}, u32[]{:S(2)}) collective-permute-start(f32[3,4,24,768]{3,2,1,0:T(8,128)S(1)} %copy-done), channel_id=1, source_target_pairs={{0,16},{16,32},{32,48},{48,64},{64,80},{80,96},{96,112},{112,128},... | collective-permute-start | bytes 2654216 | tf_op jit(solution)/shard_map/ppermute | solution.py:49
  24.0 6.6 %convolution_bitcast_fusion = f32[288,1536]{1,0:T(8,128)S(1)} fusion(f32[768,1536]{1,0:T(8,128)} %constant.48.clone, f32[288,768]{1,0:T(8,128)S(1)} %bitcast.48), kind=kOutput, calls=%fused_computation | convolution fusion | flops 4076863488 | bytes 7372800 | tf_op jit(solution)/shard_map/dot_general | solution.py:111
  31.2 7.0 %all-to-all-start.1 = ((f32[16,24,192]{2,1,0:T(8,128)}), f32[16,24,192]{2,1,0:T(8,128)}, u32[]{:S(2)}, u32[]{:S(2)}) async-start(f32[16,24,192]{2,1,0:T(8,128)} %reshape.63), calls=%async_computation.1 | async-start | bytes 786432 | tf_op jit(solution)/shard_map/all_to_all | solution.py:86
  42.8 2.2 %reshape.65 = f32[16,24,192]{2,1,0:T(8,128)} reshape(f32[16,24,4,48]{3,2,1,0:T(4,128)} %bitcast.56) | data formatting | bytes 589824 | tf_op jit(solution)/shard_map/reshape | solution.py:85
  45.0 7.8 %all-to-all-done.1 = f32[16,24,192]{2,1,0:T(8,128)} async-done(((f32[16,24,192]{2,1,0:T(8,128)}), f32[16,24,192]{2,1,0:T(8,128)}, u32[]{:S(2)}, u32[]{:S(2)}) %all-to-all-start.1) | async-done | bytes 294944 | tf_op jit(solution)/shard_map/all_to_all | solution.py:86
  52.9 3.4 %all-to-all-start.2 = ((f32[16,24,192]{2,1,0:T(8,128)}), f32[16,24,192]{2,1,0:T(8,128)S(1)}, u32[]{:S(2)}, u32[]{:S(2)}) async-start(f32[16,24,192]{2,1,0:T(8,128)} %reshape.65), calls=%async_computation.2 | async-start | bytes 786432 | tf_op jit(solution)/shard_map/all_to_all | solution.py:86
  58.1 12.2 %all-to-all-done.2 = f32[16,24,192]{2,1,0:T(8,128)S(1)} async-done(((f32[16,24,192]{2,1,0:T(8,128)}), f32[16,24,192]{2,1,0:T(8,128)S(1)}, u32[]{:S(2)}, u32[]{:S(2)}) %all-to-all-start.2) | async-done | bytes 294944 | tf_op jit(solution)/shard_map/all_to_all | solution.py:86
  82.1 10.1 %collective-permute-done.2 = f32[144,384]{1,0:T(8,128)S(1)} collective-permute-done((f32[144,384]{1,0:T(8,128)S(1)}, f32[144,384]{1,0:T(8,128)S(1)}, u32[]{:S(2)}, u32[]{:S(2)}) %collective-permute-start.2) | collective-permute-done | bytes 221216 | tf_op jit(solution)/shard_map/ppermute | solution.py:137
  95.9 4.2 %all-to-all-start.5 = ((f32[16,24,192]{2,1,0:T(8,128)}), f32[16,24,192]{2,1,0:T(8,128)}, u32[]{:S(2)}, u32[]{:S(2)}) async-start(f32[16,24,192]{2,1,0:T(8,128)} %bitcast.61), calls=%async_computation.5 | async-start | bytes 786432 | tf_op jit(solution)/shard_map/all_to_all | solution.py:92
  100.0 2.4 %fusion.46 = f32[768,192]{0,1:T(8,128)S(1)} fusion(f32[768,384]{1,0:T(8,128)S(1)} %constant_dynamic-update-slice_fusion.2, f32[384,192]{1,0:T(8,128)} %bitcast.3), kind=kOutput, calls=%fused_computation.82 | convolution fusion | flops 679477248 | bytes 2064384 | tf_op jit(solution)/shard_map/dot_general | solution.py:147
  106.4 8.3 %all-to-all-done.5 = f32[16,24,192]{2,1,0:T(8,128)} async-done(((f32[16,24,192]{2,1,0:T(8,128)}), f32[16,24,192]{2,1,0:T(8,128)}, u32[]{:S(2)}, u32[]{:S(2)}) %all-to-all-start.5) | async-done | bytes 294944 | tf_op jit(solution)/shard_map/all_to_all | solution.py:92
  114.7 4.1 %all-to-all-start.4 = ((f32[16,24,192]{2,1,0:T(8,128)}), f32[16,24,192]{2,1,0:T(8,128)}, u32[]{:S(2)}, u32[]{:S(2)}) async-start(f32[16,24,192]{2,1,0:T(8,128)} %bitcast.60), calls=%async_computation.4 | async-start | bytes 786432 | tf_op jit(solution)/shard_map/all_to_all | solution.py:92
  118.8 2.4 %fusion.45 = f32[768,192]{0,1:T(8,128)S(1)} fusion(f32[768,384]{1,0:T(8,128)S(1)} %constant_dynamic-update-slice_fusion.2, f32[384,192]{1,0:T(8,128)} %bitcast.53), kind=kOutput, calls=%fused_computation.81 | convolution fusion | flops 679477248 | bytes 2064384 | tf_op jit(solution)/shard_map/dot_general | solution.py:147
  123.5 9.1 %all-to-all-done.4 = f32[16,24,192]{2,1,0:T(8,128)} async-done(((f32[16,24,192]{2,1,0:T(8,128)}), f32[16,24,192]{2,1,0:T(8,128)}, u32[]{:S(2)}, u32[]{:S(2)}) %all-to-all-start.4) | async-done | bytes 294944 | tf_op jit(solution)/shard_map/all_to_all | solution.py:92
  132.6 4.1 %all-to-all-start.3 = ((f32[16,24,192]{2,1,0:T(8,128)}), f32[16,24,192]{2,1,0:T(8,128)}, u32[]{:S(2)}, u32[]{:S(2)}) async-start(f32[16,24,192]{2,1,0:T(8,128)} %bitcast.13), calls=%async_computation.3 | async-start | bytes 786432 | tf_op jit(solution)/shard_map/all_to_all | solution.py:92
  136.7 2.5 %broadcast_select_fusion = (f32[3,4,24,768]{3,2,1,0:T(8,128)}, f32[3,8,24,768]{3,2,1,0:T(8,128)S(1)}) fusion(f32[3,4,24,768]{3,2,1,0:T(8,128)} %collective-permute-done.1, f32[3,24,768]{2,1,0:T(8,128)S(1)} %slice_bitcast_fusion, pred[]{:T(512)S(6)} %eq.22, f32[3,4,24,768]{3,2,1,0:T(8,128)} %collective-permute-done), kind=kLoop, calls=%fused_computation.30 | loop fusion | flops 221183 | bytes 3760129 | tf_op jit(solution)/shard_map/jit(_where)/select_n | solution.py:58
  139.3 2.3 %reshape.74 = f32[16,24,4,48]{3,2,1,0:T(4,128)} reshape(f32[16,24,192]{2,1,0:T(8,128)} %all-to-all-done.5) | data formatting | bytes 589824 | tf_op jit(solution)/shard_map/reshape | solution.py:93
  141.6 2.5 %copy.43 = f32[4,24,16,48]{3,2,1,0:T(8,128)} copy(f32[4,24,16,48]{3,0,1,2:T(4,128)} %bitcast.57) | data formatting | bytes 589824 | tf_op jit(solution)/shard_map/transpose | solution.py:93
  146.2 2.3 %reshape.72 = f32[16,24,4,48]{3,2,1,0:T(4,128)} reshape(f32[16,24,192]{2,1,0:T(8,128)} %all-to-all-done.4) | data formatting | bytes 589824 | tf_op jit(solution)/shard_map/reshape | solution.py:93
  148.5 2.5 %copy.40 = f32[4,24,16,48]{3,2,1,0:T(8,128)} copy(f32[4,24,16,48]{3,0,1,2:T(4,128)} %bitcast.58) | data formatting | bytes 589824 | tf_op jit(solution)/shard_map/transpose | solution.py:93
  153.1 2.3 %reshape.70 = f32[16,24,4,48]{3,2,1,0:T(4,128)} reshape(f32[16,24,192]{2,1,0:T(8,128)} %all-to-all-done.3) | data formatting | bytes 589824 | tf_op jit(solution)/shard_map/reshape | solution.py:93
  155.4 2.5 %copy.37 = f32[4,24,16,48]{3,2,1,0:T(8,128)} copy(f32[4,24,16,48]{3,0,1,2:T(4,128)} %bitcast.59) | data formatting | bytes 589824 | tf_op jit(solution)/shard_map/transpose | solution.py:93
  160.0 4.1 %multiply_add_fusion = (f32[3,4,24,768]{3,2,1,0:T(8,128)}, f32[3,4,24,768]{3,2,1,0:T(8,128)}) fusion(f32[3,4,24,768]{3,2,1,0:T(8,128)S(1)} %copy-done, f32[1,4,24,768]{3,2,1,0:T(8,128)} %stack_reshape.11, f32[1,4,24,768]{3,2,1,0:T(8,128)} %stack_reshape.10, f32[1,4,24,768]{3,2,1,0:T(8,128)} %stack_reshape.9, f32[3,4,24,768]{3,2,1,0:T(8,128)S(1)} %negate_add_fusion, ...), kind=kLoop, calls=%fused_computation.21 | loop fusion | flops 8847360 | bytes 10027008 | tf_op jit(solution)/shard_map/add | solution.py:164
  (74 shorter events, 42.3 us)
Async XLA Ops:
  3.2 13.5 %copy-start = (f32[3,4,24,768]{3,2,1,0:T(8,128)S(1)}, f32[3,4,24,768]{3,2,1,0:T(8,128)}, u32[]{:S(2)}) copy-start(f32[3,4,24,768]{3,2,1,0:T(8,128)} %param.11) | copy-start | bytes 2654212
  4.8 26.4 %all-to-all-start = ((f32[16,24,192]{2,1,0:T(8,128)}), f32[16,24,192]{2,1,0:T(8,128)S(1)}, u32[]{:S(2)}, u32[]{:S(2)}) async-start(f32[16,24,192]{2,1,0:T(8,128)} %reshape.61), calls=%async_computation | async-start | bytes 786432 | tf_op jit(solution)/shard_map/all_to_all | solution.py:86
  16.6 53.7 %collective-permute-start = (f32[3,4,24,768]{3,2,1,0:T(8,128)S(1)}, f32[3,4,24,768]{3,2,1,0:T(8,128)}, u32[]{:S(2)}, u32[]{:S(2)}) collective-permute-start(f32[3,4,24,768]{3,2,1,0:T(8,128)S(1)} %copy-done), channel_id=1, source_target_pairs={{0,16},{16,32},{32,48},{48,64},{64,80},{80,96},{96,112},{112,128},... | collective-permute-start | bytes 2654216 | tf_op jit(solution)/shard_map/ppermute | solution.py:49
  20.7 49.6 %collective-permute-start.1 = (f32[3,4,24,768]{3,2,1,0:T(8,128)S(1)}, f32[3,4,24,768]{3,2,1,0:T(8,128)}, u32[]{:S(2)}, u32[]{:S(2)}) collective-permute-start(f32[3,4,24,768]{3,2,1,0:T(8,128)S(1)} %copy-done), channel_id=1, source_target_pairs={{16,0},{32,16},{48,32},{64,48},{80,64},{96,80},{112,96},{128,112},... | collective-permute-start | bytes 2654216 | tf_op jit(solution)/shard_map/ppermute | solution.py:50
  31.2 8.4 %copy-start.1 = (f32[16,24,192]{2,1,0:T(8,128)}, f32[16,24,192]{2,1,0:T(8,128)S(1)}, u32[]{:S(2)}) copy-start(f32[16,24,192]{2,1,0:T(8,128)S(1)} %all-to-all-done) | copy-start | bytes 884740
  31.2 21.7 %all-to-all-start.1 = ((f32[16,24,192]{2,1,0:T(8,128)}), f32[16,24,192]{2,1,0:T(8,128)}, u32[]{:S(2)}, u32[]{:S(2)}) async-start(f32[16,24,192]{2,1,0:T(8,128)} %reshape.63), calls=%async_computation.1 | async-start | bytes 786432 | tf_op jit(solution)/shard_map/all_to_all | solution.py:86
  38.2 1.4 copy-start.4
  38.2 1.7 %copy-start.5 = (f32[384,384]{1,0:T(8,128)S(1)}, f32[384,384]{1,0:T(8,128)}, u32[]{:S(2)}) copy-start(f32[384,384]{1,0:T(8,128)} %param.14) | copy-start | bytes 1769476
  40.0 5.0 %copy-start.13 = (s32[384]{0:T(512)S(1)}, s32[384]{0:T(512)}, u32[]{:S(2)}) copy-start(s32[384]{0:T(512)} %param.15) | copy-start | bytes 4612
  41.3 15.0 %copy-start.12 = (s32[384]{0:T(512)S(1)}, s32[384]{0:T(512)}, u32[]{:S(2)}) copy-start(s32[384]{0:T(512)} %param.16) | copy-start | bytes 4612
  41.4 15.0 %copy-start.16 = (f32[64]{0:T(128)S(1)}, f32[64]{0:T(128)}, u32[]{:S(2)}) copy-start(f32[64]{0:T(128)} %param.17) | copy-start | bytes 772
  45.0 30.4 %copy-start.14 = (s32[384]{0:T(512)}, s32[384]{0:T(512)S(1)}, u32[]{:S(2)}) copy-start(s32[384]{0:T(512)S(1)} %broadcast_add_fusion) | copy-start | bytes 4612
  52.9 17.4 %all-to-all-start.2 = ((f32[16,24,192]{2,1,0:T(8,128)}), f32[16,24,192]{2,1,0:T(8,128)S(1)}, u32[]{:S(2)}, u32[]{:S(2)}) async-start(f32[16,24,192]{2,1,0:T(8,128)} %reshape.65), calls=%async_computation.2 | async-start | bytes 786432 | tf_op jit(solution)/shard_map/all_to_all | solution.py:86
  56.4 18.9 %copy-start.15 = (f32[384]{0:T(512)}, f32[384]{0:T(512)S(1)}, u32[]{:S(2)}) copy-start(f32[384]{0:T(512)S(1)} %broadcast_subtract_fusion) | copy-start | bytes 4612
  73.3 4.0 %copy-start.3 = (f32[16,24,192]{2,1,0:T(8,128)S(1)}, f32[16,24,192]{2,1,0:T(8,128)}, u32[]{:S(2)}) copy-start(f32[16,24,192]{2,1,0:T(8,128)} %copy-done.2) | copy-start | bytes 884740
  77.4 15.4 %copy-start.6 = (f32[48,192]{1,0:T(8,128)S(1)}, f32[48,192]{1,0:T(8,128)}, u32[]{:S(2)}) copy-start(f32[48,192]{1,0:T(8,128)} %constant.51.clone) | copy-start | bytes 110596
  77.4 15.4 %copy-start.10 = (f32[192]{0:T(256)S(1)}, f32[192]{0:T(256)}, u32[]{:S(2)}) copy-start(f32[192]{0:T(256)} %constant.54) | copy-start | bytes 2308
  77.4 15.4 %copy-start.11 = (f32[192]{0:T(256)S(1)}, f32[192]{0:T(256)}, u32[]{:S(2)}) copy-start(f32[192]{0:T(256)} %constant.49.clone) | copy-start | bytes 2308
  79.2 13.0 %collective-permute-start.2 = (f32[144,384]{1,0:T(8,128)S(1)}, f32[144,384]{1,0:T(8,128)S(1)}, u32[]{:S(2)}, u32[]{:S(2)}) collective-permute-start(f32[144,384]{1,0:T(8,128)S(1)} %pad_maximum_fusion.1), channel_id=1, source_target_pairs={{496,0},{497,1},{498,2},{499,3},{500,4},{501,5},{502,6},{503,7},{5... | collective-permute-start | bytes 663560 | tf_op jit(solution)/shard_map/ppermute | solution.py:137
  95.9 18.8 %all-to-all-start.5 = ((f32[16,24,192]{2,1,0:T(8,128)}), f32[16,24,192]{2,1,0:T(8,128)}, u32[]{:S(2)}, u32[]{:S(2)}) async-start(f32[16,24,192]{2,1,0:T(8,128)} %bitcast.61), calls=%async_computation.5 | async-start | bytes 786432 | tf_op jit(solution)/shard_map/all_to_all | solution.py:92
  100.0 2.4 %copy-start.7 = (f32[48,192]{1,0:T(8,128)S(1)}, f32[48,192]{1,0:T(8,128)}, u32[]{:S(2)}) copy-start(f32[48,192]{1,0:T(8,128)} %constant.51.clone) | copy-start | bytes 110596
  114.7 17.9 %all-to-all-start.4 = ((f32[16,24,192]{2,1,0:T(8,128)}), f32[16,24,192]{2,1,0:T(8,128)}, u32[]{:S(2)}, u32[]{:S(2)}) async-start(f32[16,24,192]{2,1,0:T(8,128)} %bitcast.60), calls=%async_computation.4 | async-start | bytes 786432 | tf_op jit(solution)/shard_map/all_to_all | solution.py:92
  118.8 2.4 %copy-start.8 = (f32[48,192]{1,0:T(8,128)S(1)}, f32[48,192]{1,0:T(8,128)}, u32[]{:S(2)}) copy-start(f32[48,192]{1,0:T(8,128)} %constant.51.clone) | copy-start | bytes 110596
  132.6 20.5 %all-to-all-start.3 = ((f32[16,24,192]{2,1,0:T(8,128)}), f32[16,24,192]{2,1,0:T(8,128)}, u32[]{:S(2)}, u32[]{:S(2)}) async-start(f32[16,24,192]{2,1,0:T(8,128)} %bitcast.13), calls=%async_computation.3 | async-start | bytes 786432 | tf_op jit(solution)/shard_map/all_to_all | solution.py:92
  (2 other events, 1.4 us)

commit v2 on v0

--- a/solution.py
+++ b/solution.py
@@ -44,11 +44,16 @@
     return np.asarray(lower, np.float32), np.asarray(upper, np.float32)
 
 
-def streamwise(field):
+def halo_planes(field):
+    count = lax.axis_size("gx")
+    behind = lax.ppermute(field, "gx", [(i, i + 1) for i in range(count - 1)])
+    ahead = lax.ppermute(field, "gx", [(i + 1, i) for i in range(count - 1)])
+    return behind, ahead
+
+
+def streamwise(field, behind, ahead):
     count = lax.axis_size("gx")
     extent = field.shape[1]
-    behind = lax.ppermute(field, "gx", [(i, i + 1) for i in range(count - 1)])
-    ahead = lax.ppermute(field, "gx", [(i + 1, i) for i in range(count - 1)])
     at_outlet = lax.axis_index("gx") == count - 1
     ahead = jnp.where(at_outlet, jnp.broadcast_to(field[:, -1:], ahead.shape), ahead)
     padded = jnp.concatenate([behind[:, extent - HALO :], field, ahead[:, :HALO]], 1)
@@ -85,7 +90,20 @@
 
     send = velocity.reshape(comps, planes, rows_here, parts, share)
     send = send.transpose(3, 2, 0, 1, 4).reshape(parts, rows_here, width)
+    behind, ahead = halo_planes(velocity)
     cols = lax.all_to_all(send, "ga", 0, 0, tiled=True).reshape(rows, width)
+    lines = velocity.reshape(-1, span)
+    spectral = jnp.dot(
+        lines,
+        jnp.asarray(spanwise_table(span)),
+        precision=HIGHEST,
+        preferred_element_type=jnp.float32,
+    )
+    span_first = spectral[:, :span].reshape(velocity.shape)
+    span_second = spectral[:, span:].reshape(velocity.shape)
+
+    span_terms = -(velocity[2:3] * span_first) + viscosity * span_second
+    cols, span_terms, behind, ahead = lax.optimization_barrier((cols, span_terms, behind, ahead))
     grid = cols.reshape(rows, comps, planes, share)
 
     source_slab, source_plane = divmod(RECYCLE_PLANE, planes)
@@ -108,18 +126,7 @@
     back = back.reshape(parts, rows_here, comps, planes, share).transpose(2, 3, 1, 0, 4)
     back = back.reshape(comps, planes, rows_here, span)
 
-    lines = velocity.reshape(-1, span)
-    spectral = jnp.dot(
-        lines,
-        jnp.asarray(spanwise_table(span)),
-        precision=HIGHEST,
-        preferred_element_type=jnp.float32,
-    )
-    span_first = spectral[:, :span].reshape(velocity.shape)
-    span_second = spectral[:, span:].reshape(velocity.shape)
-
-    tendency = -(velocity[2:3] * span_first) + viscosity * span_second
-    tendency = tendency + streamwise(velocity)
+    tendency = span_terms + streamwise(velocity, behind, ahead)
     tendency = tendency + back
     accumulated_next = keep_rate * accumulated + step_size * tendency
     return (velocity + update_rate * accumulated_next, accumulated_next)

time: 122 us -> 126 us (1.033)
  the two profiles are of different devices: /device:TPU:1 before, /device:TPU:33 now
where the time goes in v2:
time: 126 us; the launch traced here: 125 us
  waiting for transfers between devices  36.7 us (29%)
  local copies, waits for them, and re-layouts  31.4 us (25%)
  starting transfers between devices  26.1 us (21%)
  other arithmetic  15.6 us (12%)
  matrix products  14.6 us (12%)
    all_to_all x1, waiting for transfers between devices, shards(): lax.all_to_all(wall.reshape(parts, rows_here, width), 'ga', 0, 0, tiled=T...  21.8 us
    all_to_all x1, waiting for transfers between devices, shards(): cols = lax.all_to_all(send, 'ga', 0, 0, tiled=True).reshape(rows, width)  14.8 us
    all_to_all x1, starting transfers between devices, shards(): cols = lax.all_to_all(send, 'ga', 0, 0, tiled=True).reshape(rows, width)  11.7 us
    dot_general x1, matrix products, shards(): jnp.dot(lines, jnp.asarray(spanwise_table(span)), precision=HIGHEST, pref...  8.26 us
    reshape x2, local copies, waits for them, and re-layouts, shards(): send = velocity.reshape(comps, planes, rows_here, parts, share)  6.48 us
    mul x4, local copies, waits for them, and re-layouts, shards(): wall = -(grid[:, 1:2] * normal_first) + viscosity * normal_second  6.04 us
    ppermute x1, starting transfers between devices, halo_planes(): ahead = lax.ppermute(field, 'gx', [(i + 1, i) for i in range(count - 1)])  5.49 us
    dot_general x1, matrix products, shards(): jnp.dot(both, cols, precision=HIGHEST, preferred_element_type=jnp.float32)  4.69 us
  transfers between devices with their start and end apart: 5, of which 2 were waited for; matrix products, arithmetic and copies ran while one was open for 30% of the time, Pallas kernels for 0%

profile of v2, /device:TPU:33, one launch (start us, length us, event | category | flops | bytes accessed | tf_op | source)
XLA Modules:
  0.0 125.1 jit_solution(11891960661704819802)
XLA Ops:
  0.6 3.1 %collective-permute-start = (f32[3,4,24,768]{3,2,1,0:T(8,128)}, f32[3,4,24,768]{3,2,1,0:T(8,128)}, u32[]{:S(2)}, u32[]{:S(2)}) collective-permute-start(f32[3,4,24,768]{3,2,1,0:T(8,128)} %param.10), channel_id=1, source_target_pairs={{0,16},{16,32},{32,48},{48,64},{64,80},{80,96},{96,112},{112,128},... | collective-permute-start | bytes 2654216 | tf_op jit(solution)/shard_map/ppermute | solution.py:49
  3.8 5.5 %collective-permute-start.1 = (f32[3,4,24,768]{3,2,1,0:T(8,128)}, f32[3,4,24,768]{3,2,1,0:T(8,128)}, u32[]{:S(2)}, u32[]{:S(2)}) collective-permute-start(f32[3,4,24,768]{3,2,1,0:T(8,128)} %param.10), channel_id=1, source_target_pairs={{16,0},{32,16},{48,32},{64,48},{80,64},{96,80},{112,96},{128,112},... | collective-permute-start | bytes 2654216 | tf_op jit(solution)/shard_map/ppermute | solution.py:50
  9.3 3.3 %reshape.63 = f32[3,4,24,16,48]{4,3,2,1,0:T(8,128)} reshape(f32[3,4,24,768]{3,2,1,0:T(8,128)} %param.10) | data formatting | bytes 1769472 | tf_op jit(solution)/shard_map/reshape | solution.py:91
  12.5 3.2 %copy.35 = f32[3,4,24,16,48]{4,1,0,2,3:T(4,128)S(1)} copy(f32[3,4,24,16,48]{4,3,2,1,0:T(8,128)} %reshape.63) | data formatting | bytes 1769472 | tf_op jit(solution)/shard_map/reshape | solution.py:91
  15.7 2.1 %reshape.64 = f32[16,24,576]{2,1,0:T(8,128)} reshape(f32[16,24,3,4,48]{4,3,2,1,0:T(4,128)S(1)} %bitcast.34) | data formatting | bytes 1769472 | tf_op jit(solution)/shard_map/reshape | solution.py:92
  17.8 11.7 %all-to-all-start = ((f32[16,24,576]{2,1,0:T(8,128)}), f32[16,24,576]{2,1,0:T(8,128)S(1)}, u32[]{:S(2)}, u32[]{:S(2)}) async-start(f32[16,24,576]{2,1,0:T(8,128)} %reshape.64), calls=%async_computation | async-start | bytes 1966080 | tf_op jit(solution)/shard_map/all_to_all | solution.py:94
  29.7 8.3 %convolution_bitcast_fusion = f32[288,1536]{1,0:T(8,128)} fusion(f32[768,1536]{1,0:T(8,128)} %constant.45.clone, f32[288,768]{1,0:T(8,128)S(1)} %bitcast.33), kind=kOutput, calls=%fused_computation | convolution fusion | flops 4076863488 | bytes 7372800 | tf_op jit(solution)/shard_map/dot_general | solution.py:96
  38.7 1.6 %fusion.20 = (f32[288,768]{1,0:T(8,128)S(1)}, f32[288,768]{1,0:T(8,128)S(1)}) fusion(f32[288,1536]{1,0:T(8,128)} %convolution_bitcast_fusion), kind=kLoop, calls=%fused_computation.48 | loop fusion | flops 221184 | bytes 3538944 | tf_op jit(solution)/shard_map/slice | solution.py:102
  41.3 14.8 %all-to-all-done = f32[16,24,576]{2,1,0:T(8,128)S(1)} async-done(((f32[16,24,576]{2,1,0:T(8,128)}), f32[16,24,576]{2,1,0:T(8,128)S(1)}, u32[]{:S(2)}, u32[]{:S(2)}) %all-to-all-start) | async-done | bytes 884768 | tf_op jit(solution)/shard_map/all_to_all | solution.py:94
  56.5 1.6 %fusion.6 = f32[384,144]{0,1:T(8,128)} fusion(f32[384,144]{0,1:T(8,128)S(1)} %bitcast.44, f32[384]{0:T(512)S(1)} %select_reduce_fusion, s32[384]{0:T(512)S(1)} %broadcast_add_fusion, f32[384]{0:T(512)S(1)} %broadcast_subtract_fusion, s32[384]{0:T(512)S(1)} %copy-done.5), kind=kOutput, calls=%fused_computation.20 | convolution fusion | flops 255541248 | bytes 448512 | tf_op jit(solution)/shard_map/dot_general | solution.py:112
  61.9 1.4 %mul.172 = f32[384,3,4,48]{3,2,1,0:T(4,128)S(1)} broadcast(f32[384,4,48]{2,1,0:T(4,128)} %copy.28), dimensions={0,2,3} | broadcast | bytes 1179648 | tf_op jit(solution)/shard_map/mul | solution.py:119
  63.3 2.1 %mul.173 = f32[16,24,576]{2,1,0:T(8,128)} reshape(f32[384,3,4,48]{3,2,1,0:T(4,128)S(1)} %mul.172) | data formatting | bytes 1769472 | tf_op jit(solution)/shard_map/mul | solution.py:119
  65.5 4.7 %fusion = f32[768,576]{0,1:T(8,128)S(1)} fusion(f32[384,576]{1,0:T(8,128)} %bitcast.37, f32[384,384]{1,0:T(8,128)} %param.13, f32[384,384]{1,0:T(8,128)} %param.12), kind=kOutput, calls=%fused_computation.7 | convolution fusion | flops 2038726656 | bytes 3833856 | tf_op jit(solution)/shard_map/dot_general | solution.py:116
  72.9 2.1 %copy.31 = f32[384,3,48]{2,1,0:T(4,128)} copy(f32[384,3,48]{0,2,1:T(8,128)} %bitcast.14) | data formatting | bytes 442368 | tf_op jit(solution)/shard_map/mul | solution.py:122
  75.0 2.1 %multiply_select_fusion = f32[384,3,4,48]{3,2,1,0:T(4,128)S(1)} fusion(f32[384,4,48]{2,1,0:T(4,128)} %copy.32, f32[384,3,48]{2,1,0:T(4,128)} %copy.31, pred[]{:T(512)S(6)} %eq.46), kind=kLoop, calls=%fused_computation.2 | loop fusion | flops 442368 | bytes 1400833 | tf_op jit(solution)/shard_map/jit(_where)/select_n | solution.py:123
  77.1 2.1 %select_n.38 = f32[16,24,576]{2,1,0:T(8,128)} reshape(f32[384,3,4,48]{3,2,1,0:T(4,128)S(1)} %multiply_select_fusion) | data formatting | bytes 1769472 | tf_op jit(solution)/shard_map/jit(_where)/select_n | solution.py:123
  79.2 3.2 %add_add_fusion = f32[16,24,576]{2,1,0:T(8,128)} fusion(f32[16,24,576]{2,1,0:T(8,128)} %select_n.38, f32[16,24,576]{2,1,0:T(8,128)} %bitcast.39, f32[16,24,576]{2,1,0:T(8,128)} %mul.173, f32[16,24,576]{2,1,0:T(8,128)} %bitcast.38), kind=kLoop, calls=%fused_computation.11 | loop fusion | flops 884736 | bytes 4423680 | tf_op jit(solution)/shard_map/add | solution.py:123
  82.4 4.4 %all-to-all-start.1 = ((f32[16,24,576]{2,1,0:T(8,128)}), f32[16,24,576]{2,1,0:T(8,128)}, u32[]{:S(2)}, u32[]{:S(2)}) async-start(f32[16,24,576]{2,1,0:T(8,128)} %add_add_fusion), calls=%async_computation.1 | async-start | bytes 1966080 | tf_op jit(solution)/shard_map/all_to_all | solution.py:125
  86.9 2.8 %broadcast_select_fusion = (f32[3,4,24,768]{3,2,1,0:T(8,128)}, f32[3,8,24,768]{3,2,1,0:T(8,128)}) fusion(f32[3,4,24,768]{3,2,1,0:T(8,128)} %collective-permute-done.1, f32[3,24,768]{2,1,0:T(8,128)S(1)} %slice_bitcast_fusion.3, pred[]{:T(512)S(6)} %eq.22, f32[3,4,24,768]{3,2,1,0:T(8,128)} %collective-permute-done), kind=kLoop, calls=%fused_computation.26 | loop fusion | flops 221183 | bytes 3760129 | tf_op jit(solution)/shard_map/jit(_where)/select_n | solution.py:58
  90.7 21.8 %all-to-all-done.1 = f32[16,24,576]{2,1,0:T(8,128)} async-done(((f32[16,24,576]{2,1,0:T(8,128)}), f32[16,24,576]{2,1,0:T(8,128)}, u32[]{:S(2)}, u32[]{:S(2)}) %all-to-all-start.1) | async-done | bytes 884768 | tf_op jit(solution)/shard_map/all_to_all | solution.py:125
  112.6 2.5 %reshape.70 = f32[16,24,3,4,48]{4,3,2,1,0:T(4,128)S(1)} reshape(f32[16,24,576]{2,1,0:T(8,128)} %all-to-all-done.1) | data formatting | bytes 1769472 | tf_op jit(solution)/shard_map/reshape | solution.py:126
  115.1 2.8 %copy.33 = f32[3,4,24,16,48]{4,3,2,1,0:T(8,128)} copy(f32[3,4,24,16,48]{4,1,0,2,3:T(4,128)S(1)} %bitcast.35) | data formatting | bytes 1769472 | tf_op jit(solution)/shard_map/transpose | solution.py:126
  117.9 2.6 %reshape.71 = f32[3,4,24,768]{3,2,1,0:T(8,128)S(1)} reshape(f32[3,4,24,16,48]{4,3,2,1,0:T(8,128)} %copy.33) | data formatting | bytes 1769472 | tf_op jit(solution)/shard_map/reshape | solution.py:127
  120.5 4.5 %multiply_add_fusion = (f32[3,4,24,768]{3,2,1,0:T(8,128)}, f32[3,4,24,768]{3,2,1,0:T(8,128)}) fusion(f32[3,4,24,768]{3,2,1,0:T(8,128)S(1)} %copy-done, f32[3,4,24,768]{3,2,1,0:T(8,128)S(1)} %reshape.71, f32[3,4,24,768]{3,2,1,0:T(8,128)S(1)} %copy-done.2, f32[3,4,24,768]{3,2,1,0:T(8,128)S(1)} %copy-done.3, f32[3,4,24,768]{3,2,1,0:T(8,128)} %collective-permute-done, ...), kind=kLoop, calls=%fused_computation.17 | loop fusion | flops 8404992 | bytes 10027008 | tf_op jit(solution)/shard_map/add | solution.py:132
  (37 shorter events, 9.8 us)
Async XLA Ops:
  0.6 40.7 %collective-permute-start = (f32[3,4,24,768]{3,2,1,0:T(8,128)}, f32[3,4,24,768]{3,2,1,0:T(8,128)}, u32[]{:S(2)}, u32[]{:S(2)}) collective-permute-start(f32[3,4,24,768]{3,2,1,0:T(8,128)} %param.10), channel_id=1, source_target_pairs={{0,16},{16,32},{32,48},{48,64},{64,80},{80,96},{96,112},{112,128},... | collective-permute-start | bytes 2654216 | tf_op jit(solution)/shard_map/ppermute | solution.py:49
  3.8 37.6 %collective-permute-start.1 = (f32[3,4,24,768]{3,2,1,0:T(8,128)}, f32[3,4,24,768]{3,2,1,0:T(8,128)}, u32[]{:S(2)}, u32[]{:S(2)}) collective-permute-start(f32[3,4,24,768]{3,2,1,0:T(8,128)} %param.10), channel_id=1, source_target_pairs={{16,0},{32,16},{48,32},{64,48},{80,64},{96,80},{112,96},{128,112},... | collective-permute-start | bytes 2654216 | tf_op jit(solution)/shard_map/ppermute | solution.py:50
  17.8 11.7 %copy-start.4 = (s32[384]{0:T(512)S(1)}, s32[384]{0:T(512)}, u32[]{:S(2)}) copy-start(s32[384]{0:T(512)} %param.15) | copy-start | bytes 4612
  17.8 11.7 %copy-start.8 = (f32[64]{0:T(128)S(1)}, f32[64]{0:T(128)}, u32[]{:S(2)}) copy-start(f32[64]{0:T(128)} %param.16) | copy-start | bytes 772
  17.8 11.8 %copy-start = (f32[3,4,24,768]{3,2,1,0:T(8,128)S(1)}, f32[3,4,24,768]{3,2,1,0:T(8,128)}, u32[]{:S(2)}) copy-start(f32[3,4,24,768]{3,2,1,0:T(8,128)} %param.10) | copy-start | bytes 2654212
  17.8 38.3 %all-to-all-start = ((f32[16,24,576]{2,1,0:T(8,128)}), f32[16,24,576]{2,1,0:T(8,128)S(1)}, u32[]{:S(2)}, u32[]{:S(2)}) async-start(f32[16,24,576]{2,1,0:T(8,128)} %reshape.64), calls=%async_computation | async-start | bytes 1966080 | tf_op jit(solution)/shard_map/all_to_all | solution.py:94
  29.7 8.3 %copy-start.5 = (s32[384]{0:T(512)S(1)}, s32[384]{0:T(512)}, u32[]{:S(2)}) copy-start(s32[384]{0:T(512)} %param.14) | copy-start | bytes 4612
  41.3 18.2 %copy-start.6 = (f32[4]{0:T(128)S(1)}, f32[4]{0:T(128)}, u32[]{:S(2)}) copy-start(f32[4]{0:T(128)} %constant.50) | copy-start | bytes 52
  41.3 18.2 %copy-start.7 = (f32[4]{0:T(128)S(1)}, f32[4]{0:T(128)}, u32[]{:S(2)}) copy-start(f32[4]{0:T(128)} %constant.51) | copy-start | bytes 52
  56.2 3.4 %copy-start.1 = (f32[16,24,576]{2,1,0:T(8,128)}, f32[16,24,576]{2,1,0:T(8,128)S(1)}, u32[]{:S(2)}) copy-start(f32[16,24,576]{2,1,0:T(8,128)S(1)} %all-to-all-done) | copy-start | bytes 2654212
  58.1 14.8 %collective-permute-start.2 = (f32[384,144]{0,1:T(8,128)}, f32[384,144]{0,1:T(8,128)}, u32[]{:S(2)}, u32[]{:S(2)}) collective-permute-start(f32[384,144]{0,1:T(8,128)} %fusion.6), channel_id=1, source_target_pairs={{496,0},{497,1},{498,2},{499,3},{500,4},{501,5},{502,6},{503,7},{5... | collective-permute-start | bytes 663560 | tf_op jit(solution)/shard_map/ppermute | solution.py:113
  82.4 30.2 %all-to-all-start.1 = ((f32[16,24,576]{2,1,0:T(8,128)}), f32[16,24,576]{2,1,0:T(8,128)}, u32[]{:S(2)}, u32[]{:S(2)}) async-start(f32[16,24,576]{2,1,0:T(8,128)} %add_add_fusion), calls=%async_computation.1 | async-start | bytes 1966080 | tf_op jit(solution)/shard_map/all_to_all | solution.py:125
  117.9 2.6 %copy-start.2 = (f32[3,4,24,768]{3,2,1,0:T(8,128)S(1)}, f32[3,4,24,768]{3,2,1,0:T(8,128)}, u32[]{:S(2)}) copy-start(f32[3,4,24,768]{3,2,1,0:T(8,128)} %negate_add_fusion) | copy-start | bytes 2654212
  117.9 2.6 %copy-start.3 = (f32[3,4,24,768]{3,2,1,0:T(8,128)S(1)}, f32[3,4,24,768]{3,2,1,0:T(8,128)}, u32[]{:S(2)}) copy-start(f32[3,4,24,768]{3,2,1,0:T(8,128)} %get-tuple-element.20) | copy-start | bytes 2654212

commit v3 on v2

--- a/solution.py
+++ b/solution.py
@@ -4,6 +4,8 @@
 import jax
 import jax.numpy as jnp
 from jax import lax
+from jax.experimental import pallas as pl
+from jax.experimental.pallas import tpu as pltpu
 from jax.sharding import PartitionSpec as P
 
 HALO = 4
@@ -78,19 +80,90 @@
     return lower + upper
 
 
+def pack_columns(velocity, parts):
+    comps, planes, rows_here, span = velocity.shape
+    share = span // parts
+
+    def kernel(v_ref, o_ref):
+        for d in range(parts):
+            pieces = [
+                v_ref[c, x, :, share * d : share * (d + 1)] for c in range(comps) for x in range(planes)
+            ]
+            o_ref[d] = jnp.concatenate(pieces, axis=1)
+
+    return pl.pallas_call(
+        kernel,
+        out_shape=jax.ShapeDtypeStruct((parts, rows_here, comps * planes * share), jnp.float32),
+    )(velocity)
+
+
+def wall_block(cols, both, inflow, inlet, planes):
+    rows, width = cols.shape
+    comps = 3
+    share = width // (comps * planes)
+    lower, upper = ghost_weights(planes)
+
+    def kernel(inlet_ref, c_ref, w_ref, f_ref, o_ref):
+        derived = jnp.dot(w_ref[...], c_ref[...], precision=HIGHEST, preferred_element_type=jnp.float32)
+        block = planes * share
+        v1 = c_ref[:, block : 2 * block]
+        at_inlet = inlet_ref[0] > 0
+        for c in range(comps):
+            first = derived[:rows, c * block : (c + 1) * block]
+            second = derived[rows:, c * block : (c + 1) * block]
+            wall = -(v1 * first) + viscosity * second
+            flow = f_ref[:, c * share : (c + 1) * share]
+            ghost = jnp.concatenate(
+                [
+                    flow * (c_ref[:, x * share : (x + 1) * share] * lower[x] + viscosity * upper[x])
+                    for x in range(planes)
+                ],
+                axis=1,
+            )
+            o_ref[:, c * block : (c + 1) * block] = wall + jnp.where(at_inlet, ghost, 0.0)
+
+    return pl.pallas_call(
+        kernel,
+        out_shape=jax.ShapeDtypeStruct((rows, width), jnp.float32),
+        in_specs=[
+            pl.BlockSpec(memory_space=pltpu.SMEM),
+            pl.BlockSpec(memory_space=pltpu.VMEM),
+            pl.BlockSpec(memory_space=pltpu.VMEM),
+            pl.BlockSpec(memory_space=pltpu.VMEM),
+        ],
+    )(inlet, cols, both, inflow)
+
+
+def combine(velocity, accumulated, local_terms, back):
+    comps, planes, rows_here, span = velocity.shape
+    parts = back.shape[0]
+    share = span // parts
+
+    def kernel(v_ref, a_ref, t_ref, b_ref, nv_ref, na_ref):
+        for c in range(comps):
+            for x in range(planes):
+                k = (c * planes + x) * share
+                wall = jnp.concatenate([b_ref[d, :, k : k + share] for d in range(parts)], axis=1)
+                tendency = t_ref[c, x] + wall
+                acc = keep_rate * a_ref[c, x] + step_size * tendency
+                na_ref[c, x] = acc
+                nv_ref[c, x] = v_ref[c, x] + update_rate * acc
+
+    shape = jax.ShapeDtypeStruct(velocity.shape, jnp.float32)
+    return pl.pallas_call(kernel, out_shape=(shape, shape))(velocity, accumulated, local_terms, back)
+
+
 def shards(
     velocity, accumulated, wall_first, wall_second, recycle_rows, weight_index, weight_table
 ):
     comps, planes, rows_here, span = velocity.shape
     parts = lax.axis_size("ga")
-    slabs = lax.axis_size("gx")
     share = span // parts
     rows = rows_here * parts
     width = comps * planes * share
 
-    send = velocity.reshape(comps, planes, rows_here, parts, share)
-    send = send.transpose(3, 2, 0, 1, 4).reshape(parts, rows_here, width)
     behind, ahead = halo_planes(velocity)
+    send = pack_columns(velocity, parts)
     cols = lax.all_to_all(send, "ga", 0, 0, tiled=True).reshape(rows, width)
     lines = velocity.reshape(-1, span)
     spectral = jnp.dot(
@@ -101,35 +174,25 @@
     )
     span_first = spectral[:, :span].reshape(velocity.shape)
     span_second = spectral[:, span:].reshape(velocity.shape)
-
     span_terms = -(velocity[2:3] * span_first) + viscosity * span_second
     cols, span_terms, behind, ahead = lax.optimization_barrier((cols, span_terms, behind, ahead))
-    grid = cols.reshape(rows, comps, planes, share)
 
     source_slab, source_plane = divmod(RECYCLE_PLANE, planes)
     mix = interpolation_matrix(recycle_rows, weight_index, weight_table, rows)
-    plane = grid[:, :, source_plane, :].reshape(rows, comps * share)
+    plane = jnp.concatenate(
+        [cols[:, (c * planes + source_plane) * share : (c * planes + source_plane + 1) * share] for c in range(comps)],
+        axis=1,
+    )
     inflow = jnp.dot(mix, plane, precision=HIGHEST, preferred_element_type=jnp.float32)
-    inflow = lax.ppermute(inflow, "gx", [(source_slab, 0)]).reshape(rows, comps, 1, share)
+    inflow = lax.ppermute(inflow, "gx", [(source_slab, 0)])
 
     both = jnp.concatenate([wall_first, wall_second], 0)
-    derived = jnp.dot(both, cols, precision=HIGHEST, preferred_element_type=jnp.float32)
-    normal_first = derived[:rows].reshape(rows, comps, planes, share)
-    normal_second = derived[rows:].reshape(rows, comps, planes, share)
-    wall = -(grid[:, 1:2] * normal_first) + viscosity * normal_second
-
-    lower, upper = ghost_weights(planes)
-    ghost = inflow * (grid[:, 0:1] * lower[None, None, :, None] + viscosity * upper[None, None, :, None])
-    wall = wall + jnp.where(lax.axis_index("gx") == 0, ghost, 0.0)
-
+    inlet = (lax.axis_index("gx") == 0).astype(jnp.int32).reshape(1)
+    wall = wall_block(cols, both, inflow, inlet, planes)
     back = lax.all_to_all(wall.reshape(parts, rows_here, width), "ga", 0, 0, tiled=True)
-    back = back.reshape(parts, rows_here, comps, planes, share).transpose(2, 3, 1, 0, 4)
-    back = back.reshape(comps, planes, rows_here, span)
-
-    tendency = span_terms + streamwise(velocity, behind, ahead)
-    tendency = tendency + back
-    accumulated_next = keep_rate * accumulated + step_size * tendency
-    return (velocity + update_rate * accumulated_next, accumulated_next)
+
+    local_terms = span_terms + streamwise(velocity, behind, ahead)
+    return combine(velocity, accumulated, local_terms, back)
 
 
 def solution(mesh):

time: 126 us -> 109 us (0.87)
  the two profiles are of different devices: /device:TPU:33 before, /device:TPU:1 now
where the time goes in v3:
time: 109 us
  waiting for transfers between devices  53.6 us (49%)
  starting transfers between devices  23.7 us (22%)
  Pallas kernels  13.2 us (12%)
  matrix products  8.54 us (8%)
  other arithmetic  6.83 us (6%)
  local copies, waits for them, and re-layouts  2 us (2%)
    all_to_all x1, waiting for transfers between devices, shards(): lax.all_to_all(wall.reshape(parts, rows_here, width), 'ga', 0, 0, tiled=T...  23.2 us
    all_to_all x1, waiting for transfers between devices, shards(): cols = lax.all_to_all(send, 'ga', 0, 0, tiled=True).reshape(rows, width)  18.6 us
    all_to_all x1, starting transfers between devices, shards(): cols = lax.all_to_all(send, 'ga', 0, 0, tiled=True).reshape(rows, width)  11.8 us
    ppermute x1, waiting for transfers between devices, shards(): inflow = lax.ppermute(inflow, 'gx', [(source_slab, 0)])  11.7 us
    dot_general x1, matrix products, shards(): jnp.dot(lines, jnp.asarray(spanwise_table(span)), precision=HIGHEST, pref...  6.66 us
    pallas_call x1, Pallas kernels, wall_block(): pl.pallas_call(kernel, out_shape=jax.ShapeDtypeStruct((rows, width), jnp....  6.45 us
    ppermute x1, starting transfers between devices, halo_planes(): behind = lax.ppermute(field, 'gx', [(i, i + 1) for i in range(count - 1)])  4.63 us
    all_to_all x1, starting transfers between devices, shards(): lax.all_to_all(wall.reshape(parts, rows_here, width), 'ga', 0, 0, tiled=T...  4.59 us
  transfers between devices with their start and end apart: 5, of which 3 were waited for; matrix products, arithmetic and copies ran while one was open for 13% of the time, Pallas kernels for 3%

profile of v3, /device:TPU:1, one launch (start us, length us, event | category | flops | bytes accessed | tf_op | source)
XLA Modules:
  0.0 108.7 jit_solution(5396960376499775125)
XLA Ops:
  0.7 1.4 %collective-permute-start.1 = (f32[3,4,24,768]{3,2,1,0:T(8,128)}, f32[3,4,24,768]{3,2,1,0:T(8,128)}, u32[]{:S(2)}, u32[]{:S(2)}) collective-permute-start(f32[3,4,24,768]{3,2,1,0:T(8,128)} %v_ref.3), channel_id=1, source_target_pairs={{16,0},{32,16},{48,32},{64,48},{80,64},{96,80},{112,96},{128,112},... | collective-permute-start | bytes 2654216 | tf_op jit(solution)/shard_map/ppermute | solution.py:52
  2.1 4.6 %collective-permute-start = (f32[3,4,24,768]{3,2,1,0:T(8,128)}, f32[3,4,24,768]{3,2,1,0:T(8,128)S(1)}, u32[]{:S(2)}, u32[]{:S(2)}) collective-permute-start(f32[3,4,24,768]{3,2,1,0:T(8,128)} %v_ref.3), channel_id=1, source_target_pairs={{0,16},{16,32},{32,48},{48,64},{64,80},{80,96},{96,112},{112,128},... | collective-permute-start | bytes 2654216 | tf_op jit(solution)/shard_map/ppermute | solution.py:51
  6.7 2.9 %shard_map.95 = f32[16,24,576]{2,1,0:T(8,128)} custom-call(f32[3,4,24,768]{3,2,1,0:T(8,128)} %v_ref.3), custom_call_target="tpu_custom_call" | custom-call | tf_op jit(solution)/shard_map/pallas_call | solution.py:94
  9.6 11.8 %all-to-all-start = ((f32[16,24,576]{2,1,0:T(8,128)}), f32[16,24,576]{2,1,0:T(8,128)S(1)}, u32[]{:S(2)}, u32[]{:S(2)}) async-start(f32[16,24,576]{2,1,0:T(8,128)} %shard_map.95), calls=%async_computation | async-start | bytes 1966080 | tf_op jit(solution)/shard_map/all_to_all | solution.py:167
  21.4 0.1 select_reduce_fusion
  21.5 6.7 %convolution_bitcast_fusion = f32[288,1536]{1,0:T(8,128)S(1)} fusion(f32[768,1536]{1,0:T(8,128)} %constant.36.clone, f32[288,768]{1,0:T(8,128)S(1)} %bitcast.16), kind=kOutput, calls=%fused_computation | convolution fusion | flops 4076863488 | bytes 7372800 | tf_op jit(solution)/shard_map/dot_general | solution.py:169
  28.3 0.1 fusion.18
  28.4 1.0 negate_add_fusion
  29.4 18.6 %all-to-all-done = f32[16,24,576]{2,1,0:T(8,128)S(1)} async-done(((f32[16,24,576]{2,1,0:T(8,128)}), f32[16,24,576]{2,1,0:T(8,128)S(1)}, u32[]{:S(2)}, u32[]{:S(2)}) %all-to-all-start) | async-done | bytes 884768 | tf_op jit(solution)/shard_map/all_to_all | solution.py:167
  48.0 0.1 fusion.19
  48.1 1.9 %fusion.2 = f32[384,144]{1,0:T(8,128)} fusion(f32[384,48]{1,0:T(8,128)S(1)} %get-tuple-element.13, f32[384,48]{1,0:T(8,128)S(1)} %get-tuple-element.14, f32[384,48]{1,0:T(8,128)S(1)} %get-tuple-element.12, f32[384]{0:T(512)S(1)} %select_reduce_fusion, s32[384]{0:T(512)S(1)} %broadcast_add_fusion, f32[384]{0:T(512)S(1)} %broadcast_subtract_fusion, ...), kind=kOutput, calls=%fused_computation.12 | convolution fusion | flops 255651840 | bytes 448512 | tf_op jit(solution)/shard_map/dot_general | solution.py:186
  50.0 1.3 %collective-permute-start.2 = (f32[384,144]{1,0:T(8,128)}, f32[384,144]{1,0:T(8,128)S(1)}, u32[]{:S(2)}, u32[]{:S(2)}) collective-permute-start(f32[384,144]{1,0:T(8,128)} %fusion.2), channel_id=1, source_target_pairs={{496,0},{497,1},{498,2},{499,3},{500,4},{501,5},{502,6},{503,7},{5... | collective-permute-start | bytes 663560 | tf_op jit(solution)/shard_map/ppermute | solution.py:187
  51.3 2.3 %pad_maximum_fusion.w_ref = f32[768,384]{1,0:T(8,128)} fusion(f32[384,384]{1,0:T(8,128)} %param.11, f32[384,384]{1,0:T(8,128)} %param.10), kind=kLoop, calls=%fused_computation.5 | loop fusion | flops 294912 | bytes 2359296 | tf_op jit(solution)/shard_map/concatenate | solution.py:189
  53.6 11.7 %collective-permute-done.2.f_ref = f32[384,144]{1,0:T(8,128)S(1)} collective-permute-done((f32[384,144]{1,0:T(8,128)}, f32[384,144]{1,0:T(8,128)S(1)}, u32[]{:S(2)}, u32[]{:S(2)}) %collective-permute-start.2) | collective-permute-done | bytes 221216 | tf_op jit(solution)/shard_map/ppermute | solution.py:187
  65.4 0.7 copy-done.4
  66.1 6.4 %shard_map.96 = f32[384,576]{1,0:T(8,128)} custom-call(s32[1]{0:T(128)} %bitcast.8.inlet_ref, f32[384,576]{1,0:T(8,128)} %bitcast.18, f32[768,384]{1,0:T(8,128)} %pad_maximum_fusion.w_ref, f32[384,144]{1,0:T(8,128)} %copy-done.4), custom_call_target="tpu_custom_call" | custom-call | tf_op jit(solution)/shard_map/pallas_call | solution.py:125
  72.6 4.6 %all-to-all-start.1 = ((f32[16,24,576]{2,1,0:T(8,128)}), f32[16,24,576]{2,1,0:T(8,128)S(1)}, u32[]{:S(2)}, u32[]{:S(2)}) async-start(f32[16,24,576]{2,1,0:T(8,128)} %bitcast.19), calls=%async_computation.1 | async-start | bytes 1966080 | tf_op jit(solution)/shard_map/all_to_all | solution.py:192
  77.2 0.1 constant_dynamic-update-slice_fusion.1
  77.3 1.4 %broadcast_select_fusion = (f32[3,4,24,768]{3,2,1,0:T(8,128)S(1)}, f32[3,8,24,768]{3,2,1,0:T(8,128)S(1)}) fusion(f32[3,4,24,768]{3,2,1,0:T(8,128)} %collective-permute-done.1, f32[3,24,768]{2,1,0:T(8,128)S(1)} %slice_bitcast_fusion.2, pred[]{:T(512)S(6)} %eq.22, f32[3,8,24,768]{3,2,1,0:T(8,128)S(1)} %constant_dynamic-update-slice_fusion.1, ...), kind=kLoop, calls=%fused_computation.18 | loop fusion | flops 221184 | bytes 3760129 | tf_op jit(solution)/shard_map/jit(_where)/select_n | solution.py:60
  78.7 0.0 copy-done.3
  78.7 1.8 %add_add_fusion.t_ref = f32[3,4,24,768]{3,2,1,0:T(8,128)} fusion(f32[3,4,24,768]{3,2,1,0:T(8,128)S(1)} %copy-done.3, f32[3,4,24,768]{3,2,1,0:T(8,128)S(1)} %get-tuple-element.17, f32[3,4,24,768]{3,2,1,0:T(8,128)S(1)} %collective-permute-done, f32[3,4,24,768]{3,2,1,0:T(8,128)S(1)} %copy-done, f32[3,8,24,768]{3,2,1,0:T(8,128)S(1)} %get-tuple-element.18, ...), kind=kLoop, calls=%fused_computation.10 | loop fusion | flops 7077888 | bytes 7372800 | tf_op jit(solution)/shard_map/add | solution.py:194
  80.5 23.2 %all-to-all-done.1.b_ref = f32[16,24,576]{2,1,0:T(8,128)S(1)} async-done(((f32[16,24,576]{2,1,0:T(8,128)}), f32[16,24,576]{2,1,0:T(8,128)S(1)}, u32[]{:S(2)}, u32[]{:S(2)}) %all-to-all-start.1) | async-done | bytes 884768 | tf_op jit(solution)/shard_map/all_to_all | solution.py:192
  103.8 1.0 copy-done.2
  104.7 3.9 %shard_map.97 = (f32[3,4,24,768]{3,2,1,0:T(8,128)}, f32[3,4,24,768]{3,2,1,0:T(8,128)}) custom-call(f32[3,4,24,768]{3,2,1,0:T(8,128)} %v_ref.3, f32[3,4,24,768]{3,2,1,0:T(8,128)} %a_ref.1, f32[3,4,24,768]{3,2,1,0:T(8,128)} %add_add_fusion.t_ref, f32[16,24,576]{2,1,0:T(8,128)} %copy-done.2), custom_call_target="tpu_custom_call" | custom-call | tf_op jit(solution)/shard_map/pallas_call | solution.py:153
  (19 shorter events, 0.1 us)
Async XLA Ops:
  0.6 20.9 %copy-start = (f32[3,4,24,768]{3,2,1,0:T(8,128)S(1)}, f32[3,4,24,768]{3,2,1,0:T(8,128)}, u32[]{:S(2)}) copy-start(f32[3,4,24,768]{3,2,1,0:T(8,128)} %v_ref.3) | copy-start | bytes 2654212
  0.6 20.8 %copy-start.7 = (f32[64]{0:T(128)S(1)}, f32[64]{0:T(128)}, u32[]{:S(2)}) copy-start(f32[64]{0:T(128)} %param.14) | copy-start | bytes 772
  0.7 20.8 %copy-start.5 = (s32[384]{0:T(512)S(1)}, s32[384]{0:T(512)}, u32[]{:S(2)}) copy-start(s32[384]{0:T(512)} %param.13) | copy-start | bytes 4612
  0.7 28.8 %collective-permute-start.1 = (f32[3,4,24,768]{3,2,1,0:T(8,128)}, f32[3,4,24,768]{3,2,1,0:T(8,128)}, u32[]{:S(2)}, u32[]{:S(2)}) collective-permute-start(f32[3,4,24,768]{3,2,1,0:T(8,128)} %v_ref.3), channel_id=1, source_target_pairs={{16,0},{32,16},{48,32},{64,48},{80,64},{96,80},{112,96},{128,112},... | collective-permute-start | bytes 2654216 | tf_op jit(solution)/shard_map/ppermute | solution.py:52
  2.1 27.3 %collective-permute-start = (f32[3,4,24,768]{3,2,1,0:T(8,128)}, f32[3,4,24,768]{3,2,1,0:T(8,128)S(1)}, u32[]{:S(2)}, u32[]{:S(2)}) collective-permute-start(f32[3,4,24,768]{3,2,1,0:T(8,128)} %v_ref.3), channel_id=1, source_target_pairs={{0,16},{16,32},{32,48},{48,64},{64,80},{80,96},{96,112},{112,128},... | collective-permute-start | bytes 2654216 | tf_op jit(solution)/shard_map/ppermute | solution.py:51
  9.6 38.4 %all-to-all-start = ((f32[16,24,576]{2,1,0:T(8,128)}), f32[16,24,576]{2,1,0:T(8,128)S(1)}, u32[]{:S(2)}, u32[]{:S(2)}) async-start(f32[16,24,576]{2,1,0:T(8,128)} %shard_map.95), calls=%async_computation | async-start | bytes 1966080 | tf_op jit(solution)/shard_map/all_to_all | solution.py:167
  21.5 6.7 %copy-start.6 = (s32[384]{0:T(512)S(1)}, s32[384]{0:T(512)}, u32[]{:S(2)}) copy-start(s32[384]{0:T(512)} %param.12) | copy-start | bytes 4612
  48.0 5.6 %copy-start.1 = (f32[16,24,576]{2,1,0:T(8,128)}, f32[16,24,576]{2,1,0:T(8,128)S(1)}, u32[]{:S(2)}) copy-start(f32[16,24,576]{2,1,0:T(8,128)S(1)} %all-to-all-done) | copy-start | bytes 2654212
  50.0 15.4 %collective-permute-start.2 = (f32[384,144]{1,0:T(8,128)}, f32[384,144]{1,0:T(8,128)S(1)}, u32[]{:S(2)}, u32[]{:S(2)}) collective-permute-start(f32[384,144]{1,0:T(8,128)} %fusion.2), channel_id=1, source_target_pairs={{496,0},{497,1},{498,2},{499,3},{500,4},{501,5},{502,6},{503,7},{5... | collective-permute-start | bytes 663560 | tf_op jit(solution)/shard_map/ppermute | solution.py:187
  65.4 0.7 copy-start.4
  72.6 31.2 %all-to-all-start.1 = ((f32[16,24,576]{2,1,0:T(8,128)}), f32[16,24,576]{2,1,0:T(8,128)S(1)}, u32[]{:S(2)}, u32[]{:S(2)}) async-start(f32[16,24,576]{2,1,0:T(8,128)} %bitcast.19), calls=%async_computation.1 | async-start | bytes 1966080 | tf_op jit(solution)/shard_map/all_to_all | solution.py:192
  77.3 1.4 %copy-start.3 = (f32[3,4,24,768]{3,2,1,0:T(8,128)S(1)}, f32[3,4,24,768]{3,2,1,0:T(8,128)}, u32[]{:S(2)}) copy-start(f32[3,4,24,768]{3,2,1,0:T(8,128)} %negate_add_fusion) | copy-start | bytes 2654212
  103.8 1.0 copy-start.2

commit v4 on v3

--- a/solution.py
+++ b/solution.py
@@ -97,21 +97,35 @@
     )(velocity)
 
 
-def wall_block(cols, both, inflow, inlet, planes):
+def wall_block(cols, wall_first, wall_second, planes):
+    rows, width = cols.shape
+    comps = 3
+    block = width // comps
+
+    def kernel(c_ref, f_ref, s_ref, o_ref):
+        field = c_ref[...]
+        first = jnp.dot(f_ref[...], field, precision=HIGHEST, preferred_element_type=jnp.float32)
+        second = jnp.dot(s_ref[...], field, precision=HIGHEST, preferred_element_type=jnp.float32)
+        v1 = c_ref[:, block : 2 * block]
+        for c in range(comps):
+            part = slice(c * block, (c + 1) * block)
+            o_ref[:, part] = -(v1 * first[:, part]) + viscosity * second[:, part]
+
+    return pl.pallas_call(kernel, out_shape=jax.ShapeDtypeStruct((rows, width), jnp.float32))(
+        cols, wall_first, wall_second
+    )
+
+
+def add_ghost(wall, cols, inflow, inlet, planes):
     rows, width = cols.shape
     comps = 3
     share = width // (comps * planes)
+    block = planes * share
     lower, upper = ghost_weights(planes)
 
-    def kernel(inlet_ref, c_ref, w_ref, f_ref, o_ref):
-        derived = jnp.dot(w_ref[...], c_ref[...], precision=HIGHEST, preferred_element_type=jnp.float32)
-        block = planes * share
-        v1 = c_ref[:, block : 2 * block]
+    def kernel(inlet_ref, w_ref, c_ref, f_ref, o_ref):
         at_inlet = inlet_ref[0] > 0
         for c in range(comps):
-            first = derived[:rows, c * block : (c + 1) * block]
-            second = derived[rows:, c * block : (c + 1) * block]
-            wall = -(v1 * first) + viscosity * second
             flow = f_ref[:, c * share : (c + 1) * share]
             ghost = jnp.concatenate(
                 [
@@ -120,7 +134,8 @@
                 ],
                 axis=1,
             )
-            o_ref[:, c * block : (c + 1) * block] = wall + jnp.where(at_inlet, ghost, 0.0)
+            part = slice(c * block, (c + 1) * block)
+            o_ref[:, part] = w_ref[:, part] + jnp.where(at_inlet, ghost, 0.0)
 
     return pl.pallas_call(
         kernel,
@@ -131,7 +146,8 @@
             pl.BlockSpec(memory_space=pltpu.VMEM),
             pl.BlockSpec(memory_space=pltpu.VMEM),
         ],
-    )(inlet, cols, both, inflow)
+        input_output_aliases={1: 0},
+    )(inlet, wall, cols, inflow)
 
 
 def combine(velocity, accumulated, local_terms, back):
@@ -165,7 +181,19 @@
     behind, ahead = halo_planes(velocity)
     send = pack_columns(velocity, parts)
     cols = lax.all_to_all(send, "ga", 0, 0, tiled=True).reshape(rows, width)
-    lines = velocity.reshape(-1, span)
+    cols, behind, ahead, field = lax.optimization_barrier((cols, behind, ahead, velocity))
+
+    source_slab, source_plane = divmod(RECYCLE_PLANE, planes)
+    mix = interpolation_matrix(recycle_rows, weight_index, weight_table, rows)
+    plane = jnp.concatenate(
+        [cols[:, (c * planes + source_plane) * share : (c * planes + source_plane + 1) * share] for c in range(comps)],
+        axis=1,
+    )
+    inflow = jnp.dot(mix, plane, precision=HIGHEST, preferred_element_type=jnp.float32)
+    inflow = lax.ppermute(inflow, "gx", [(source_slab, 0)])
+
+    wall = wall_block(cols, wall_first, wall_second, planes)
+    lines = field.reshape(-1, span)
     spectral = jnp.dot(
         lines,
         jnp.asarray(spanwise_table(span)),
@@ -174,21 +202,11 @@
     )
     span_first = spectral[:, :span].reshape(velocity.shape)
     span_second = spectral[:, span:].reshape(velocity.shape)
-    span_terms = -(velocity[2:3] * span_first) + viscosity * span_second
-    cols, span_terms, behind, ahead = lax.optimization_barrier((cols, span_terms, behind, ahead))
-
-    source_slab, source_plane = divmod(RECYCLE_PLANE, planes)
-    mix = interpolation_matrix(recycle_rows, weight_index, weight_table, rows)
-    plane = jnp.concatenate(
-        [cols[:, (c * planes + source_plane) * share : (c * planes + source_plane + 1) * share] for c in range(comps)],
-        axis=1,
-    )
-    inflow = jnp.dot(mix, plane, precision=HIGHEST, preferred_element_type=jnp.float32)
-    inflow = lax.ppermute(inflow, "gx", [(source_slab, 0)])
-
-    both = jnp.concatenate([wall_first, wall_second], 0)
+    span_terms = -(field[2:3] * span_first) + viscosity * span_second
+    inflow, wall, span_terms = lax.optimization_barrier((inflow, wall, span_terms))
+
     inlet = (lax.axis_index("gx") == 0).astype(jnp.int32).reshape(1)
-    wall = wall_block(cols, both, inflow, inlet, planes)
+    wall = add_ghost(wall, cols, inflow, inlet, planes)
     back = lax.all_to_all(wall.reshape(parts, rows_here, width), "ga", 0, 0, tiled=True)
 
     local_terms = span_terms + streamwise(velocity, behind, ahead)

time: 109 us -> 108 us (level)
  the two profiles are of different devices: /device:TPU:1 before, /device:TPU:31 now
where the time goes in v4:
time: 108 us; the launch traced here: 107 us
  waiting for transfers between devices  47.3 us (44%)
  starting transfers between devices  26.1 us (24%)
  Pallas kernels  17.2 us (16%)
  matrix products  8.41 us (8%)
  other arithmetic  5.4 us (5%)
  local copies, waits for them, and re-layouts  2.02 us (2%)
    all_to_all x1, waiting for transfers between devices, shards(): lax.all_to_all(wall.reshape(parts, rows_here, width), 'ga', 0, 0, tiled=T...  23.2 us
    ppermute x1, waiting for transfers between devices, halo_planes(): behind = lax.ppermute(field, 'gx', [(i, i + 1) for i in range(count - 1)])  16.9 us
    all_to_all x1, starting transfers between devices, shards(): cols = lax.all_to_all(send, 'ga', 0, 0, tiled=True).reshape(rows, width)  11 us
    all_to_all x1, starting transfers between devices, shards(): lax.all_to_all(wall.reshape(parts, rows_here, width), 'ga', 0, 0, tiled=T...  8.16 us
    ppermute x1, waiting for transfers between devices, halo_planes(): ahead = lax.ppermute(field, 'gx', [(i + 1, i) for i in range(count - 1)])  7.22 us
    dot_general x1, matrix products, shards(): jnp.dot(lines, jnp.asarray(spanwise_table(span)), precision=HIGHEST, pref...  6.53 us
    pallas_call x1, Pallas kernels, wall_block(): pl.pallas_call(kernel, out_shape=jax.ShapeDtypeStruct((rows, width), jnp....  6.44 us
    ppermute x1, starting transfers between devices, halo_planes(): behind = lax.ppermute(field, 'gx', [(i, i + 1) for i in range(count - 1)])  4.35 us
  transfers between devices with their start and end apart: 5, of which 3 were waited for; matrix products, arithmetic and copies ran while one was open for 11% of the time, Pallas kernels for 6%

profile of v4, /device:TPU:31, one launch (start us, length us, event | category | flops | bytes accessed | tf_op | source)
XLA Modules:
  0.0 107.3 jit_solution(3872427582114340792)
XLA Ops:
  0.7 2.9 %shard_map.95 = f32[16,24,576]{2,1,0:T(8,128)} custom-call(f32[3,4,24,768]{3,2,1,0:T(8,128)} %v_ref.3), custom_call_target="tpu_custom_call" | custom-call | tf_op jit(solution)/shard_map/pallas_call | solution.py:94
  3.6 11.0 %all-to-all-start = ((f32[16,24,576]{2,1,0:T(8,128)}), f32[16,24,576]{2,1,0:T(8,128)S(1)}, u32[]{:S(2)}, u32[]{:S(2)}) async-start(f32[16,24,576]{2,1,0:T(8,128)} %shard_map.95), calls=%async_computation | async-start | bytes 1966080 | tf_op jit(solution)/shard_map/all_to_all | solution.py:183
  14.6 4.4 %collective-permute-start = (f32[3,4,24,768]{3,2,1,0:T(8,128)S(1)}, f32[3,4,24,768]{3,2,1,0:T(8,128)S(1)}, u32[]{:S(2)}, u32[]{:S(2)}) collective-permute-start(f32[3,4,24,768]{3,2,1,0:T(8,128)S(1)} %copy-done), channel_id=1, source_target_pairs={{0,16},{16,32},{32,48},{48,64},{64,80},{80,96},{96,112},{112,128},... | collective-permute-start | bytes 2654216 | tf_op jit(solution)/shard_map/ppermute | solution.py:51
  19.0 1.9 %collective-permute-start.1 = (f32[3,4,24,768]{3,2,1,0:T(8,128)S(1)}, f32[3,4,24,768]{3,2,1,0:T(8,128)}, u32[]{:S(2)}, u32[]{:S(2)}) collective-permute-start(f32[3,4,24,768]{3,2,1,0:T(8,128)S(1)} %copy-done), channel_id=1, source_target_pairs={{16,0},{32,16},{48,32},{64,48},{80,64},{96,80},{112,96},{128,112},... | collective-permute-start | bytes 2654216 | tf_op jit(solution)/shard_map/ppermute | solution.py:52
  20.9 0.1 select_reduce_fusion
  21.1 16.9 %collective-permute-done = f32[3,4,24,768]{3,2,1,0:T(8,128)S(1)} collective-permute-done((f32[3,4,24,768]{3,2,1,0:T(8,128)S(1)}, f32[3,4,24,768]{3,2,1,0:T(8,128)S(1)}, u32[]{:S(2)}, u32[]{:S(2)}) %collective-permute-start) | collective-permute-done | bytes 884768 | tf_op jit(solution)/shard_map/ppermute | solution.py:51
  37.9 7.2 %collective-permute-done.1 = f32[3,4,24,768]{3,2,1,0:T(8,128)} collective-permute-done((f32[3,4,24,768]{3,2,1,0:T(8,128)S(1)}, f32[3,4,24,768]{3,2,1,0:T(8,128)}, u32[]{:S(2)}, u32[]{:S(2)}) %collective-permute-start.1) | collective-permute-done | bytes 884768 | tf_op jit(solution)/shard_map/ppermute | solution.py:52
  45.2 0.1 fusion.19
  45.3 1.9 %fusion.2 = f32[384,144]{1,0:T(8,128)} fusion(f32[384,48]{1,0:T(8,128)S(1)} %get-tuple-element.19, f32[384,48]{1,0:T(8,128)S(1)} %get-tuple-element.20, f32[384,48]{1,0:T(8,128)S(1)} %get-tuple-element.18, f32[384]{0:T(512)S(1)} %select_reduce_fusion, s32[384]{0:T(512)S(1)} %broadcast_add_fusion, f32[384]{0:T(512)S(1)} %broadcast_subtract_fusion, ...), kind=kOutput, calls=%fused_computation.10 | convolution fusion | flops 255651840 | bytes 448512 | tf_op jit(solution)/shard_map/dot_general | solution.py:192
  47.2 0.7 collective-permute-start.2
  47.9 6.5 %fusion.20 = f32[288,1536]{1,0:T(8,128)S(1)} fusion(f32[288,768]{1,0:T(8,128)S(1)} %bitcast.14, f32[768,1536]{1,0:T(8,128)} %constant.36.clone), kind=kOutput, calls=%fused_computation.40 | convolution fusion | flops 4076863488 | bytes 7372800 | tf_op jit(solution)/shard_map/dot_general | solution.py:197
  54.4 1.0 fusion.18
  55.5 6.4 %shard_map.96.w_ref = f32[384,576]{1,0:T(8,128)} custom-call(f32[384,576]{1,0:T(8,128)} %bitcast.16, f32[384,384]{1,0:T(8,128)} %f_ref.1, f32[384,384]{1,0:T(8,128)} %s_ref.1), custom_call_target="tpu_custom_call" | custom-call | tf_op jit(solution)/shard_map/pallas_call | solution.py:114
  61.9 1.0 negate_add_fusion
  63.0 0.8 copy-done.7
  63.7 3.9 %shard_map.97 = f32[384,576]{1,0:T(8,128)} custom-call(s32[1]{0:T(128)} %bitcast.7.inlet_ref, f32[384,576]{1,0:T(8,128)} %shard_map.96.w_ref, f32[384,576]{1,0:T(8,128)} %bitcast.17, f32[384,144]{1,0:T(8,128)} %copy-done.7), custom_call_target="tpu_custom_call", output_to_operand_aliasing={{}: (1, {})} | custom-call | tf_op jit(solution)/shard_map/pallas_call | solution.py:140
  67.6 8.2 %all-to-all-start.1 = ((f32[16,24,576]{2,1,0:T(8,128)}), f32[16,24,576]{2,1,0:T(8,128)S(1)}, u32[]{:S(2)}, u32[]{:S(2)}) async-start(f32[16,24,576]{2,1,0:T(8,128)} %bitcast.18), calls=%async_computation.1 | async-start | bytes 1966080 | tf_op jit(solution)/shard_map/all_to_all | solution.py:210
  75.9 0.1 constant_dynamic-update-slice_fusion.1
  75.9 1.4 %broadcast_select_fusion = (f32[3,4,24,768]{3,2,1,0:T(8,128)S(1)}, f32[3,8,24,768]{3,2,1,0:T(8,128)S(1)}) fusion(f32[3,4,24,768]{3,2,1,0:T(8,128)} %collective-permute-done.1, f32[3,24,768]{2,1,0:T(8,128)S(1)} %slice_bitcast_fusion.2, pred[]{:T(512)S(6)} %eq.54, f32[3,8,24,768]{3,2,1,0:T(8,128)S(1)} %constant_dynamic-update-slice_fusion.1, ...), kind=kLoop, calls=%fused_computation.16 | loop fusion | flops 221184 | bytes 3760129 | tf_op jit(solution)/shard_map/jit(_where)/select_n | solution.py:60
  77.3 0.0 copy-done.6
  77.4 1.9 %add_add_fusion.t_ref = f32[3,4,24,768]{3,2,1,0:T(8,128)} fusion(f32[3,4,24,768]{3,2,1,0:T(8,128)S(1)} %copy-done.6, f32[3,4,24,768]{3,2,1,0:T(8,128)S(1)} %get-tuple-element.21, f32[3,4,24,768]{3,2,1,0:T(8,128)S(1)} %copy-done.5, f32[3,4,24,768]{3,2,1,0:T(8,128)S(1)} %copy-done, f32[3,8,24,768]{3,2,1,0:T(8,128)S(1)} %get-tuple-element.22, ...), kind=kLoop, calls=%fused_computation.8 | loop fusion | flops 7077888 | bytes 7372800 | tf_op jit(solution)/shard_map/add | solution.py:212
  79.2 23.2 %all-to-all-done.1.b_ref = f32[16,24,576]{2,1,0:T(8,128)S(1)} async-done(((f32[16,24,576]{2,1,0:T(8,128)}), f32[16,24,576]{2,1,0:T(8,128)S(1)}, u32[]{:S(2)}, u32[]{:S(2)}) %all-to-all-start.1) | async-done | bytes 884768 | tf_op jit(solution)/shard_map/all_to_all | solution.py:210
  102.4 1.0 copy-done.2
  103.4 3.9 %shard_map.98 = (f32[3,4,24,768]{3,2,1,0:T(8,128)}, f32[3,4,24,768]{3,2,1,0:T(8,128)}) custom-call(f32[3,4,24,768]{3,2,1,0:T(8,128)} %v_ref.3, f32[3,4,24,768]{3,2,1,0:T(8,128)} %a_ref.1, f32[3,4,24,768]{3,2,1,0:T(8,128)} %add_add_fusion.t_ref, f32[16,24,576]{2,1,0:T(8,128)} %copy-done.2), custom_call_target="tpu_custom_call" | custom-call | tf_op jit(solution)/shard_map/pallas_call | solution.py:169
  (26 shorter events, 0.1 us)
Async XLA Ops:
  0.6 14.0 %copy-start = (f32[3,4,24,768]{3,2,1,0:T(8,128)S(1)}, f32[3,4,24,768]{3,2,1,0:T(8,128)}, u32[]{:S(2)}) copy-start(f32[3,4,24,768]{3,2,1,0:T(8,128)} %v_ref.3) | copy-start | bytes 2654212
  0.6 20.3 %copy-start.8 = (s32[384]{0:T(512)S(1)}, s32[384]{0:T(512)}, u32[]{:S(2)}) copy-start(s32[384]{0:T(512)} %param.13) | copy-start | bytes 4612
  0.7 20.3 %copy-start.10 = (f32[64]{0:T(128)S(1)}, f32[64]{0:T(128)}, u32[]{:S(2)}) copy-start(f32[64]{0:T(128)} %param.14) | copy-start | bytes 772
  0.7 20.4 %copy-start.9 = (s32[384]{0:T(512)S(1)}, s32[384]{0:T(512)}, u32[]{:S(2)}) copy-start(s32[384]{0:T(512)} %param.12) | copy-start | bytes 4612
  3.6 41.6 %all-to-all-start = ((f32[16,24,576]{2,1,0:T(8,128)}), f32[16,24,576]{2,1,0:T(8,128)S(1)}, u32[]{:S(2)}, u32[]{:S(2)}) async-start(f32[16,24,576]{2,1,0:T(8,128)} %shard_map.95), calls=%async_computation | async-start | bytes 1966080 | tf_op jit(solution)/shard_map/all_to_all | solution.py:183
  14.6 23.3 %collective-permute-start = (f32[3,4,24,768]{3,2,1,0:T(8,128)S(1)}, f32[3,4,24,768]{3,2,1,0:T(8,128)S(1)}, u32[]{:S(2)}, u32[]{:S(2)}) collective-permute-start(f32[3,4,24,768]{3,2,1,0:T(8,128)S(1)} %copy-done), channel_id=1, source_target_pairs={{0,16},{16,32},{32,48},{48,64},{64,80},{80,96},{96,112},{112,128},... | collective-permute-start | bytes 2654216 | tf_op jit(solution)/shard_map/ppermute | solution.py:51
  19.0 26.2 %collective-permute-start.1 = (f32[3,4,24,768]{3,2,1,0:T(8,128)S(1)}, f32[3,4,24,768]{3,2,1,0:T(8,128)}, u32[]{:S(2)}, u32[]{:S(2)}) collective-permute-start(f32[3,4,24,768]{3,2,1,0:T(8,128)S(1)} %copy-done), channel_id=1, source_target_pairs={{16,0},{32,16},{48,32},{64,48},{80,64},{96,80},{112,96},{128,112},... | collective-permute-start | bytes 2654216 | tf_op jit(solution)/shard_map/ppermute | solution.py:52
  37.9 9.9 %copy-start.4 = (f32[3,4,24,768]{3,2,1,0:T(8,128)}, f32[3,4,24,768]{3,2,1,0:T(8,128)S(1)}, u32[]{:S(2)}) copy-start(f32[3,4,24,768]{3,2,1,0:T(8,128)S(1)} %collective-permute-done) | copy-start | bytes 2654212
  45.2 9.3 %copy-start.1 = (f32[16,24,576]{2,1,0:T(8,128)}, f32[16,24,576]{2,1,0:T(8,128)S(1)}, u32[]{:S(2)}) copy-start(f32[16,24,576]{2,1,0:T(8,128)S(1)} %all-to-all-done) | copy-start | bytes 2654212
  47.2 15.8 %collective-permute-start.2 = (f32[384,144]{1,0:T(8,128)}, f32[384,144]{1,0:T(8,128)S(1)}, u32[]{:S(2)}, u32[]{:S(2)}) collective-permute-start(f32[384,144]{1,0:T(8,128)} %fusion.2), channel_id=1, source_target_pairs={{496,0},{497,1},{498,2},{499,3},{500,4},{501,5},{502,6},{503,7},{5... | collective-permute-start | bytes 663560 | tf_op jit(solution)/shard_map/ppermute | solution.py:193
  55.5 6.4 %copy-start.3 = (f32[288,768]{1,0:T(8,128)S(1)}, f32[288,768]{1,0:T(8,128)}, u32[]{:S(2)}) copy-start(f32[288,768]{1,0:T(8,128)} %get-tuple-element.17) | copy-start | bytes 2654212
  63.0 0.8 copy-start.7
  67.6 8.2 %copy-start.5 = (f32[3,4,24,768]{3,2,1,0:T(8,128)S(1)}, f32[3,4,24,768]{3,2,1,0:T(8,128)}, u32[]{:S(2)}) copy-start(f32[3,4,24,768]{3,2,1,0:T(8,128)} %copy-done.4) | copy-start | bytes 2654212
  67.6 34.8 %all-to-all-start.1 = ((f32[16,24,576]{2,1,0:T(8,128)}), f32[16,24,576]{2,1,0:T(8,128)S(1)}, u32[]{:S(2)}, u32[]{:S(2)}) async-start(f32[16,24,576]{2,1,0:T(8,128)} %bitcast.18), calls=%async_computation.1 | async-start | bytes 1966080 | tf_op jit(solution)/shard_map/all_to_all | solution.py:210
  75.9 1.4 %copy-start.6 = (f32[3,4,24,768]{3,2,1,0:T(8,128)S(1)}, f32[3,4,24,768]{3,2,1,0:T(8,128)}, u32[]{:S(2)}) copy-start(f32[3,4,24,768]{3,2,1,0:T(8,128)} %negate_add_fusion) | copy-start | bytes 2654212
  102.4 1.0 copy-start.2

commit v5 on v4

--- a/solution.py
+++ b/solution.py
@@ -181,7 +181,17 @@
     behind, ahead = halo_planes(velocity)
     send = pack_columns(velocity, parts)
     cols = lax.all_to_all(send, "ga", 0, 0, tiled=True).reshape(rows, width)
-    cols, behind, ahead, field = lax.optimization_barrier((cols, behind, ahead, velocity))
+    lines = velocity.reshape(-1, span)
+    spectral = jnp.dot(
+        lines,
+        jnp.asarray(spanwise_table(span)),
+        precision=HIGHEST,
+        preferred_element_type=jnp.float32,
+    )
+    span_first = spectral[:, :span].reshape(velocity.shape)
+    span_second = spectral[:, span:].reshape(velocity.shape)
+    span_terms = -(velocity[2:3] * span_first) + viscosity * span_second
+    cols, behind, ahead, span_terms = lax.optimization_barrier((cols, behind, ahead, span_terms))
 
     source_slab, source_plane = divmod(RECYCLE_PLANE, planes)
     mix = interpolation_matrix(recycle_rows, weight_index, weight_table, rows)
@@ -193,17 +203,7 @@
     inflow = lax.ppermute(inflow, "gx", [(source_slab, 0)])
 
     wall = wall_block(cols, wall_first, wall_second, planes)
-    lines = field.reshape(-1, span)
-    spectral = jnp.dot(
-        lines,
-        jnp.asarray(spanwise_table(span)),
-        precision=HIGHEST,
-        preferred_element_type=jnp.float32,
-    )
-    span_first = spectral[:, :span].reshape(velocity.shape)
-    span_second = spectral[:, span:].reshape(velocity.shape)
-    span_terms = -(field[2:3] * span_first) + viscosity * span_second
-    inflow, wall, span_terms = lax.optimization_barrier((inflow, wall, span_terms))
+    inflow, wall = lax.optimization_barrier((inflow, wall))
 
     inlet = (lax.axis_index("gx") == 0).astype(jnp.int32).reshape(1)
     wall = add_ghost(wall, cols, inflow, inlet, planes)

time: 108 us -> 108 us (level)
  the two profiles are of different devices: /device:TPU:31 before, /device:TPU:1 now
where the time goes in v5:
time: 108 us; the launch traced here: 107 us
  waiting for transfers between devices  49.1 us (45%)
  starting transfers between devices  24.6 us (23%)
  Pallas kernels  17.1 us (16%)
  matrix products  8.54 us (8%)
  other arithmetic  4.92 us (5%)
  local copies, waits for them, and re-layouts  1.96 us (2%)
    all_to_all x1, waiting for transfers between devices, shards(): lax.all_to_all(wall.reshape(parts, rows_here, width), 'ga', 0, 0, tiled=T...  21.9 us
    all_to_all x1, waiting for transfers between devices, shards(): cols = lax.all_to_all(send, 'ga', 0, 0, tiled=True).reshape(rows, width)  19.5 us
    all_to_all x1, starting transfers between devices, shards(): cols = lax.all_to_all(send, 'ga', 0, 0, tiled=True).reshape(rows, width)  11.8 us
    ppermute x1, waiting for transfers between devices, shards(): inflow = lax.ppermute(inflow, 'gx', [(source_slab, 0)])  7.7 us
    dot_general x1, matrix products, shards(): jnp.dot(lines, jnp.asarray(spanwise_table(span)), precision=HIGHEST, pref...  6.66 us
    pallas_call x1, Pallas kernels, wall_block(): pl.pallas_call(kernel, out_shape=jax.ShapeDtypeStruct((rows, width), jnp....  6.39 us
    ppermute x1, starting transfers between devices, halo_planes(): behind = lax.ppermute(field, 'gx', [(i, i + 1) for i in range(count - 1)])  5.51 us
    all_to_all x1, starting transfers between devices, shards(): lax.all_to_all(wall.reshape(parts, rows_here, width), 'ga', 0, 0, tiled=T...  4.59 us
  transfers between devices with their start and end apart: 5, of which 3 were waited for; matrix products, arithmetic and copies ran while one was open for 11% of the time, Pallas kernels for 9%

profile of v5, /device:TPU:1, one launch (start us, length us, event | category | flops | bytes accessed | tf_op | source)
XLA Modules:
  0.0 107.0 jit_solution(4974866741962727841)
XLA Ops:
  0.6 0.0 copy-start
  0.7 1.4 %collective-permute-start.1 = (f32[3,4,24,768]{3,2,1,0:T(8,128)}, f32[3,4,24,768]{3,2,1,0:T(8,128)}, u32[]{:S(2)}, u32[]{:S(2)}) collective-permute-start(f32[3,4,24,768]{3,2,1,0:T(8,128)} %v_ref.3), channel_id=1, source_target_pairs={{16,0},{32,16},{48,32},{64,48},{80,64},{96,80},{112,96},{128,112},... | collective-permute-start | bytes 2654216 | tf_op jit(solution)/shard_map/ppermute | solution.py:52
  2.1 5.5 %collective-permute-start = (f32[3,4,24,768]{3,2,1,0:T(8,128)}, f32[3,4,24,768]{3,2,1,0:T(8,128)}, u32[]{:S(2)}, u32[]{:S(2)}) collective-permute-start(f32[3,4,24,768]{3,2,1,0:T(8,128)} %v_ref.3), channel_id=1, source_target_pairs={{0,16},{16,32},{32,48},{48,64},{64,80},{80,96},{96,112},{112,128},... | collective-permute-start | bytes 2654216 | tf_op jit(solution)/shard_map/ppermute | solution.py:51
  7.6 2.8 %shard_map.95 = f32[16,24,576]{2,1,0:T(8,128)} custom-call(f32[3,4,24,768]{3,2,1,0:T(8,128)} %v_ref.3), custom_call_target="tpu_custom_call" | custom-call | tf_op jit(solution)/shard_map/pallas_call | solution.py:94
  10.4 11.8 %all-to-all-start = ((f32[16,24,576]{2,1,0:T(8,128)}), f32[16,24,576]{2,1,0:T(8,128)S(1)}, u32[]{:S(2)}, u32[]{:S(2)}) async-start(f32[16,24,576]{2,1,0:T(8,128)} %shard_map.95), calls=%async_computation | async-start | bytes 1966080 | tf_op jit(solution)/shard_map/all_to_all | solution.py:183
  22.3 0.1 select_reduce_fusion
  22.4 6.7 %convolution_bitcast_fusion = f32[288,1536]{1,0:T(8,128)S(1)} fusion(f32[768,1536]{1,0:T(8,128)} %constant.36.clone, f32[288,768]{1,0:T(8,128)S(1)} %bitcast.16), kind=kOutput, calls=%fused_computation | convolution fusion | flops 4076863488 | bytes 7372800 | tf_op jit(solution)/shard_map/dot_general | solution.py:185
  29.1 0.1 fusion.18
  29.3 0.1 negate_add_fusion
  29.4 19.5 %all-to-all-done = f32[16,24,576]{2,1,0:T(8,128)S(1)} async-done(((f32[16,24,576]{2,1,0:T(8,128)}), f32[16,24,576]{2,1,0:T(8,128)S(1)}, u32[]{:S(2)}, u32[]{:S(2)}) %all-to-all-start) | async-done | bytes 884768 | tf_op jit(solution)/shard_map/all_to_all | solution.py:183
  48.9 0.1 fusion.19
  49.0 1.9 %fusion.2 = f32[384,144]{1,0:T(8,128)} fusion(f32[384,48]{1,0:T(8,128)S(1)} %get-tuple-element.17, f32[384,48]{1,0:T(8,128)S(1)} %get-tuple-element.18, f32[384,48]{1,0:T(8,128)S(1)} %get-tuple-element.16, f32[384]{0:T(512)S(1)} %select_reduce_fusion, s32[384]{0:T(512)S(1)} %broadcast_add_fusion, f32[384]{0:T(512)S(1)} %broadcast_subtract_fusion, ...), kind=kOutput, calls=%fused_computation.11 | convolution fusion | flops 255651840 | bytes 448512 | tf_op jit(solution)/shard_map/dot_general | solution.py:202
  50.9 1.3 %collective-permute-start.2 = (f32[384,144]{1,0:T(8,128)}, f32[384,144]{1,0:T(8,128)S(1)}, u32[]{:S(2)}, u32[]{:S(2)}) collective-permute-start(f32[384,144]{1,0:T(8,128)} %fusion.2), channel_id=1, source_target_pairs={{496,0},{497,1},{498,2},{499,3},{500,4},{501,5},{502,6},{503,7},{5... | collective-permute-start | bytes 663560 | tf_op jit(solution)/shard_map/ppermute | solution.py:203
  52.2 6.4 %shard_map.96.w_ref = f32[384,576]{1,0:T(8,128)} custom-call(f32[384,576]{1,0:T(8,128)} %bitcast.18, f32[384,384]{1,0:T(8,128)} %f_ref.1, f32[384,384]{1,0:T(8,128)} %s_ref.1), custom_call_target="tpu_custom_call" | custom-call | tf_op jit(solution)/shard_map/pallas_call | solution.py:114
  58.6 7.7 %collective-permute-done.2.f_ref = f32[384,144]{1,0:T(8,128)S(1)} collective-permute-done((f32[384,144]{1,0:T(8,128)}, f32[384,144]{1,0:T(8,128)S(1)}, u32[]{:S(2)}, u32[]{:S(2)}) %collective-permute-start.2) | collective-permute-done | bytes 221216 | tf_op jit(solution)/shard_map/ppermute | solution.py:203
  66.3 0.7 copy-done.3
  67.0 3.9 %shard_map.97 = f32[384,576]{1,0:T(8,128)} custom-call(s32[1]{0:T(128)} %bitcast.8.inlet_ref, f32[384,576]{1,0:T(8,128)} %shard_map.96.w_ref, f32[384,576]{1,0:T(8,128)} %bitcast.19, f32[384,144]{1,0:T(8,128)} %copy-done.3), custom_call_target="tpu_custom_call", output_to_operand_aliasing={{}: (1, {})} | custom-call | tf_op jit(solution)/shard_map/pallas_call | solution.py:140
  70.9 4.6 %all-to-all-start.1 = ((f32[16,24,576]{2,1,0:T(8,128)}), f32[16,24,576]{2,1,0:T(8,128)S(1)}, u32[]{:S(2)}, u32[]{:S(2)}) async-start(f32[16,24,576]{2,1,0:T(8,128)} %bitcast.20), calls=%async_computation.1 | async-start | bytes 1966080 | tf_op jit(solution)/shard_map/all_to_all | solution.py:210
  75.5 1.6 %broadcast_select_fusion = (f32[3,4,24,768]{3,2,1,0:T(8,128)S(1)}, f32[3,8,24,768]{3,2,1,0:T(8,128)S(1)}) fusion(f32[3,4,24,768]{3,2,1,0:T(8,128)} %collective-permute-done.1, f32[3,24,768]{2,1,0:T(8,128)S(1)} %slice_bitcast_fusion.2, pred[]{:T(512)S(6)} %eq.22, f32[3,4,24,768]{3,2,1,0:T(8,128)} %collective-permute-done), kind=kLoop, calls=%fused_computation.17 | loop fusion | flops 221183 | bytes 3760129 | tf_op jit(solution)/shard_map/jit(_where)/select_n | solution.py:60
  77.1 0.1 constant_dynamic-update-slice_fusion
  77.2 3.0 %add_add_fusion.t_ref = f32[3,4,24,768]{3,2,1,0:T(8,128)} fusion(f32[3,4,24,768]{3,2,1,0:T(8,128)S(1)} %negate_add_fusion, f32[3,4,24,768]{3,2,1,0:T(8,128)S(1)} %get-tuple-element.21, f32[3,4,24,768]{3,2,1,0:T(8,128)} %collective-permute-done, f32[3,4,24,768]{3,2,1,0:T(8,128)S(1)} %copy-done, f32[3,8,24,768]{3,2,1,0:T(8,128)S(1)} %constant_dynamic-update-slice_fusion, ...), kind=kLoop, calls=%fused_computation.9 | loop fusion | flops 7077888 | bytes 7372800 | tf_op jit(solution)/shard_map/add | solution.py:212
  80.2 21.9 %all-to-all-done.1.b_ref = f32[16,24,576]{2,1,0:T(8,128)S(1)} async-done(((f32[16,24,576]{2,1,0:T(8,128)}), f32[16,24,576]{2,1,0:T(8,128)S(1)}, u32[]{:S(2)}, u32[]{:S(2)}) %all-to-all-start.1) | async-done | bytes 884768 | tf_op jit(solution)/shard_map/all_to_all | solution.py:210
  102.1 0.9 copy-done.2
  103.1 3.9 %shard_map.98 = (f32[3,4,24,768]{3,2,1,0:T(8,128)}, f32[3,4,24,768]{3,2,1,0:T(8,128)}) custom-call(f32[3,4,24,768]{3,2,1,0:T(8,128)} %v_ref.3, f32[3,4,24,768]{3,2,1,0:T(8,128)} %a_ref.1, f32[3,4,24,768]{3,2,1,0:T(8,128)} %add_add_fusion.t_ref, f32[16,24,576]{2,1,0:T(8,128)} %copy-done.2), custom_call_target="tpu_custom_call" | custom-call | tf_op jit(solution)/shard_map/pallas_call | solution.py:169
  (17 shorter events, 0.1 us)
Async XLA Ops:
  0.6 21.7 %copy-start = (f32[3,4,24,768]{3,2,1,0:T(8,128)S(1)}, f32[3,4,24,768]{3,2,1,0:T(8,128)}, u32[]{:S(2)}) copy-start(f32[3,4,24,768]{3,2,1,0:T(8,128)} %v_ref.3) | copy-start | bytes 2654212
  0.6 21.6 %copy-start.6 = (f32[64]{0:T(128)S(1)}, f32[64]{0:T(128)}, u32[]{:S(2)}) copy-start(f32[64]{0:T(128)} %param.14) | copy-start | bytes 772
  0.7 21.6 %copy-start.4 = (s32[384]{0:T(512)S(1)}, s32[384]{0:T(512)}, u32[]{:S(2)}) copy-start(s32[384]{0:T(512)} %param.13) | copy-start | bytes 4612
  0.7 28.7 %collective-permute-start.1 = (f32[3,4,24,768]{3,2,1,0:T(8,128)}, f32[3,4,24,768]{3,2,1,0:T(8,128)}, u32[]{:S(2)}, u32[]{:S(2)}) collective-permute-start(f32[3,4,24,768]{3,2,1,0:T(8,128)} %v_ref.3), channel_id=1, source_target_pairs={{16,0},{32,16},{48,32},{64,48},{80,64},{96,80},{112,96},{128,112},... | collective-permute-start | bytes 2654216 | tf_op jit(solution)/shard_map/ppermute | solution.py:52
  2.1 27.3 %collective-permute-start = (f32[3,4,24,768]{3,2,1,0:T(8,128)}, f32[3,4,24,768]{3,2,1,0:T(8,128)}, u32[]{:S(2)}, u32[]{:S(2)}) collective-permute-start(f32[3,4,24,768]{3,2,1,0:T(8,128)} %v_ref.3), channel_id=1, source_target_pairs={{0,16},{16,32},{32,48},{48,64},{64,80},{80,96},{96,112},{112,128},... | collective-permute-start | bytes 2654216 | tf_op jit(solution)/shard_map/ppermute | solution.py:51
  10.4 38.4 %all-to-all-start = ((f32[16,24,576]{2,1,0:T(8,128)}), f32[16,24,576]{2,1,0:T(8,128)S(1)}, u32[]{:S(2)}, u32[]{:S(2)}) async-start(f32[16,24,576]{2,1,0:T(8,128)} %shard_map.95), calls=%async_computation | async-start | bytes 1966080 | tf_op jit(solution)/shard_map/all_to_all | solution.py:183
  22.4 6.7 %copy-start.5 = (s32[384]{0:T(512)S(1)}, s32[384]{0:T(512)}, u32[]{:S(2)}) copy-start(s32[384]{0:T(512)} %param.12) | copy-start | bytes 4612
  48.9 3.3 %copy-start.1 = (f32[16,24,576]{2,1,0:T(8,128)}, f32[16,24,576]{2,1,0:T(8,128)S(1)}, u32[]{:S(2)}) copy-start(f32[16,24,576]{2,1,0:T(8,128)S(1)} %all-to-all-done) | copy-start | bytes 2654212
  50.9 15.4 %collective-permute-start.2 = (f32[384,144]{1,0:T(8,128)}, f32[384,144]{1,0:T(8,128)S(1)}, u32[]{:S(2)}, u32[]{:S(2)}) collective-permute-start(f32[384,144]{1,0:T(8,128)} %fusion.2), channel_id=1, source_target_pairs={{496,0},{497,1},{498,2},{499,3},{500,4},{501,5},{502,6},{503,7},{5... | collective-permute-start | bytes 663560 | tf_op jit(solution)/shard_map/ppermute | solution.py:203
  66.2 0.7 copy-start.3
  70.9 31.2 %all-to-all-start.1 = ((f32[16,24,576]{2,1,0:T(8,128)}), f32[16,24,576]{2,1,0:T(8,128)S(1)}, u32[]{:S(2)}, u32[]{:S(2)}) async-start(f32[16,24,576]{2,1,0:T(8,128)} %bitcast.20), calls=%async_computation.1 | async-start | bytes 1966080 | tf_op jit(solution)/shard_map/all_to_all | solution.py:210
  102.1 0.9 copy-start.2

commit v6 on v5

--- a/solution.py
+++ b/solution.py
@@ -116,57 +116,34 @@
     )
 
 
-def add_ghost(wall, cols, inflow, inlet, planes):
-    rows, width = cols.shape
-    comps = 3
-    share = width // (comps * planes)
-    block = planes * share
-    lower, upper = ghost_weights(planes)
-
-    def kernel(inlet_ref, w_ref, c_ref, f_ref, o_ref):
-        at_inlet = inlet_ref[0] > 0
-        for c in range(comps):
-            flow = f_ref[:, c * share : (c + 1) * share]
-            ghost = jnp.concatenate(
-                [
-                    flow * (c_ref[:, x * share : (x + 1) * share] * lower[x] + viscosity * upper[x])
-                    for x in range(planes)
-                ],
-                axis=1,
-            )
-            part = slice(c * block, (c + 1) * block)
-            o_ref[:, part] = w_ref[:, part] + jnp.where(at_inlet, ghost, 0.0)
-
-    return pl.pallas_call(
-        kernel,
-        out_shape=jax.ShapeDtypeStruct((rows, width), jnp.float32),
-        in_specs=[
-            pl.BlockSpec(memory_space=pltpu.SMEM),
-            pl.BlockSpec(memory_space=pltpu.VMEM),
-            pl.BlockSpec(memory_space=pltpu.VMEM),
-            pl.BlockSpec(memory_space=pltpu.VMEM),
-        ],
-        input_output_aliases={1: 0},
-    )(inlet, wall, cols, inflow)
-
-
-def combine(velocity, accumulated, local_terms, back):
+def combine(velocity, accumulated, local_terms, back, inflow, inlet):
     comps, planes, rows_here, span = velocity.shape
     parts = back.shape[0]
     share = span // parts
+    lower, upper = ghost_weights(planes)
 
-    def kernel(v_ref, a_ref, t_ref, b_ref, nv_ref, na_ref):
+    def kernel(inlet_ref, v_ref, a_ref, t_ref, b_ref, f_ref, nv_ref, na_ref):
+        at_inlet = inlet_ref[0] > 0
         for c in range(comps):
+            flow = jnp.concatenate(
+                [f_ref[d, :, c * share : (c + 1) * share] for d in range(parts)], axis=1
+            )
             for x in range(planes):
                 k = (c * planes + x) * share
                 wall = jnp.concatenate([b_ref[d, :, k : k + share] for d in range(parts)], axis=1)
-                tendency = t_ref[c, x] + wall
+                ghost = flow * (v_ref[0, x] * lower[x] + viscosity * upper[x])
+                tendency = t_ref[c, x] + wall + jnp.where(at_inlet, ghost, 0.0)
                 acc = keep_rate * a_ref[c, x] + step_size * tendency
                 na_ref[c, x] = acc
                 nv_ref[c, x] = v_ref[c, x] + update_rate * acc
 
     shape = jax.ShapeDtypeStruct(velocity.shape, jnp.float32)
-    return pl.pallas_call(kernel, out_shape=(shape, shape))(velocity, accumulated, local_terms, back)
+    vmem = pl.BlockSpec(memory_space=pltpu.VMEM)
+    return pl.pallas_call(
+        kernel,
+        out_shape=(shape, shape),
+        in_specs=[pl.BlockSpec(memory_space=pltpu.SMEM)] + [vmem] * 5,
+    )(inlet, velocity, accumulated, local_terms, back, inflow)
 
 
 def shards(
@@ -203,14 +180,13 @@
     inflow = lax.ppermute(inflow, "gx", [(source_slab, 0)])
 
     wall = wall_block(cols, wall_first, wall_second, planes)
-    inflow, wall = lax.optimization_barrier((inflow, wall))
+    back = lax.all_to_all(wall.reshape(parts, rows_here, width), "ga", 0, 0, tiled=True)
+    local_terms = span_terms + streamwise(velocity, behind, ahead)
+    inflow, back, local_terms = lax.optimization_barrier((inflow, back, local_terms))
+    inflow = lax.all_to_all(inflow.reshape(parts, rows_here, comps * share), "ga", 0, 0, tiled=True)
 
     inlet = (lax.axis_index("gx") == 0).astype(jnp.int32).reshape(1)
-    wall = add_ghost(wall, cols, inflow, inlet, planes)
-    back = lax.all_to_all(wall.reshape(parts, rows_here, width), "ga", 0, 0, tiled=True)
-
-    local_terms = span_terms + streamwise(velocity, behind, ahead)
-    return combine(velocity, accumulated, local_terms, back)
+    return combine(velocity, accumulated, local_terms, back, inflow, inlet)
 
 
 def solution(mesh):

time: 108 us -> 112 us (1.037)
  the two profiles are of different devices: /device:TPU:1 before, /device:TPU:31 now
where the time goes in v6:
time: 112 us; the launch traced here: 111 us
  waiting for transfers between devices  50.9 us (45%)
  starting transfers between devices  29.6 us (26%)
  Pallas kernels  13.5 us (12%)
  matrix products  7.99 us (7%)
  other arithmetic  4.53 us (4%)
  local copies, waits for them, and re-layouts  3.96 us (4%)
    all_to_all x1, waiting for transfers between devices, shards(): lax.all_to_all(wall.reshape(parts, rows_here, width), 'ga', 0, 0, tiled=T...  21 us
    all_to_all x1, waiting for transfers between devices, shards(): lax.all_to_all(inflow.reshape(parts, rows_here, comps * share), 'ga', 0,...  14.5 us
    all_to_all x1, starting transfers between devices, shards(): cols = lax.all_to_all(send, 'ga', 0, 0, tiled=True).reshape(rows, width)  11 us
    ppermute x1, waiting for transfers between devices, halo_planes(): behind = lax.ppermute(field, 'gx', [(i, i + 1) for i in range(count - 1)])  9.03 us
    all_to_all x1, starting transfers between devices, shards(): lax.all_to_all(wall.reshape(parts, rows_here, width), 'ga', 0, 0, tiled=T...  8.16 us
    dot_general x1, matrix products, shards(): jnp.dot(lines, jnp.asarray(spanwise_table(span)), precision=HIGHEST, pref...  6.66 us
    pallas_call x1, Pallas kernels, wall_block(): pl.pallas_call(kernel, out_shape=jax.ShapeDtypeStruct((rows, width), jnp....  6.35 us
    ppermute x1, waiting for transfers between devices, halo_planes(): ahead = lax.ppermute(field, 'gx', [(i + 1, i) for i in range(count - 1)])  6.31 us
  transfers between devices with their start and end apart: 6, of which 4 were waited for; matrix products, arithmetic and copies ran while one was open for 11% of the time, Pallas kernels for 0%

profile of v6, /device:TPU:31, one launch (start us, length us, event | category | flops | bytes accessed | tf_op | source)
XLA Modules:
  0.0 111.3 jit_solution(17627363130551415030)
XLA Ops:
  0.7 2.9 %shard_map.95 = f32[16,24,576]{2,1,0:T(8,128)} custom-call(f32[3,4,24,768]{3,2,1,0:T(8,128)} %v_ref.3), custom_call_target="tpu_custom_call" | custom-call | tf_op jit(solution)/shard_map/pallas_call | solution.py:94
  3.6 11.0 %all-to-all-start = ((f32[16,24,576]{2,1,0:T(8,128)}), f32[16,24,576]{2,1,0:T(8,128)S(1)}, u32[]{:S(2)}, u32[]{:S(2)}) async-start(f32[16,24,576]{2,1,0:T(8,128)} %shard_map.95), calls=%async_computation | async-start | bytes 1966080 | tf_op jit(solution)/shard_map/all_to_all | solution.py:160
  14.6 4.4 %collective-permute-start = (f32[3,4,24,768]{3,2,1,0:T(8,128)S(1)}, f32[3,4,24,768]{3,2,1,0:T(8,128)S(1)}, u32[]{:S(2)}, u32[]{:S(2)}) collective-permute-start(f32[3,4,24,768]{3,2,1,0:T(8,128)S(1)} %copy-done), channel_id=1, source_target_pairs={{0,16},{16,32},{32,48},{48,64},{64,80},{80,96},{96,112},{112,128},... | collective-permute-start | bytes 2654216 | tf_op jit(solution)/shard_map/ppermute | solution.py:51
  19.0 1.9 %collective-permute-start.1 = (f32[3,4,24,768]{3,2,1,0:T(8,128)S(1)}, f32[3,4,24,768]{3,2,1,0:T(8,128)}, u32[]{:S(2)}, u32[]{:S(2)}) collective-permute-start(f32[3,4,24,768]{3,2,1,0:T(8,128)S(1)} %copy-done), channel_id=1, source_target_pairs={{16,0},{32,16},{48,32},{64,48},{80,64},{96,80},{112,96},{128,112},... | collective-permute-start | bytes 2654216 | tf_op jit(solution)/shard_map/ppermute | solution.py:52
  21.0 6.7 %convolution_bitcast_fusion = f32[288,1536]{1,0:T(8,128)S(1)} fusion(f32[768,1536]{1,0:T(8,128)} %constant.36.clone, f32[288,768]{1,0:T(8,128)S(1)} %bitcast.17), kind=kOutput, calls=%fused_computation | convolution fusion | flops 4076863488 | bytes 7372800 | tf_op jit(solution)/shard_map/dot_general | solution.py:162
  27.7 0.1 fusion.18
  27.9 1.0 negate_add_fusion
  28.9 9.0 %collective-permute-done = f32[3,4,24,768]{3,2,1,0:T(8,128)S(1)} collective-permute-done((f32[3,4,24,768]{3,2,1,0:T(8,128)S(1)}, f32[3,4,24,768]{3,2,1,0:T(8,128)S(1)}, u32[]{:S(2)}, u32[]{:S(2)}) %collective-permute-start) | collective-permute-done | bytes 884768 | tf_op jit(solution)/shard_map/ppermute | solution.py:51
  37.9 0.9 copy-done.4
  38.9 6.3 %collective-permute-done.1 = f32[3,4,24,768]{3,2,1,0:T(8,128)} collective-permute-done((f32[3,4,24,768]{3,2,1,0:T(8,128)S(1)}, f32[3,4,24,768]{3,2,1,0:T(8,128)}, u32[]{:S(2)}, u32[]{:S(2)}) %collective-permute-start.1) | collective-permute-done | bytes 884768 | tf_op jit(solution)/shard_map/ppermute | solution.py:52
  45.2 1.0 copy-done.1
  46.1 6.4 %shard_map.96 = f32[384,576]{1,0:T(8,128)} custom-call(f32[384,576]{1,0:T(8,128)} %bitcast.18, f32[384,384]{1,0:T(8,128)} %f_ref.1, f32[384,384]{1,0:T(8,128)} %s_ref.1), custom_call_target="tpu_custom_call" | custom-call | tf_op jit(solution)/shard_map/pallas_call | solution.py:114
  52.5 8.2 %all-to-all-start.1 = ((f32[16,24,576]{2,1,0:T(8,128)}), f32[16,24,576]{2,1,0:T(8,128)S(1)}, u32[]{:S(2)}, u32[]{:S(2)}) async-start(f32[16,24,576]{2,1,0:T(8,128)} %bitcast.20), calls=%async_computation.1 | async-start | bytes 1966080 | tf_op jit(solution)/shard_map/all_to_all | solution.py:183
  60.7 0.1 fusion.19
  60.8 1.3 %fusion.2 = f32[384,144]{0,1:T(8,128)S(1)} fusion(f32[384,48]{1,0:T(8,128)S(1)} %get-tuple-element.19, f32[384,48]{1,0:T(8,128)S(1)} %get-tuple-element.20, f32[384,48]{1,0:T(8,128)S(1)} %get-tuple-element.18, f32[384]{0:T(512)S(1)} %select_reduce_fusion, s32[384]{0:T(512)S(1)} %broadcast_add_fusion, f32[384]{0:T(512)S(1)} %broadcast_subtract_fusion, ...), kind=kOutput, calls=%fused_computation.11 | convolution fusion | flops 255651840 | bytes 448512 | tf_op jit(solution)/shard_map/dot_general | solution.py:179
  62.2 0.7 collective-permute-start.2
  63.0 1.4 %broadcast_select_fusion = (f32[3,4,24,768]{3,2,1,0:T(8,128)S(1)}, f32[3,8,24,768]{3,2,1,0:T(8,128)S(1)}) fusion(f32[3,4,24,768]{3,2,1,0:T(8,128)} %collective-permute-done.1, f32[3,24,768]{2,1,0:T(8,128)S(1)} %slice_bitcast_fusion.2, pred[]{:T(512)S(6)} %eq.55, f32[3,8,24,768]{3,2,1,0:T(8,128)S(1)} %constant_dynamic-update-slice_fusion.1, ...), kind=kLoop, calls=%fused_computation.17 | loop fusion | flops 221184 | bytes 3760129 | tf_op jit(solution)/shard_map/jit(_where)/select_n | solution.py:60
  64.4 1.9 %add_add_fusion.t_ref = f32[3,4,24,768]{3,2,1,0:T(8,128)} fusion(f32[3,4,24,768]{3,2,1,0:T(8,128)S(1)} %copy-done.6, f32[3,4,24,768]{3,2,1,0:T(8,128)S(1)} %get-tuple-element.23, f32[3,4,24,768]{3,2,1,0:T(8,128)S(1)} %copy-done.5, f32[3,4,24,768]{3,2,1,0:T(8,128)S(1)} %copy-done, f32[3,8,24,768]{3,2,1,0:T(8,128)S(1)} %get-tuple-element.24, ...), kind=kLoop, calls=%fused_computation.9 | loop fusion | flops 7077888 | bytes 7372800 | tf_op jit(solution)/shard_map/add | solution.py:184
  66.3 21.0 %all-to-all-done.1.b_ref = f32[16,24,576]{2,1,0:T(8,128)S(1)} async-done(((f32[16,24,576]{2,1,0:T(8,128)}), f32[16,24,576]{2,1,0:T(8,128)S(1)}, u32[]{:S(2)}, u32[]{:S(2)}) %all-to-all-start.1) | async-done | bytes 884768 | tf_op jit(solution)/shard_map/all_to_all | solution.py:183
  87.3 1.1 copy.11
  88.3 3.5 %all-to-all-start.2 = ((f32[16,24,144]{2,1,0:T(8,128)}), f32[16,24,144]{2,1,0:T(8,128)S(1)}, u32[]{:S(2)}, u32[]{:S(2)}) async-start(f32[16,24,144]{2,1,0:T(8,128)} %bitcast.10), calls=%async_computation.2 | async-start | bytes 786432 | tf_op jit(solution)/shard_map/all_to_all | solution.py:186
  91.8 14.5 %all-to-all-done.2.f_ref = f32[16,24,144]{2,1,0:T(8,128)S(1)} async-done(((f32[16,24,144]{2,1,0:T(8,128)}), f32[16,24,144]{2,1,0:T(8,128)S(1)}, u32[]{:S(2)}, u32[]{:S(2)}) %all-to-all-start.2) | async-done | bytes 221216 | tf_op jit(solution)/shard_map/all_to_all | solution.py:186
  106.3 0.7 copy-done.7
  107.1 4.2 %shard_map.97 = (f32[3,4,24,768]{3,2,1,0:T(8,128)}, f32[3,4,24,768]{3,2,1,0:T(8,128)}) custom-call(s32[1]{0:T(128)} %bitcast.inlet_ref, f32[3,4,24,768]{3,2,1,0:T(8,128)} %v_ref.3, f32[3,4,24,768]{3,2,1,0:T(8,128)} %a_ref.1, f32[3,4,24,768]{3,2,1,0:T(8,128)} %add_add_fusion.t_ref, f32[16,24,576]{2,1,0:T(8,128)} %copy-done.3, f32[16,24,144]{2,1,0:T(8,128)} %copy-done.7), custom_call_target="tpu_custom_call" | custom-call | tf_op jit(solution)/shard_map/pallas_call | solution.py:142
  (27 shorter events, 0.3 us)
Async XLA Ops:
  0.6 14.0 %copy-start = (f32[3,4,24,768]{3,2,1,0:T(8,128)S(1)}, f32[3,4,24,768]{3,2,1,0:T(8,128)}, u32[]{:S(2)}) copy-start(f32[3,4,24,768]{3,2,1,0:T(8,128)} %v_ref.3) | copy-start | bytes 2654212
  0.6 20.3 %copy-start.8 = (s32[384]{0:T(512)S(1)}, s32[384]{0:T(512)}, u32[]{:S(2)}) copy-start(s32[384]{0:T(512)} %param.13) | copy-start | bytes 4612
  0.7 20.3 %copy-start.10 = (f32[64]{0:T(128)S(1)}, f32[64]{0:T(128)}, u32[]{:S(2)}) copy-start(f32[64]{0:T(128)} %param.14) | copy-start | bytes 772
  3.6 41.6 %all-to-all-start = ((f32[16,24,576]{2,1,0:T(8,128)}), f32[16,24,576]{2,1,0:T(8,128)S(1)}, u32[]{:S(2)}, u32[]{:S(2)}) async-start(f32[16,24,576]{2,1,0:T(8,128)} %shard_map.95), calls=%async_computation | async-start | bytes 1966080 | tf_op jit(solution)/shard_map/all_to_all | solution.py:160
  14.6 23.3 %collective-permute-start = (f32[3,4,24,768]{3,2,1,0:T(8,128)S(1)}, f32[3,4,24,768]{3,2,1,0:T(8,128)S(1)}, u32[]{:S(2)}, u32[]{:S(2)}) collective-permute-start(f32[3,4,24,768]{3,2,1,0:T(8,128)S(1)} %copy-done), channel_id=1, source_target_pairs={{0,16},{16,32},{32,48},{48,64},{64,80},{80,96},{96,112},{112,128},... | collective-permute-start | bytes 2654216 | tf_op jit(solution)/shard_map/ppermute | solution.py:51
  19.0 26.2 %collective-permute-start.1 = (f32[3,4,24,768]{3,2,1,0:T(8,128)S(1)}, f32[3,4,24,768]{3,2,1,0:T(8,128)}, u32[]{:S(2)}, u32[]{:S(2)}) collective-permute-start(f32[3,4,24,768]{3,2,1,0:T(8,128)S(1)} %copy-done), channel_id=1, source_target_pairs={{16,0},{32,16},{48,32},{64,48},{80,64},{96,80},{112,96},{128,112},... | collective-permute-start | bytes 2654216 | tf_op jit(solution)/shard_map/ppermute | solution.py:52
  37.9 0.9 copy-start.4
  45.2 1.0 copy-start.1
  52.5 8.2 %copy-start.9 = (s32[384]{0:T(512)S(1)}, s32[384]{0:T(512)}, u32[]{:S(2)}) copy-start(s32[384]{0:T(512)} %param.12) | copy-start | bytes 4612
  52.5 8.2 %copy-start.2 = (f32[16,24,576]{2,1,0:T(8,128)S(1)}, f32[16,24,576]{2,1,0:T(8,128)}, u32[]{:S(2)}) copy-start(f32[16,24,576]{2,1,0:T(8,128)} %copy-done.1) | copy-start | bytes 2654212
  52.5 34.8 %all-to-all-start.1 = ((f32[16,24,576]{2,1,0:T(8,128)}), f32[16,24,576]{2,1,0:T(8,128)S(1)}, u32[]{:S(2)}, u32[]{:S(2)}) async-start(f32[16,24,576]{2,1,0:T(8,128)} %bitcast.20), calls=%async_computation.1 | async-start | bytes 1966080 | tf_op jit(solution)/shard_map/all_to_all | solution.py:183
  60.7 2.2 %copy-start.5 = (f32[3,4,24,768]{3,2,1,0:T(8,128)S(1)}, f32[3,4,24,768]{3,2,1,0:T(8,128)}, u32[]{:S(2)}) copy-start(f32[3,4,24,768]{3,2,1,0:T(8,128)} %copy-done.4) | copy-start | bytes 2654212
  62.2 4.1 %collective-permute-start.2 = (f32[384,144]{0,1:T(8,128)S(1)}, f32[384,144]{0,1:T(8,128)S(1)}, u32[]{:S(2)}, u32[]{:S(2)}) collective-permute-start(f32[384,144]{0,1:T(8,128)S(1)} %fusion.2), channel_id=1, source_target_pairs={{496,0},{497,1},{498,2},{499,3},{500,4},{501,5},{502,6},{503,7},{5... | collective-permute-start | bytes 663560 | tf_op jit(solution)/shard_map/ppermute | solution.py:180
  62.9 1.4 %copy-start.6 = (f32[3,4,24,768]{3,2,1,0:T(8,128)S(1)}, f32[3,4,24,768]{3,2,1,0:T(8,128)}, u32[]{:S(2)}) copy-start(f32[3,4,24,768]{3,2,1,0:T(8,128)} %negate_add_fusion) | copy-start | bytes 2654212
  87.3 19.1 %copy-start.3 = (f32[16,24,576]{2,1,0:T(8,128)}, f32[16,24,576]{2,1,0:T(8,128)S(1)}, u32[]{:S(2)}) copy-start(f32[16,24,576]{2,1,0:T(8,128)S(1)} %all-to-all-done.1.b_ref) | copy-start | bytes 2654212
  88.3 18.0 %all-to-all-start.2 = ((f32[16,24,144]{2,1,0:T(8,128)}), f32[16,24,144]{2,1,0:T(8,128)S(1)}, u32[]{:S(2)}, u32[]{:S(2)}) async-start(f32[16,24,144]{2,1,0:T(8,128)} %bitcast.10), calls=%async_computation.2 | async-start | bytes 786432 | tf_op jit(solution)/shard_map/all_to_all | solution.py:186
  106.3 0.7 copy-start.7

commit v7 on v5

--- a/solution.py
+++ b/solution.py
@@ -178,7 +178,6 @@
     rows = rows_here * parts
     width = comps * planes * share
 
-    behind, ahead = halo_planes(velocity)
     send = pack_columns(velocity, parts)
     cols = lax.all_to_all(send, "ga", 0, 0, tiled=True).reshape(rows, width)
     lines = velocity.reshape(-1, span)
@@ -191,7 +190,9 @@
     span_first = spectral[:, :span].reshape(velocity.shape)
     span_second = spectral[:, span:].reshape(velocity.shape)
     span_terms = -(velocity[2:3] * span_first) + viscosity * span_second
-    cols, behind, ahead, span_terms = lax.optimization_barrier((cols, behind, ahead, span_terms))
+    span_terms, halo_source = lax.optimization_barrier((span_terms, velocity))
+    behind, ahead = halo_planes(halo_source)
+    cols, span_terms = lax.optimization_barrier((cols, span_terms))
 
     source_slab, source_plane = divmod(RECYCLE_PLANE, planes)
     mix = interpolation_matrix(recycle_rows, weight_index, weight_table, rows)

time: 108 us -> 102 us (0.944)
  waiting for transfers between devices: 49.1 us -> 43.6 us
  starting transfers between devices: 24.6 us -> 23.2 us
  local copies, waits for them, and re-layouts: 1.96 us -> 3.21 us
    all_to_all x1, waiting for transfers between devices: 21.9 us -> 0.01 us  [shards(): lax.all_to_all(wall.reshape(parts, rows_here, width), 'ga', 0, 0, tiled=T...]
    ppermute x1, waiting for transfers between devices: 0.01 us -> 20.6 us  [halo_planes(): ahead = lax.ppermute(field, 'gx', [(i + 1, i) for i in range(count - 1)])]
    all_to_all x1, waiting for transfers between devices: 19.5 us -> 15.4 us  [shards(): cols = lax.all_to_all(send, 'ga', 0, 0, tiled=True).reshape(rows, width)]
    ppermute x1, starting transfers between devices: 5.51 us -> 4.06 us  [halo_planes(): behind = lax.ppermute(field, 'gx', [(i, i + 1) for i in range(count - 1)])]
    unnamed x14 -> x15, local copies, waits for them, and re-layouts: 1.71 us -> 2.96 us
  transfers between devices with their start and end apart: 5 -> 5, of which waited for: 3 -> 3; matrix products, arithmetic and copies ran while one was open for 11% -> 14% of each run, Pallas kernels for 9% -> 10%
where the time goes in v7:
time: 102 us; the launch traced here: 101 us
  waiting for transfers between devices  43.6 us (43%)
  starting transfers between devices  23.2 us (23%)
  Pallas kernels  17.3 us (17%)
  matrix products  8.53 us (8%)
  other arithmetic  4.6 us (5%)
  local copies, waits for them, and re-layouts  3.21 us (3%)
    ppermute x1, waiting for transfers between devices, halo_planes(): ahead = lax.ppermute(field, 'gx', [(i + 1, i) for i in range(count - 1)])  20.6 us
    all_to_all x1, waiting for transfers between devices, shards(): cols = lax.all_to_all(send, 'ga', 0, 0, tiled=True).reshape(rows, width)  15.4 us
    all_to_all x1, starting transfers between devices, shards(): cols = lax.all_to_all(send, 'ga', 0, 0, tiled=True).reshape(rows, width)  11.8 us
    ppermute x1, waiting for transfers between devices, shards(): inflow = lax.ppermute(inflow, 'gx', [(source_slab, 0)])  7.69 us
    dot_general x1, matrix products, shards(): jnp.dot(lines, jnp.asarray(spanwise_table(span)), precision=HIGHEST, pref...  6.66 us
    pallas_call x1, Pallas kernels, wall_block(): pl.pallas_call(kernel, out_shape=jax.ShapeDtypeStruct((rows, width), jnp....  6.4 us
    all_to_all x1, starting transfers between devices, shards(): lax.all_to_all(wall.reshape(parts, rows_here, width), 'ga', 0, 0, tiled=T...  4.73 us
    ppermute x1, starting transfers between devices, halo_planes(): behind = lax.ppermute(field, 'gx', [(i, i + 1) for i in range(count - 1)])  4.06 us
  transfers between devices with their start and end apart: 5, of which 3 were waited for; matrix products, arithmetic and copies ran while one was open for 14% of the time, Pallas kernels for 10%

profile of v7, /device:TPU:1, one launch (start us, length us, event | category | flops | bytes accessed | tf_op | source)
XLA Modules:
  0.0 101.2 jit_solution(6586770971724854681)
XLA Ops:
  0.6 3.0 %shard_map.95 = f32[16,24,576]{2,1,0:T(8,128)} custom-call(f32[3,4,24,768]{3,2,1,0:T(8,128)} %v_ref.3), custom_call_target="tpu_custom_call" | custom-call | tf_op jit(solution)/shard_map/pallas_call | solution.py:94
  3.6 11.8 %all-to-all-start = ((f32[16,24,576]{2,1,0:T(8,128)}), f32[16,24,576]{2,1,0:T(8,128)S(1)}, u32[]{:S(2)}, u32[]{:S(2)}) async-start(f32[16,24,576]{2,1,0:T(8,128)} %shard_map.95), calls=%async_computation | async-start | bytes 1966080 | tf_op jit(solution)/shard_map/all_to_all | solution.py:182
  15.5 6.7 %convolution_bitcast_fusion = f32[288,1536]{1,0:T(8,128)S(1)} fusion(f32[768,1536]{1,0:T(8,128)} %constant.36.clone, f32[288,768]{1,0:T(8,128)S(1)} %bitcast.16), kind=kOutput, calls=%fused_computation | convolution fusion | flops 4076863488 | bytes 7372800 | tf_op jit(solution)/shard_map/dot_general | solution.py:184
  22.2 0.1 fusion.18
  22.4 0.1 negate_add_fusion
  22.5 4.1 %collective-permute-start.1 = (f32[3,4,24,768]{3,2,1,0:T(8,128)S(1)}, f32[3,4,24,768]{3,2,1,0:T(8,128)}, u32[]{:S(2)}, u32[]{:S(2)}) collective-permute-start(f32[3,4,24,768]{3,2,1,0:T(8,128)S(1)} %copy-done), channel_id=1, source_target_pairs={{0,16},{16,32},{32,48},{48,64},{64,80},{80,96},{96,112},{112,128},... | collective-permute-start | bytes 2654216 | tf_op jit(solution)/shard_map/ppermute | solution.py:51
  26.6 0.1 select_reduce_fusion
  26.7 15.4 %all-to-all-done = f32[16,24,576]{2,1,0:T(8,128)S(1)} async-done(((f32[16,24,576]{2,1,0:T(8,128)}), f32[16,24,576]{2,1,0:T(8,128)S(1)}, u32[]{:S(2)}, u32[]{:S(2)}) %all-to-all-start) | async-done | bytes 884768 | tf_op jit(solution)/shard_map/all_to_all | solution.py:182
  42.1 0.1 fusion.19
  42.2 1.9 %fusion.2 = f32[384,144]{1,0:T(8,128)} fusion(f32[384,48]{1,0:T(8,128)S(1)} %get-tuple-element.17, f32[384,48]{1,0:T(8,128)S(1)} %get-tuple-element.18, f32[384,48]{1,0:T(8,128)S(1)} %get-tuple-element.16, f32[384]{0:T(512)S(1)} %select_reduce_fusion, s32[384]{0:T(512)S(1)} %broadcast_add_fusion, f32[384]{0:T(512)S(1)} %broadcast_subtract_fusion, ...), kind=kOutput, calls=%fused_computation.11 | convolution fusion | flops 255651840 | bytes 448512 | tf_op jit(solution)/shard_map/dot_general | solution.py:203
  44.1 1.3 %collective-permute-start.2 = (f32[384,144]{1,0:T(8,128)}, f32[384,144]{1,0:T(8,128)S(1)}, u32[]{:S(2)}, u32[]{:S(2)}) collective-permute-start(f32[384,144]{1,0:T(8,128)} %fusion.2), channel_id=1, source_target_pairs={{496,0},{497,1},{498,2},{499,3},{500,4},{501,5},{502,6},{503,7},{5... | collective-permute-start | bytes 663560 | tf_op jit(solution)/shard_map/ppermute | solution.py:204
  45.4 6.4 %shard_map.96.w_ref = f32[384,576]{1,0:T(8,128)} custom-call(f32[384,576]{1,0:T(8,128)} %bitcast.18, f32[384,384]{1,0:T(8,128)} %f_ref.1, f32[384,384]{1,0:T(8,128)} %s_ref.1), custom_call_target="tpu_custom_call" | custom-call | tf_op jit(solution)/shard_map/pallas_call | solution.py:114
  51.8 7.7 %collective-permute-done.2.f_ref = f32[384,144]{1,0:T(8,128)S(1)} collective-permute-done((f32[384,144]{1,0:T(8,128)}, f32[384,144]{1,0:T(8,128)S(1)}, u32[]{:S(2)}, u32[]{:S(2)}) %collective-permute-start.2) | collective-permute-done | bytes 221216 | tf_op jit(solution)/shard_map/ppermute | solution.py:204
  59.5 0.7 copy-done.3
  60.2 4.0 %shard_map.97 = f32[384,576]{1,0:T(8,128)} custom-call(s32[1]{0:T(128)} %bitcast.8.inlet_ref, f32[384,576]{1,0:T(8,128)} %shard_map.96.w_ref, f32[384,576]{1,0:T(8,128)} %bitcast.19, f32[384,144]{1,0:T(8,128)} %copy-done.3), custom_call_target="tpu_custom_call", output_to_operand_aliasing={{}: (1, {})} | custom-call | tf_op jit(solution)/shard_map/pallas_call | solution.py:140
  64.2 4.7 %all-to-all-start.1 = ((f32[16,24,576]{2,1,0:T(8,128)}), f32[16,24,576]{2,1,0:T(8,128)S(1)}, u32[]{:S(2)}, u32[]{:S(2)}) async-start(f32[16,24,576]{2,1,0:T(8,128)} %bitcast.20), calls=%async_computation.1 | async-start | bytes 1966080 | tf_op jit(solution)/shard_map/all_to_all | solution.py:211
  68.9 1.3 %collective-permute-start = (f32[3,4,24,768]{3,2,1,0:T(8,128)S(1)}, f32[3,4,24,768]{3,2,1,0:T(8,128)}, u32[]{:S(2)}, u32[]{:S(2)}) collective-permute-start(f32[3,4,24,768]{3,2,1,0:T(8,128)S(1)} %copy-done), channel_id=1, source_target_pairs={{16,0},{32,16},{48,32},{64,48},{80,64},{96,80},{112,96},{128,112},... | collective-permute-start | bytes 2654216 | tf_op jit(solution)/shard_map/ppermute | solution.py:52
  70.2 1.2 %constant_dynamic-update-slice_fusion.1 = f32[3,8,24,768]{3,2,1,0:T(8,128)S(1)} fusion(f32[3,4,24,768]{3,2,1,0:T(8,128)} %collective-permute-done.1), kind=kLoop, calls=%fused_computation.34 | loop fusion | bytes 1769472
  71.5 0.1 constant_dynamic-update-slice_fusion
  71.5 20.6 %collective-permute-done = f32[3,4,24,768]{3,2,1,0:T(8,128)} collective-permute-done((f32[3,4,24,768]{3,2,1,0:T(8,128)S(1)}, f32[3,4,24,768]{3,2,1,0:T(8,128)}, u32[]{:S(2)}, u32[]{:S(2)}) %collective-permute-start) | collective-permute-done | bytes 884768 | tf_op jit(solution)/shard_map/ppermute | solution.py:52
  92.1 1.2 %broadcast_select_fusion = f32[3,4,24,768]{3,2,1,0:T(8,128)S(1)} fusion(f32[3,4,24,768]{3,2,1,0:T(8,128)} %collective-permute-done, f32[3,24,768]{2,1,0:T(8,128)S(1)} %slice_bitcast_fusion.2, pred[]{:T(512)S(6)} %eq.22), kind=kLoop, calls=%fused_computation.17 | loop fusion | flops 221184 | bytes 1990657 | tf_op jit(solution)/shard_map/jit(_where)/select_n | solution.py:60
  93.3 3.0 %add_add_fusion.t_ref = f32[3,4,24,768]{3,2,1,0:T(8,128)} fusion(f32[3,4,24,768]{3,2,1,0:T(8,128)S(1)} %negate_add_fusion, f32[3,4,24,768]{3,2,1,0:T(8,128)S(1)} %broadcast_select_fusion, f32[3,4,24,768]{3,2,1,0:T(8,128)} %collective-permute-done.1, f32[3,4,24,768]{3,2,1,0:T(8,128)S(1)} %copy-done, ...), kind=kLoop, calls=%fused_computation.9 | loop fusion | flops 7077888 | bytes 7372800 | tf_op jit(solution)/shard_map/add | solution.py:213
  96.3 0.9 copy-done.2
  97.3 3.9 %shard_map.98 = (f32[3,4,24,768]{3,2,1,0:T(8,128)}, f32[3,4,24,768]{3,2,1,0:T(8,128)}) custom-call(f32[3,4,24,768]{3,2,1,0:T(8,128)} %v_ref.3, f32[3,4,24,768]{3,2,1,0:T(8,128)} %a_ref.1, f32[3,4,24,768]{3,2,1,0:T(8,128)} %add_add_fusion.t_ref, f32[16,24,576]{2,1,0:T(8,128)} %copy-done.2), custom_call_target="tpu_custom_call" | custom-call | tf_op jit(solution)/shard_map/pallas_call | solution.py:169
  (18 shorter events, 0.1 us)
Async XLA Ops:
  0.6 14.8 %copy-start = (f32[3,4,24,768]{3,2,1,0:T(8,128)S(1)}, f32[3,4,24,768]{3,2,1,0:T(8,128)}, u32[]{:S(2)}) copy-start(f32[3,4,24,768]{3,2,1,0:T(8,128)} %v_ref.3) | copy-start | bytes 2654212
  3.6 38.4 %all-to-all-start = ((f32[16,24,576]{2,1,0:T(8,128)}), f32[16,24,576]{2,1,0:T(8,128)S(1)}, u32[]{:S(2)}, u32[]{:S(2)}) async-start(f32[16,24,576]{2,1,0:T(8,128)} %shard_map.95), calls=%async_computation | async-start | bytes 1966080 | tf_op jit(solution)/shard_map/all_to_all | solution.py:182
  22.3 4.2 %copy-start.4 = (s32[384]{0:T(512)S(1)}, s32[384]{0:T(512)}, u32[]{:S(2)}) copy-start(s32[384]{0:T(512)} %param.13) | copy-start | bytes 4612
  22.3 4.2 %copy-start.6 = (f32[64]{0:T(128)S(1)}, f32[64]{0:T(128)}, u32[]{:S(2)}) copy-start(f32[64]{0:T(128)} %param.14) | copy-start | bytes 772
  22.3 4.3 %copy-start.5 = (s32[384]{0:T(512)S(1)}, s32[384]{0:T(512)}, u32[]{:S(2)}) copy-start(s32[384]{0:T(512)} %param.12) | copy-start | bytes 4612
  22.5 47.7 %collective-permute-start.1 = (f32[3,4,24,768]{3,2,1,0:T(8,128)S(1)}, f32[3,4,24,768]{3,2,1,0:T(8,128)}, u32[]{:S(2)}, u32[]{:S(2)}) collective-permute-start(f32[3,4,24,768]{3,2,1,0:T(8,128)S(1)} %copy-done), channel_id=1, source_target_pairs={{0,16},{16,32},{32,48},{48,64},{64,80},{80,96},{96,112},{112,128},... | collective-permute-start | bytes 2654216 | tf_op jit(solution)/shard_map/ppermute | solution.py:51
  42.1 3.3 %copy-start.1 = (f32[16,24,576]{2,1,0:T(8,128)}, f32[16,24,576]{2,1,0:T(8,128)S(1)}, u32[]{:S(2)}) copy-start(f32[16,24,576]{2,1,0:T(8,128)S(1)} %all-to-all-done) | copy-start | bytes 2654212
  44.1 15.4 %collective-permute-start.2 = (f32[384,144]{1,0:T(8,128)}, f32[384,144]{1,0:T(8,128)S(1)}, u32[]{:S(2)}, u32[]{:S(2)}) collective-permute-start(f32[384,144]{1,0:T(8,128)} %fusion.2), channel_id=1, source_target_pairs={{496,0},{497,1},{498,2},{499,3},{500,4},{501,5},{502,6},{503,7},{5... | collective-permute-start | bytes 663560 | tf_op jit(solution)/shard_map/ppermute | solution.py:204
  59.5 0.7 copy-start.3
  64.2 32.2 %all-to-all-start.1 = ((f32[16,24,576]{2,1,0:T(8,128)}), f32[16,24,576]{2,1,0:T(8,128)S(1)}, u32[]{:S(2)}, u32[]{:S(2)}) async-start(f32[16,24,576]{2,1,0:T(8,128)} %bitcast.20), calls=%async_computation.1 | async-start | bytes 1966080 | tf_op jit(solution)/shard_map/all_to_all | solution.py:211
  68.9 23.2 %collective-permute-start = (f32[3,4,24,768]{3,2,1,0:T(8,128)S(1)}, f32[3,4,24,768]{3,2,1,0:T(8,128)}, u32[]{:S(2)}, u32[]{:S(2)}) collective-permute-start(f32[3,4,24,768]{3,2,1,0:T(8,128)S(1)} %copy-done), channel_id=1, source_target_pairs={{16,0},{32,16},{48,32},{64,48},{80,64},{96,80},{112,96},{128,112},... | collective-permute-start | bytes 2654216 | tf_op jit(solution)/shard_map/ppermute | solution.py:52
  96.3 1.0 copy-start.2

commit v8 on v7

--- a/solution.py
+++ b/solution.py
@@ -192,7 +192,7 @@
     span_terms = -(velocity[2:3] * span_first) + viscosity * span_second
     span_terms, halo_source = lax.optimization_barrier((span_terms, velocity))
     behind, ahead = halo_planes(halo_source)
-    cols, span_terms = lax.optimization_barrier((cols, span_terms))
+    cols, span_terms, behind = lax.optimization_barrier((cols, span_terms, behind))
 
     source_slab, source_plane = divmod(RECYCLE_PLANE, planes)
     mix = interpolation_matrix(recycle_rows, weight_index, weight_table, rows)

time: 102 us -> 108 us (1.059)
  starting transfers between devices: 23.2 us -> 26.4 us
  waiting for transfers between devices: 43.6 us -> 46.5 us
    all_to_all x1, waiting for transfers between devices: 0.01 us -> 21 us  [shards(): lax.all_to_all(wall.reshape(parts, rows_here, width), 'ga', 0, 0, tiled=T...]
    ppermute x1, waiting for transfers between devices: 20.6 us -> 0.01 us  [halo_planes(): ahead = lax.ppermute(field, 'gx', [(i + 1, i) for i in range(count - 1)])]
    ppermute x1, waiting for transfers between devices: 0.01 us -> 16.6 us  [halo_planes(): behind = lax.ppermute(field, 'gx', [(i, i + 1) for i in range(count - 1)])]
    all_to_all x1, waiting for transfers between devices: 15.4 us -> 0.01 us  [shards(): cols = lax.all_to_all(send, 'ga', 0, 0, tiled=True).reshape(rows, width)]
    all_to_all x1, starting transfers between devices: 4.73 us -> 7.98 us  [shards(): lax.all_to_all(wall.reshape(parts, rows_here, width), 'ga', 0, 0, tiled=T...]
    ppermute x1, waiting for transfers between devices: 7.69 us -> 8.85 us  [shards(): inflow = lax.ppermute(inflow, 'gx', [(source_slab, 0)])]
where the time goes in v8:
time: 108 us; the launch traced here: 107 us
  waiting for transfers between devices  46.5 us (43%)
  starting transfers between devices  26.4 us (24%)
  Pallas kernels  17.2 us (16%)
  matrix products  8.53 us (8%)
  other arithmetic  4.58 us (4%)
  local copies, waits for them, and re-layouts  3.2 us (3%)
    all_to_all x1, waiting for transfers between devices, shards(): lax.all_to_all(wall.reshape(parts, rows_here, width), 'ga', 0, 0, tiled=T...  21 us
    ppermute x1, waiting for transfers between devices, halo_planes(): behind = lax.ppermute(field, 'gx', [(i, i + 1) for i in range(count - 1)])  16.6 us
    all_to_all x1, starting transfers between devices, shards(): cols = lax.all_to_all(send, 'ga', 0, 0, tiled=True).reshape(rows, width)  11.8 us
    ppermute x1, waiting for transfers between devices, shards(): inflow = lax.ppermute(inflow, 'gx', [(source_slab, 0)])  8.85 us
    all_to_all x1, starting transfers between devices, shards(): lax.all_to_all(wall.reshape(parts, rows_here, width), 'ga', 0, 0, tiled=T...  7.98 us
    dot_general x1, matrix products, shards(): jnp.dot(lines, jnp.asarray(spanwise_table(span)), precision=HIGHEST, pref...  6.66 us
    pallas_call x1, Pallas kernels, wall_block(): pl.pallas_call(kernel, out_shape=jax.ShapeDtypeStruct((rows, width), jnp....  6.41 us
    ppermute x1, starting transfers between devices, halo_planes(): behind = lax.ppermute(field, 'gx', [(i, i + 1) for i in range(count - 1)])  4.07 us
  transfers between devices with their start and end apart: 5, of which 3 were waited for; matrix products, arithmetic and copies ran while one was open for 14% of the time, Pallas kernels for 10%

profile of v8, /device:TPU:1, one launch (start us, length us, event | category | flops | bytes accessed | tf_op | source)
XLA Modules:
  0.0 107.3 jit_solution(3664836219608272714)
XLA Ops:
  0.6 2.9 %shard_map.95 = f32[16,24,576]{2,1,0:T(8,128)} custom-call(f32[3,4,24,768]{3,2,1,0:T(8,128)} %v_ref.3), custom_call_target="tpu_custom_call" | custom-call | tf_op jit(solution)/shard_map/pallas_call | solution.py:94
  3.6 11.8 %all-to-all-start = ((f32[16,24,576]{2,1,0:T(8,128)}), f32[16,24,576]{2,1,0:T(8,128)S(1)}, u32[]{:S(2)}, u32[]{:S(2)}) async-start(f32[16,24,576]{2,1,0:T(8,128)} %shard_map.95), calls=%async_computation | async-start | bytes 1966080 | tf_op jit(solution)/shard_map/all_to_all | solution.py:182
  15.4 6.7 %convolution_bitcast_fusion = f32[288,1536]{1,0:T(8,128)S(1)} fusion(f32[768,1536]{1,0:T(8,128)} %constant.36.clone, f32[288,768]{1,0:T(8,128)S(1)} %bitcast.16), kind=kOutput, calls=%fused_computation | convolution fusion | flops 4076863488 | bytes 7372800 | tf_op jit(solution)/shard_map/dot_general | solution.py:184
  22.1 0.1 fusion.18
  22.3 0.1 negate_add_fusion
  22.4 4.1 %collective-permute-start = (f32[3,4,24,768]{3,2,1,0:T(8,128)S(1)}, f32[3,4,24,768]{3,2,1,0:T(8,128)}, u32[]{:S(2)}, u32[]{:S(2)}) collective-permute-start(f32[3,4,24,768]{3,2,1,0:T(8,128)S(1)} %copy-done), channel_id=1, source_target_pairs={{0,16},{16,32},{32,48},{48,64},{64,80},{80,96},{96,112},{112,128},... | collective-permute-start | bytes 2654216 | tf_op jit(solution)/shard_map/ppermute | solution.py:51
  26.5 1.3 %collective-permute-start.1 = (f32[3,4,24,768]{3,2,1,0:T(8,128)S(1)}, f32[3,4,24,768]{3,2,1,0:T(8,128)}, u32[]{:S(2)}, u32[]{:S(2)}) collective-permute-start(f32[3,4,24,768]{3,2,1,0:T(8,128)S(1)} %copy-done), channel_id=1, source_target_pairs={{16,0},{32,16},{48,32},{64,48},{80,64},{96,80},{112,96},{128,112},... | collective-permute-start | bytes 2654216 | tf_op jit(solution)/shard_map/ppermute | solution.py:52
  27.8 0.1 select_reduce_fusion
  27.9 16.6 %collective-permute-done = f32[3,4,24,768]{3,2,1,0:T(8,128)} collective-permute-done((f32[3,4,24,768]{3,2,1,0:T(8,128)S(1)}, f32[3,4,24,768]{3,2,1,0:T(8,128)}, u32[]{:S(2)}, u32[]{:S(2)}) %collective-permute-start) | collective-permute-done | bytes 884768 | tf_op jit(solution)/shard_map/ppermute | solution.py:51
  44.5 0.1 fusion.19
  44.7 1.9 %fusion.2 = f32[384,144]{1,0:T(8,128)} fusion(f32[384,48]{1,0:T(8,128)S(1)} %get-tuple-element.19, f32[384,48]{1,0:T(8,128)S(1)} %get-tuple-element.20, f32[384,48]{1,0:T(8,128)S(1)} %get-tuple-element.18, f32[384]{0:T(512)S(1)} %select_reduce_fusion, s32[384]{0:T(512)S(1)} %broadcast_add_fusion, f32[384]{0:T(512)S(1)} %broadcast_subtract_fusion, ...), kind=kOutput, calls=%fused_computation.11 | convolution fusion | flops 255651840 | bytes 448512 | tf_op jit(solution)/shard_map/dot_general | solution.py:203
  46.5 1.3 %collective-permute-start.2 = (f32[384,144]{1,0:T(8,128)}, f32[384,144]{1,0:T(8,128)S(1)}, u32[]{:S(2)}, u32[]{:S(2)}) collective-permute-start(f32[384,144]{1,0:T(8,128)} %fusion.2), channel_id=1, source_target_pairs={{496,0},{497,1},{498,2},{499,3},{500,4},{501,5},{502,6},{503,7},{5... | collective-permute-start | bytes 663560 | tf_op jit(solution)/shard_map/ppermute | solution.py:204
  47.8 6.4 %shard_map.96.w_ref = f32[384,576]{1,0:T(8,128)} custom-call(f32[384,576]{1,0:T(8,128)} %bitcast.18, f32[384,384]{1,0:T(8,128)} %f_ref.1, f32[384,384]{1,0:T(8,128)} %s_ref.1), custom_call_target="tpu_custom_call" | custom-call | tf_op jit(solution)/shard_map/pallas_call | solution.py:114
  54.2 8.8 %collective-permute-done.2.f_ref = f32[384,144]{1,0:T(8,128)S(1)} collective-permute-done((f32[384,144]{1,0:T(8,128)}, f32[384,144]{1,0:T(8,128)S(1)}, u32[]{:S(2)}, u32[]{:S(2)}) %collective-permute-start.2) | collective-permute-done | bytes 221216 | tf_op jit(solution)/shard_map/ppermute | solution.py:204
  63.1 0.7 copy-done.3
  63.8 4.0 %shard_map.97 = f32[384,576]{1,0:T(8,128)} custom-call(s32[1]{0:T(128)} %bitcast.8.inlet_ref, f32[384,576]{1,0:T(8,128)} %shard_map.96.w_ref, f32[384,576]{1,0:T(8,128)} %bitcast.19, f32[384,144]{1,0:T(8,128)} %copy-done.3), custom_call_target="tpu_custom_call", output_to_operand_aliasing={{}: (1, {})} | custom-call | tf_op jit(solution)/shard_map/pallas_call | solution.py:140
  67.8 8.0 %all-to-all-start.1 = ((f32[16,24,576]{2,1,0:T(8,128)}), f32[16,24,576]{2,1,0:T(8,128)S(1)}, u32[]{:S(2)}, u32[]{:S(2)}) async-start(f32[16,24,576]{2,1,0:T(8,128)} %bitcast.20), calls=%async_computation.1 | async-start | bytes 1966080 | tf_op jit(solution)/shard_map/all_to_all | solution.py:211
  75.8 1.2 %broadcast_select_fusion = f32[3,4,24,768]{3,2,1,0:T(8,128)S(1)} fusion(f32[3,4,24,768]{3,2,1,0:T(8,128)} %collective-permute-done.1, f32[3,24,768]{2,1,0:T(8,128)S(1)} %slice_bitcast_fusion.2, pred[]{:T(512)S(6)} %eq.22), kind=kLoop, calls=%fused_computation.17 | loop fusion | flops 221184 | bytes 1990657 | tf_op jit(solution)/shard_map/jit(_where)/select_n | solution.py:60
  77.1 1.2 %constant_dynamic-update-slice_fusion.1 = f32[3,8,24,768]{3,2,1,0:T(8,128)S(1)} fusion(f32[3,4,24,768]{3,2,1,0:T(8,128)} %collective-permute-done), kind=kLoop, calls=%fused_computation.34 | loop fusion | bytes 1769472
  78.3 0.1 constant_dynamic-update-slice_fusion
  78.4 3.0 %add_add_fusion.t_ref = f32[3,4,24,768]{3,2,1,0:T(8,128)} fusion(f32[3,4,24,768]{3,2,1,0:T(8,128)S(1)} %negate_add_fusion, f32[3,4,24,768]{3,2,1,0:T(8,128)S(1)} %broadcast_select_fusion, f32[3,4,24,768]{3,2,1,0:T(8,128)} %collective-permute-done, f32[3,4,24,768]{3,2,1,0:T(8,128)S(1)} %copy-done, f32[3,8,24,768]{3,2,1,0:T(8,128)S(1)} %constant_dynamic-update-slice_fusion, ...), kind=kLoop, calls=%fused_computation.9 | loop fusion | flops 7077888 | bytes 7372800 | tf_op jit(solution)/shard_map/add | solution.py:213
  81.4 21.0 %all-to-all-done.1.b_ref = f32[16,24,576]{2,1,0:T(8,128)S(1)} async-done(((f32[16,24,576]{2,1,0:T(8,128)}), f32[16,24,576]{2,1,0:T(8,128)S(1)}, u32[]{:S(2)}, u32[]{:S(2)}) %all-to-all-start.1) | async-done | bytes 884768 | tf_op jit(solution)/shard_map/all_to_all | solution.py:211
  102.4 0.9 copy-done.2
  103.3 3.9 %shard_map.98 = (f32[3,4,24,768]{3,2,1,0:T(8,128)}, f32[3,4,24,768]{3,2,1,0:T(8,128)}) custom-call(f32[3,4,24,768]{3,2,1,0:T(8,128)} %v_ref.3, f32[3,4,24,768]{3,2,1,0:T(8,128)} %a_ref.1, f32[3,4,24,768]{3,2,1,0:T(8,128)} %add_add_fusion.t_ref, f32[16,24,576]{2,1,0:T(8,128)} %copy-done.2), custom_call_target="tpu_custom_call" | custom-call | tf_op jit(solution)/shard_map/pallas_call | solution.py:169
  (18 shorter events, 0.1 us)
Async XLA Ops:
  0.6 14.8 %copy-start = (f32[3,4,24,768]{3,2,1,0:T(8,128)S(1)}, f32[3,4,24,768]{3,2,1,0:T(8,128)}, u32[]{:S(2)}) copy-start(f32[3,4,24,768]{3,2,1,0:T(8,128)} %v_ref.3) | copy-start | bytes 2654212
  3.6 41.0 %all-to-all-start = ((f32[16,24,576]{2,1,0:T(8,128)}), f32[16,24,576]{2,1,0:T(8,128)S(1)}, u32[]{:S(2)}, u32[]{:S(2)}) async-start(f32[16,24,576]{2,1,0:T(8,128)} %shard_map.95), calls=%async_computation | async-start | bytes 1966080 | tf_op jit(solution)/shard_map/all_to_all | solution.py:182
  22.3 5.5 %copy-start.4 = (s32[384]{0:T(512)S(1)}, s32[384]{0:T(512)}, u32[]{:S(2)}) copy-start(s32[384]{0:T(512)} %param.13) | copy-start | bytes 4612
  22.3 5.5 %copy-start.6 = (f32[64]{0:T(128)S(1)}, f32[64]{0:T(128)}, u32[]{:S(2)}) copy-start(f32[64]{0:T(128)} %param.14) | copy-start | bytes 772
  22.3 5.6 %copy-start.5 = (s32[384]{0:T(512)S(1)}, s32[384]{0:T(512)}, u32[]{:S(2)}) copy-start(s32[384]{0:T(512)} %param.12) | copy-start | bytes 4612
  22.4 22.1 %collective-permute-start = (f32[3,4,24,768]{3,2,1,0:T(8,128)S(1)}, f32[3,4,24,768]{3,2,1,0:T(8,128)}, u32[]{:S(2)}, u32[]{:S(2)}) collective-permute-start(f32[3,4,24,768]{3,2,1,0:T(8,128)S(1)} %copy-done), channel_id=1, source_target_pairs={{0,16},{16,32},{32,48},{48,64},{64,80},{80,96},{96,112},{112,128},... | collective-permute-start | bytes 2654216 | tf_op jit(solution)/shard_map/ppermute | solution.py:51
  26.5 49.3 %collective-permute-start.1 = (f32[3,4,24,768]{3,2,1,0:T(8,128)S(1)}, f32[3,4,24,768]{3,2,1,0:T(8,128)}, u32[]{:S(2)}, u32[]{:S(2)}) collective-permute-start(f32[3,4,24,768]{3,2,1,0:T(8,128)S(1)} %copy-done), channel_id=1, source_target_pairs={{16,0},{32,16},{48,32},{64,48},{80,64},{96,80},{112,96},{128,112},... | collective-permute-start | bytes 2654216 | tf_op jit(solution)/shard_map/ppermute | solution.py:52
  44.5 3.3 %copy-start.1 = (f32[16,24,576]{2,1,0:T(8,128)}, f32[16,24,576]{2,1,0:T(8,128)S(1)}, u32[]{:S(2)}) copy-start(f32[16,24,576]{2,1,0:T(8,128)S(1)} %all-to-all-done) | copy-start | bytes 2654212
  46.5 16.6 %collective-permute-start.2 = (f32[384,144]{1,0:T(8,128)}, f32[384,144]{1,0:T(8,128)S(1)}, u32[]{:S(2)}, u32[]{:S(2)}) collective-permute-start(f32[384,144]{1,0:T(8,128)} %fusion.2), channel_id=1, source_target_pairs={{496,0},{497,1},{498,2},{499,3},{500,4},{501,5},{502,6},{503,7},{5... | collective-permute-start | bytes 663560 | tf_op jit(solution)/shard_map/ppermute | solution.py:204
  63.1 0.7 copy-start.3
  67.8 34.6 %all-to-all-start.1 = ((f32[16,24,576]{2,1,0:T(8,128)}), f32[16,24,576]{2,1,0:T(8,128)S(1)}, u32[]{:S(2)}, u32[]{:S(2)}) async-start(f32[16,24,576]{2,1,0:T(8,128)} %bitcast.20), calls=%async_computation.1 | async-start | bytes 1966080 | tf_op jit(solution)/shard_map/all_to_all | solution.py:211
  102.4 0.9 copy-start.2

commit v9 on v4

--- a/solution.py
+++ b/solution.py
@@ -178,13 +178,14 @@
     rows = rows_here * parts
     width = comps * planes * share
 
-    behind, ahead = halo_planes(velocity)
     send = pack_columns(velocity, parts)
     cols = lax.all_to_all(send, "ga", 0, 0, tiled=True).reshape(rows, width)
-    cols, behind, ahead, field = lax.optimization_barrier((cols, behind, ahead, velocity))
+    mix = interpolation_matrix(recycle_rows, weight_index, weight_table, rows)
+    mix, halo_source = lax.optimization_barrier((mix, velocity))
+    behind, ahead = halo_planes(halo_source)
+    cols, mix, span_source = lax.optimization_barrier((cols, mix, velocity))
 
     source_slab, source_plane = divmod(RECYCLE_PLANE, planes)
-    mix = interpolation_matrix(recycle_rows, weight_index, weight_table, rows)
     plane = jnp.concatenate(
         [cols[:, (c * planes + source_plane) * share : (c * planes + source_plane + 1) * share] for c in range(comps)],
         axis=1,
@@ -193,7 +194,7 @@
     inflow = lax.ppermute(inflow, "gx", [(source_slab, 0)])
 
     wall = wall_block(cols, wall_first, wall_second, planes)
-    lines = field.reshape(-1, span)
+    lines = span_source.reshape(-1, span)
     spectral = jnp.dot(
         lines,
         jnp.asarray(spanwise_table(span)),
@@ -202,7 +203,7 @@
     )
     span_first = spectral[:, :span].reshape(velocity.shape)
     span_second = spectral[:, span:].reshape(velocity.shape)
-    span_terms = -(field[2:3] * span_first) + viscosity * span_second
+    span_terms = -(span_source[2:3] * span_first) + viscosity * span_second
     inflow, wall, span_terms = lax.optimization_barrier((inflow, wall, span_terms))
 
     inlet = (lax.axis_index("gx") == 0).astype(jnp.int32).reshape(1)

time: 108 us -> 102 us (0.944)
  the two profiles are of different devices: /device:TPU:31 before, /device:TPU:30 now
where the time goes in v9:
time: 102 us; the launch traced here: 101 us
  waiting for transfers between devices  43.3 us (42%)
  starting transfers between devices  24 us (24%)
  Pallas kernels  17.3 us (17%)
  matrix products  7.56 us (7%)
  other arithmetic  5.49 us (5%)
  local copies, waits for them, and re-layouts  2.46 us (2%)
    ppermute x1, waiting for transfers between devices, halo_planes(): ahead = lax.ppermute(field, 'gx', [(i + 1, i) for i in range(count - 1)])  23.1 us
    all_to_all x1, waiting for transfers between devices, shards(): cols = lax.all_to_all(send, 'ga', 0, 0, tiled=True).reshape(rows, width)  20.1 us
    all_to_all x1, starting transfers between devices, shards(): cols = lax.all_to_all(send, 'ga', 0, 0, tiled=True).reshape(rows, width)  10.4 us
    dot_general x1, matrix products, shards(): jnp.dot(lines, jnp.asarray(spanwise_table(span)), precision=HIGHEST, pref...  6.53 us
    pallas_call x1, Pallas kernels, wall_block(): pl.pallas_call(kernel, out_shape=jax.ShapeDtypeStruct((rows, width), jnp....  6.48 us
    all_to_all x1, starting transfers between devices, shards(): lax.all_to_all(wall.reshape(parts, rows_here, width), 'ga', 0, 0, tiled=T...  4.85 us
    ppermute x1, starting transfers between devices, halo_planes(): behind = lax.ppermute(field, 'gx', [(i, i + 1) for i in range(count - 1)])  4.61 us
    pallas_call x1, Pallas kernels, add_ghost(): pl.pallas_call(kernel, out_shape=jax.ShapeDtypeStruct((rows, width), jnp....  3.95 us
  transfers between devices with their start and end apart: 5, of which 2 were waited for; matrix products, arithmetic and copies ran while one was open for 14% of the time, Pallas kernels for 10%

profile of v9, /device:TPU:30, one launch (start us, length us, event | category | flops | bytes accessed | tf_op | source)
XLA Modules:
  0.0 101.0 jit_solution(6963460213796929293)
XLA Ops:
  0.6 0.0 copy-start
  0.7 3.0 %shard_map.95 = f32[16,24,576]{2,1,0:T(8,128)} custom-call(f32[3,4,24,768]{3,2,1,0:T(8,128)} %v_ref.3), custom_call_target="tpu_custom_call" | custom-call | tf_op jit(solution)/shard_map/pallas_call | solution.py:94
  3.7 10.4 %all-to-all-start = ((f32[16,24,576]{2,1,0:T(8,128)}), f32[16,24,576]{2,1,0:T(8,128)S(1)}, u32[]{:S(2)}, u32[]{:S(2)}) async-start(f32[16,24,576]{2,1,0:T(8,128)} %shard_map.95), calls=%async_computation | async-start | bytes 1966080 | tf_op jit(solution)/shard_map/all_to_all | solution.py:182
  14.1 0.1 select_reduce_fusion
  14.2 0.3 select_add_fusion
  14.5 4.6 %collective-permute-start.2 = (f32[3,4,24,768]{3,2,1,0:T(8,128)S(1)}, f32[3,4,24,768]{3,2,1,0:T(8,128)}, u32[]{:S(2)}, u32[]{:S(2)}) collective-permute-start(f32[3,4,24,768]{3,2,1,0:T(8,128)S(1)} %copy-done), channel_id=1, source_target_pairs={{0,16},{16,32},{32,48},{48,64},{64,80},{80,96},{96,112},{112,128},... | collective-permute-start | bytes 2654216 | tf_op jit(solution)/shard_map/ppermute | solution.py:51
  19.1 20.1 %all-to-all-done = f32[16,24,576]{2,1,0:T(8,128)S(1)} async-done(((f32[16,24,576]{2,1,0:T(8,128)}), f32[16,24,576]{2,1,0:T(8,128)S(1)}, u32[]{:S(2)}, u32[]{:S(2)}) %all-to-all-start) | async-done | bytes 884768 | tf_op jit(solution)/shard_map/all_to_all | solution.py:182
  39.3 0.1 fusion.10
  39.4 1.0 %fusion.2 = f32[384,144]{1,0:T(8,128)S(1)} fusion(f32[384,384]{1,0:T(8,128)S(1)} %select_add_fusion, f32[384,48]{1,0:T(8,128)S(1)} %get-tuple-element.21, f32[384,48]{1,0:T(8,128)S(1)} %get-tuple-element.22, f32[384,48]{1,0:T(8,128)S(1)} %get-tuple-element.20), kind=kOutput, calls=%fused_computation.14 | convolution fusion | flops 254914560 | bytes 1032192 | tf_op jit(solution)/shard_map/dot_general | solution.py:193
  40.4 1.4 %collective-permute-start = (f32[384,144]{1,0:T(8,128)S(1)}, f32[384,144]{1,0:T(8,128)}, u32[]{:S(2)}, u32[]{:S(2)}) collective-permute-start(f32[384,144]{1,0:T(8,128)S(1)} %fusion.2), channel_id=1, source_target_pairs={{496,0},{497,1},{498,2},{499,3},{500,4},{501,5},{502,6},{503,7},{5... | collective-permute-start | bytes 663560 | tf_op jit(solution)/shard_map/ppermute | solution.py:194
  41.9 6.5 %fusion.11 = f32[288,1536]{1,0:T(8,128)S(1)} fusion(f32[288,768]{1,0:T(8,128)S(1)} %bitcast.15, f32[768,1536]{1,0:T(8,128)} %constant.36.clone), kind=kOutput, calls=%fused_computation.32 | convolution fusion | flops 4076863488 | bytes 7372800 | tf_op jit(solution)/shard_map/dot_general | solution.py:198
  48.4 1.0 %fusion.9 = (f32[288,768]{1,0:T(8,128)S(1)}, f32[288,768]{1,0:T(8,128)}) fusion(f32[288,1536]{1,0:T(8,128)S(1)} %fusion.11), kind=kLoop, calls=%fused_computation.30 | loop fusion | flops 221184 | bytes 3538944 | tf_op jit(solution)/shard_map/slice | solution.py:204
  49.5 6.5 %shard_map.96.w_ref = f32[384,576]{1,0:T(8,128)} custom-call(f32[384,576]{1,0:T(8,128)} %bitcast.17, f32[384,384]{1,0:T(8,128)} %f_ref.1, f32[384,384]{1,0:T(8,128)} %s_ref.1), custom_call_target="tpu_custom_call" | custom-call | tf_op jit(solution)/shard_map/pallas_call | solution.py:114
  55.9 1.0 %negate_add_fusion = f32[3,4,24,768]{3,2,1,0:T(8,128)} fusion(f32[3,4,24,768]{3,2,1,0:T(8,128)S(1)} %bitcast.21, f32[3,4,24,768]{3,2,1,0:T(8,128)S(1)} %bitcast.20, f32[4,24,768]{2,1,0:T(8,128)S(1)} %slice_bitcast_fusion.1), kind=kLoop, calls=%fused_computation.9 | loop fusion | flops 663552 | bytes 2949120 | tf_op jit(solution)/shard_map/add | solution.py:206
  57.0 4.0 %shard_map.97 = f32[384,576]{1,0:T(8,128)} custom-call(s32[1]{0:T(128)} %bitcast.7.inlet_ref, f32[384,576]{1,0:T(8,128)} %shard_map.96.w_ref, f32[384,576]{1,0:T(8,128)} %bitcast.18, f32[384,144]{1,0:T(8,128)} %collective-permute-done.f_ref), custom_call_target="tpu_custom_call", output_to_operand_aliasing={{}: (1, {})} | custom-call | tf_op jit(solution)/shard_map/pallas_call | solution.py:140
  60.9 4.9 %all-to-all-start.1 = ((f32[16,24,576]{2,1,0:T(8,128)}), f32[16,24,576]{2,1,0:T(8,128)S(1)}, u32[]{:S(2)}, u32[]{:S(2)}) async-start(f32[16,24,576]{2,1,0:T(8,128)} %bitcast.19), calls=%async_computation.1 | async-start | bytes 1966080 | tf_op jit(solution)/shard_map/all_to_all | solution.py:211
  65.8 2.7 %collective-permute-start.1 = (f32[3,4,24,768]{3,2,1,0:T(8,128)S(1)}, f32[3,4,24,768]{3,2,1,0:T(8,128)S(1)}, u32[]{:S(2)}, u32[]{:S(2)}) collective-permute-start(f32[3,4,24,768]{3,2,1,0:T(8,128)S(1)} %copy-done), channel_id=1, source_target_pairs={{16,0},{32,16},{48,32},{64,48},{80,64},{96,80},{112,96},{128,112},... | collective-permute-start | bytes 2654216 | tf_op jit(solution)/shard_map/ppermute | solution.py:52
  68.6 1.2 %constant_dynamic-update-slice_fusion.1 = f32[3,8,24,768]{3,2,1,0:T(8,128)S(1)} fusion(f32[3,4,24,768]{3,2,1,0:T(8,128)} %collective-permute-done.2), kind=kLoop, calls=%fused_computation.26 | loop fusion | bytes 1769472
  69.9 0.1 constant_dynamic-update-slice_fusion
  69.9 23.1 %collective-permute-done.1 = f32[3,4,24,768]{3,2,1,0:T(8,128)S(1)} collective-permute-done((f32[3,4,24,768]{3,2,1,0:T(8,128)S(1)}, f32[3,4,24,768]{3,2,1,0:T(8,128)S(1)}, u32[]{:S(2)}, u32[]{:S(2)}) %collective-permute-start.1) | collective-permute-done | bytes 884768 | tf_op jit(solution)/shard_map/ppermute | solution.py:52
  93.1 0.1 broadcast_select_fusion
  93.1 3.0 %add_add_fusion.t_ref = f32[3,4,24,768]{3,2,1,0:T(8,128)} fusion(f32[3,4,24,768]{3,2,1,0:T(8,128)S(1)} %copy-done.4, f32[3,4,24,768]{3,2,1,0:T(8,128)S(1)} %broadcast_select_fusion, f32[3,4,24,768]{3,2,1,0:T(8,128)} %collective-permute-done.2, f32[3,4,24,768]{3,2,1,0:T(8,128)S(1)} %copy-done, f32[3,8,24,768]{3,2,1,0:T(8,128)S(1)} %constant_dynamic-update-slice_fusion, ...), kind=kLoop, calls=%fused_computation.8 | loop fusion | flops 7077888 | bytes 7372800 | tf_op jit(solution)/shard_map/add | solution.py:213
  96.1 0.9 copy-done.2
  97.1 3.9 %shard_map.98 = (f32[3,4,24,768]{3,2,1,0:T(8,128)}, f32[3,4,24,768]{3,2,1,0:T(8,128)}) custom-call(f32[3,4,24,768]{3,2,1,0:T(8,128)} %v_ref.3, f32[3,4,24,768]{3,2,1,0:T(8,128)} %a_ref.1, f32[3,4,24,768]{3,2,1,0:T(8,128)} %add_add_fusion.t_ref, f32[16,24,576]{2,1,0:T(8,128)} %copy-done.2), custom_call_target="tpu_custom_call" | custom-call | tf_op jit(solution)/shard_map/pallas_call | solution.py:169
  (22 shorter events, 0.1 us)
Async XLA Ops:
  0.6 13.9 %copy-start = (f32[3,4,24,768]{3,2,1,0:T(8,128)S(1)}, f32[3,4,24,768]{3,2,1,0:T(8,128)}, u32[]{:S(2)}) copy-start(f32[3,4,24,768]{3,2,1,0:T(8,128)} %v_ref.3) | copy-start | bytes 2654212
  0.6 13.4 %copy-start.6 = (s32[384]{0:T(512)S(1)}, s32[384]{0:T(512)}, u32[]{:S(2)}) copy-start(s32[384]{0:T(512)} %param.13) | copy-start | bytes 4612
  0.7 13.4 %copy-start.7 = (f32[64]{0:T(128)S(1)}, f32[64]{0:T(128)}, u32[]{:S(2)}) copy-start(f32[64]{0:T(128)} %param.14) | copy-start | bytes 772
  0.7 13.5 %copy-start.5 = (s32[384]{0:T(512)S(1)}, s32[384]{0:T(512)}, u32[]{:S(2)}) copy-start(s32[384]{0:T(512)} %param.12) | copy-start | bytes 4612
  3.7 35.6 %all-to-all-start = ((f32[16,24,576]{2,1,0:T(8,128)}), f32[16,24,576]{2,1,0:T(8,128)S(1)}, u32[]{:S(2)}, u32[]{:S(2)}) async-start(f32[16,24,576]{2,1,0:T(8,128)} %shard_map.95), calls=%async_computation | async-start | bytes 1966080 | tf_op jit(solution)/shard_map/all_to_all | solution.py:182
  14.5 54.1 %collective-permute-start.2 = (f32[3,4,24,768]{3,2,1,0:T(8,128)S(1)}, f32[3,4,24,768]{3,2,1,0:T(8,128)}, u32[]{:S(2)}, u32[]{:S(2)}) collective-permute-start(f32[3,4,24,768]{3,2,1,0:T(8,128)S(1)} %copy-done), channel_id=1, source_target_pairs={{0,16},{16,32},{32,48},{48,64},{64,80},{80,96},{96,112},{112,128},... | collective-permute-start | bytes 2654216 | tf_op jit(solution)/shard_map/ppermute | solution.py:51
  39.3 9.1 %copy-start.1 = (f32[16,24,576]{2,1,0:T(8,128)}, f32[16,24,576]{2,1,0:T(8,128)S(1)}, u32[]{:S(2)}) copy-start(f32[16,24,576]{2,1,0:T(8,128)S(1)} %all-to-all-done) | copy-start | bytes 2654212
  40.4 16.5 %collective-permute-start = (f32[384,144]{1,0:T(8,128)S(1)}, f32[384,144]{1,0:T(8,128)}, u32[]{:S(2)}, u32[]{:S(2)}) collective-permute-start(f32[384,144]{1,0:T(8,128)S(1)} %fusion.2), channel_id=1, source_target_pairs={{496,0},{497,1},{498,2},{499,3},{500,4},{501,5},{502,6},{503,7},{5... | collective-permute-start | bytes 663560 | tf_op jit(solution)/shard_map/ppermute | solution.py:194
  49.5 6.5 %copy-start.3 = (f32[288,768]{1,0:T(8,128)S(1)}, f32[288,768]{1,0:T(8,128)}, u32[]{:S(2)}) copy-start(f32[288,768]{1,0:T(8,128)} %get-tuple-element.19) | copy-start | bytes 2654212
  60.9 35.2 %all-to-all-start.1 = ((f32[16,24,576]{2,1,0:T(8,128)}), f32[16,24,576]{2,1,0:T(8,128)S(1)}, u32[]{:S(2)}, u32[]{:S(2)}) async-start(f32[16,24,576]{2,1,0:T(8,128)} %bitcast.19), calls=%async_computation.1 | async-start | bytes 1966080 | tf_op jit(solution)/shard_map/all_to_all | solution.py:211
  65.8 27.3 %collective-permute-start.1 = (f32[3,4,24,768]{3,2,1,0:T(8,128)S(1)}, f32[3,4,24,768]{3,2,1,0:T(8,128)S(1)}, u32[]{:S(2)}, u32[]{:S(2)}) collective-permute-start(f32[3,4,24,768]{3,2,1,0:T(8,128)S(1)} %copy-done), channel_id=1, source_target_pairs={{16,0},{32,16},{48,32},{64,48},{80,64},{96,80},{112,96},{128,112},... | collective-permute-start | bytes 2654216 | tf_op jit(solution)/shard_map/ppermute | solution.py:52
  69.8 23.3 %copy-start.4 = (f32[3,4,24,768]{3,2,1,0:T(8,128)S(1)}, f32[3,4,24,768]{3,2,1,0:T(8,128)}, u32[]{:S(2)}) copy-start(f32[3,4,24,768]{3,2,1,0:T(8,128)} %negate_add_fusion) | copy-start | bytes 2654212
  96.1 1.0 copy-start.2

commit v10 on v9

--- a/solution.py
+++ b/solution.py
@@ -122,32 +122,33 @@
     share = width // (comps * planes)
     block = planes * share
     lower, upper = ghost_weights(planes)
-
-    def kernel(inlet_ref, w_ref, c_ref, f_ref, o_ref):
+    gain = np.tile(np.repeat(lower, share), comps)[None, :]
+    bias = np.tile(np.repeat(viscosity * upper, share), comps)[None, :]
+
+    def kernel(inlet_ref, w_ref, c_ref, f_ref, g_ref, b_ref, o_ref):
         at_inlet = inlet_ref[0] > 0
-        for c in range(comps):
-            flow = f_ref[:, c * share : (c + 1) * share]
-            ghost = jnp.concatenate(
-                [
-                    flow * (c_ref[:, x * share : (x + 1) * share] * lower[x] + viscosity * upper[x])
-                    for x in range(planes)
-                ],
+
+        @pl.when(at_inlet)
+        def _():
+            flow = jnp.concatenate(
+                [f_ref[:, c * share : (c + 1) * share] for c in range(comps) for x in range(planes)],
                 axis=1,
             )
-            part = slice(c * block, (c + 1) * block)
-            o_ref[:, part] = w_ref[:, part] + jnp.where(at_inlet, ghost, 0.0)
-
+            first = c_ref[:, 0:block]
+            spread = jnp.concatenate([first] * comps, axis=1)
+            o_ref[...] = w_ref[...] + flow * (spread * g_ref[...] + b_ref[...])
+
+        @pl.when(jnp.logical_not(at_inlet))
+        def _():
+            o_ref[...] = w_ref[...]
+
+    vmem = pl.BlockSpec(memory_space=pltpu.VMEM)
     return pl.pallas_call(
         kernel,
         out_shape=jax.ShapeDtypeStruct((rows, width), jnp.float32),
-        in_specs=[
-            pl.BlockSpec(memory_space=pltpu.SMEM),
-            pl.BlockSpec(memory_space=pltpu.VMEM),
-            pl.BlockSpec(memory_space=pltpu.VMEM),
-            pl.BlockSpec(memory_space=pltpu.VMEM),
-        ],
+        in_specs=[pl.BlockSpec(memory_space=pltpu.SMEM)] + [vmem] * 5,
         input_output_aliases={1: 0},
-    )(inlet, wall, cols, inflow)
+    )(inlet, wall, cols, inflow, jnp.asarray(gain, jnp.float32), jnp.asarray(bias, jnp.float32))
 
 
 def combine(velocity, accumulated, local_terms, back):

time: 102 us -> 100 us (0.980)
  Pallas kernels: 17.3 us -> 16.1 us
    pallas_call x1, Pallas kernels: 3.95 us -> 2.68 us  [add_ghost(): pl.pallas_call(kernel, out_shape=jax.ShapeDtypeStruct((rows, width), jnp....]
  transfers between devices with their start and end apart: 5 -> 5, of which waited for: 2 -> 2; matrix products, arithmetic and copies ran while one was open for 14% -> 15% of each run, Pallas kernels for 10% -> 9%
where the time goes in v10:
time: 100 us; the launch traced here: 99.8 us
  waiting for transfers between devices  43.3 us (43%)
  starting transfers between devices  24 us (24%)
  Pallas kernels  16.1 us (16%)
  matrix products  7.56 us (8%)
  other arithmetic  5.49 us (5%)
  local copies, waits for them, and re-layouts  2.46 us (2%)
    ppermute x1, waiting for transfers between devices, halo_planes(): ahead = lax.ppermute(field, 'gx', [(i + 1, i) for i in range(count - 1)])  23.1 us
    all_to_all x1, waiting for transfers between devices, shards(): cols = lax.all_to_all(send, 'ga', 0, 0, tiled=True).reshape(rows, width)  20.1 us
    all_to_all x1, starting transfers between devices, shards(): cols = lax.all_to_all(send, 'ga', 0, 0, tiled=True).reshape(rows, width)  10.4 us
    dot_general x1, matrix products, shards(): jnp.dot(lines, jnp.asarray(spanwise_table(span)), precision=HIGHEST, pref...  6.53 us
    pallas_call x1, Pallas kernels, wall_block(): pl.pallas_call(kernel, out_shape=jax.ShapeDtypeStruct((rows, width), jnp....  6.48 us
    all_to_all x1, starting transfers between devices, shards(): lax.all_to_all(wall.reshape(parts, rows_here, width), 'ga', 0, 0, tiled=T...  4.85 us
    ppermute x1, starting transfers between devices, halo_planes(): behind = lax.ppermute(field, 'gx', [(i, i + 1) for i in range(count - 1)])  4.61 us
    pallas_call x1, Pallas kernels, combine(): pl.pallas_call(kernel, out_shape=(shape, shape))  3.94 us
  transfers between devices with their start and end apart: 5, of which 2 were waited for; matrix products, arithmetic and copies ran while one was open for 15% of the time, Pallas kernels for 9%

profile of v10, /device:TPU:30, one launch (start us, length us, event | category | flops | bytes accessed | tf_op | source)
XLA Modules:
  0.0 99.8 jit_solution(3305387339594728037)
XLA Ops:
  0.6 0.0 copy-start
  0.7 3.0 %shard_map.113 = f32[16,24,576]{2,1,0:T(8,128)} custom-call(f32[3,4,24,768]{3,2,1,0:T(8,128)} %v_ref.3), custom_call_target="tpu_custom_call" | custom-call | tf_op jit(solution)/shard_map/pallas_call | solution.py:94
  3.7 10.4 %all-to-all-start = ((f32[16,24,576]{2,1,0:T(8,128)}), f32[16,24,576]{2,1,0:T(8,128)S(1)}, u32[]{:S(2)}, u32[]{:S(2)}) async-start(f32[16,24,576]{2,1,0:T(8,128)} %shard_map.113), calls=%async_computation | async-start | bytes 1966080 | tf_op jit(solution)/shard_map/all_to_all | solution.py:183
  14.1 0.1 select_reduce_fusion
  14.2 0.3 select_add_fusion
  14.5 4.6 %collective-permute-start.2 = (f32[3,4,24,768]{3,2,1,0:T(8,128)S(1)}, f32[3,4,24,768]{3,2,1,0:T(8,128)}, u32[]{:S(2)}, u32[]{:S(2)}) collective-permute-start(f32[3,4,24,768]{3,2,1,0:T(8,128)S(1)} %copy-done), channel_id=1, source_target_pairs={{0,16},{16,32},{32,48},{48,64},{64,80},{80,96},{96,112},{112,128},... | collective-permute-start | bytes 2654216 | tf_op jit(solution)/shard_map/ppermute | solution.py:51
  19.1 20.1 %all-to-all-done = f32[16,24,576]{2,1,0:T(8,128)S(1)} async-done(((f32[16,24,576]{2,1,0:T(8,128)}), f32[16,24,576]{2,1,0:T(8,128)S(1)}, u32[]{:S(2)}, u32[]{:S(2)}) %all-to-all-start) | async-done | bytes 884768 | tf_op jit(solution)/shard_map/all_to_all | solution.py:183
  39.3 0.1 fusion.10
  39.4 1.0 %fusion.2 = f32[384,144]{1,0:T(8,128)S(1)} fusion(f32[384,384]{1,0:T(8,128)S(1)} %select_add_fusion, f32[384,48]{1,0:T(8,128)S(1)} %get-tuple-element.21, f32[384,48]{1,0:T(8,128)S(1)} %get-tuple-element.22, f32[384,48]{1,0:T(8,128)S(1)} %get-tuple-element.20), kind=kOutput, calls=%fused_computation.14 | convolution fusion | flops 254914560 | bytes 1032192 | tf_op jit(solution)/shard_map/dot_general | solution.py:194
  40.4 1.4 %collective-permute-start = (f32[384,144]{1,0:T(8,128)S(1)}, f32[384,144]{1,0:T(8,128)}, u32[]{:S(2)}, u32[]{:S(2)}) collective-permute-start(f32[384,144]{1,0:T(8,128)S(1)} %fusion.2), channel_id=1, source_target_pairs={{496,0},{497,1},{498,2},{499,3},{500,4},{501,5},{502,6},{503,7},{5... | collective-permute-start | bytes 663560 | tf_op jit(solution)/shard_map/ppermute | solution.py:195
  41.9 6.5 %fusion.11 = f32[288,1536]{1,0:T(8,128)S(1)} fusion(f32[288,768]{1,0:T(8,128)S(1)} %bitcast.15, f32[768,1536]{1,0:T(8,128)} %constant.40.clone), kind=kOutput, calls=%fused_computation.32 | convolution fusion | flops 4076863488 | bytes 7372800 | tf_op jit(solution)/shard_map/dot_general | solution.py:199
  48.4 1.0 %fusion.9 = (f32[288,768]{1,0:T(8,128)S(1)}, f32[288,768]{1,0:T(8,128)}) fusion(f32[288,1536]{1,0:T(8,128)S(1)} %fusion.11), kind=kLoop, calls=%fused_computation.30 | loop fusion | flops 221184 | bytes 3538944 | tf_op jit(solution)/shard_map/slice | solution.py:205
  49.5 6.5 %shard_map.114.w_ref = f32[384,576]{1,0:T(8,128)} custom-call(f32[384,576]{1,0:T(8,128)} %bitcast.17, f32[384,384]{1,0:T(8,128)} %f_ref.1, f32[384,384]{1,0:T(8,128)} %s_ref.1), custom_call_target="tpu_custom_call" | custom-call | tf_op jit(solution)/shard_map/pallas_call | solution.py:114
  55.9 1.0 %negate_add_fusion = f32[3,4,24,768]{3,2,1,0:T(8,128)} fusion(f32[3,4,24,768]{3,2,1,0:T(8,128)S(1)} %bitcast.21, f32[3,4,24,768]{3,2,1,0:T(8,128)S(1)} %bitcast.20, f32[4,24,768]{2,1,0:T(8,128)S(1)} %slice_bitcast_fusion.1), kind=kLoop, calls=%fused_computation.9 | loop fusion | flops 663552 | bytes 2949120 | tf_op jit(solution)/shard_map/add | solution.py:207
  57.0 2.7 %shard_map.115 = f32[384,576]{1,0:T(8,128)} custom-call(s32[1]{0:T(128)} %bitcast.7.inlet_ref, f32[384,576]{1,0:T(8,128)} %shard_map.114.w_ref, f32[384,576]{1,0:T(8,128)} %bitcast.18, f32[384,144]{1,0:T(8,128)} %collective-permute-done.f_ref, f32[1,576]{1,0:T(1,128)} %constant.41.clone.g_ref, ...), custom_call_target="tpu_custom_call", output_to_operand_aliasing={{}: (1, {})} | custom-call | tf_op jit(solution)/shard_map/pallas_call | solution.py:146
  59.6 4.9 %all-to-all-start.1 = ((f32[16,24,576]{2,1,0:T(8,128)}), f32[16,24,576]{2,1,0:T(8,128)S(1)}, u32[]{:S(2)}, u32[]{:S(2)}) async-start(f32[16,24,576]{2,1,0:T(8,128)} %bitcast.19), calls=%async_computation.1 | async-start | bytes 1966080 | tf_op jit(solution)/shard_map/all_to_all | solution.py:212
  64.5 2.7 %collective-permute-start.1 = (f32[3,4,24,768]{3,2,1,0:T(8,128)S(1)}, f32[3,4,24,768]{3,2,1,0:T(8,128)S(1)}, u32[]{:S(2)}, u32[]{:S(2)}) collective-permute-start(f32[3,4,24,768]{3,2,1,0:T(8,128)S(1)} %copy-done), channel_id=1, source_target_pairs={{16,0},{32,16},{48,32},{64,48},{80,64},{96,80},{112,96},{128,112},... | collective-permute-start | bytes 2654216 | tf_op jit(solution)/shard_map/ppermute | solution.py:52
  67.3 1.2 %constant_dynamic-update-slice_fusion.1 = f32[3,8,24,768]{3,2,1,0:T(8,128)S(1)} fusion(f32[3,4,24,768]{3,2,1,0:T(8,128)} %collective-permute-done.2), kind=kLoop, calls=%fused_computation.26 | loop fusion | bytes 1769472
  68.6 0.1 constant_dynamic-update-slice_fusion
  68.7 23.1 %collective-permute-done.1 = f32[3,4,24,768]{3,2,1,0:T(8,128)S(1)} collective-permute-done((f32[3,4,24,768]{3,2,1,0:T(8,128)S(1)}, f32[3,4,24,768]{3,2,1,0:T(8,128)S(1)}, u32[]{:S(2)}, u32[]{:S(2)}) %collective-permute-start.1) | collective-permute-done | bytes 884768 | tf_op jit(solution)/shard_map/ppermute | solution.py:52
  91.8 0.1 broadcast_select_fusion
  91.9 3.0 %add_add_fusion.t_ref = f32[3,4,24,768]{3,2,1,0:T(8,128)} fusion(f32[3,4,24,768]{3,2,1,0:T(8,128)S(1)} %copy-done.4, f32[3,4,24,768]{3,2,1,0:T(8,128)S(1)} %broadcast_select_fusion, f32[3,4,24,768]{3,2,1,0:T(8,128)} %collective-permute-done.2, f32[3,4,24,768]{3,2,1,0:T(8,128)S(1)} %copy-done, f32[3,8,24,768]{3,2,1,0:T(8,128)S(1)} %constant_dynamic-update-slice_fusion, ...), kind=kLoop, calls=%fused_computation.8 | loop fusion | flops 7077888 | bytes 7372800 | tf_op jit(solution)/shard_map/add | solution.py:214
  94.9 0.9 copy-done.2
  95.8 3.9 %shard_map.116 = (f32[3,4,24,768]{3,2,1,0:T(8,128)}, f32[3,4,24,768]{3,2,1,0:T(8,128)}) custom-call(f32[3,4,24,768]{3,2,1,0:T(8,128)} %v_ref.3, f32[3,4,24,768]{3,2,1,0:T(8,128)} %a_ref.1, f32[3,4,24,768]{3,2,1,0:T(8,128)} %add_add_fusion.t_ref, f32[16,24,576]{2,1,0:T(8,128)} %copy-done.2), custom_call_target="tpu_custom_call" | custom-call | tf_op jit(solution)/shard_map/pallas_call | solution.py:170
  (22 shorter events, 0.1 us)
Async XLA Ops:
  0.6 13.9 %copy-start = (f32[3,4,24,768]{3,2,1,0:T(8,128)S(1)}, f32[3,4,24,768]{3,2,1,0:T(8,128)}, u32[]{:S(2)}) copy-start(f32[3,4,24,768]{3,2,1,0:T(8,128)} %v_ref.3) | copy-start | bytes 2654212
  0.6 13.4 %copy-start.6 = (s32[384]{0:T(512)S(1)}, s32[384]{0:T(512)}, u32[]{:S(2)}) copy-start(s32[384]{0:T(512)} %param.15) | copy-start | bytes 4612
  0.7 13.4 %copy-start.7 = (f32[64]{0:T(128)S(1)}, f32[64]{0:T(128)}, u32[]{:S(2)}) copy-start(f32[64]{0:T(128)} %param.16) | copy-start | bytes 772
  0.7 13.5 %copy-start.5 = (s32[384]{0:T(512)S(1)}, s32[384]{0:T(512)}, u32[]{:S(2)}) copy-start(s32[384]{0:T(512)} %param.14) | copy-start | bytes 4612
  3.7 35.6 %all-to-all-start = ((f32[16,24,576]{2,1,0:T(8,128)}), f32[16,24,576]{2,1,0:T(8,128)S(1)}, u32[]{:S(2)}, u32[]{:S(2)}) async-start(f32[16,24,576]{2,1,0:T(8,128)} %shard_map.113), calls=%async_computation | async-start | bytes 1966080 | tf_op jit(solution)/shard_map/all_to_all | solution.py:183
  14.5 52.8 %collective-permute-start.2 = (f32[3,4,24,768]{3,2,1,0:T(8,128)S(1)}, f32[3,4,24,768]{3,2,1,0:T(8,128)}, u32[]{:S(2)}, u32[]{:S(2)}) collective-permute-start(f32[3,4,24,768]{3,2,1,0:T(8,128)S(1)} %copy-done), channel_id=1, source_target_pairs={{0,16},{16,32},{32,48},{48,64},{64,80},{80,96},{96,112},{112,128},... | collective-permute-start | bytes 2654216 | tf_op jit(solution)/shard_map/ppermute | solution.py:51
  39.3 9.1 %copy-start.1 = (f32[16,24,576]{2,1,0:T(8,128)}, f32[16,24,576]{2,1,0:T(8,128)S(1)}, u32[]{:S(2)}) copy-start(f32[16,24,576]{2,1,0:T(8,128)S(1)} %all-to-all-done) | copy-start | bytes 2654212
  40.4 16.5 %collective-permute-start = (f32[384,144]{1,0:T(8,128)S(1)}, f32[384,144]{1,0:T(8,128)}, u32[]{:S(2)}, u32[]{:S(2)}) collective-permute-start(f32[384,144]{1,0:T(8,128)S(1)} %fusion.2), channel_id=1, source_target_pairs={{496,0},{497,1},{498,2},{499,3},{500,4},{501,5},{502,6},{503,7},{5... | collective-permute-start | bytes 663560 | tf_op jit(solution)/shard_map/ppermute | solution.py:195
  49.5 6.5 %copy-start.3 = (f32[288,768]{1,0:T(8,128)S(1)}, f32[288,768]{1,0:T(8,128)}, u32[]{:S(2)}) copy-start(f32[288,768]{1,0:T(8,128)} %get-tuple-element.19) | copy-start | bytes 2654212
  59.6 35.2 %all-to-all-start.1 = ((f32[16,24,576]{2,1,0:T(8,128)}), f32[16,24,576]{2,1,0:T(8,128)S(1)}, u32[]{:S(2)}, u32[]{:S(2)}) async-start(f32[16,24,576]{2,1,0:T(8,128)} %bitcast.19), calls=%async_computation.1 | async-start | bytes 1966080 | tf_op jit(solution)/shard_map/all_to_all | solution.py:212
  64.5 27.3 %collective-permute-start.1 = (f32[3,4,24,768]{3,2,1,0:T(8,128)S(1)}, f32[3,4,24,768]{3,2,1,0:T(8,128)S(1)}, u32[]{:S(2)}, u32[]{:S(2)}) collective-permute-start(f32[3,4,24,768]{3,2,1,0:T(8,128)S(1)} %copy-done), channel_id=1, source_target_pairs={{16,0},{32,16},{48,32},{64,48},{80,64},{96,80},{112,96},{128,112},... | collective-permute-start | bytes 2654216 | tf_op jit(solution)/shard_map/ppermute | solution.py:52
  68.6 23.3 %copy-start.4 = (f32[3,4,24,768]{3,2,1,0:T(8,128)S(1)}, f32[3,4,24,768]{3,2,1,0:T(8,128)}, u32[]{:S(2)}) copy-start(f32[3,4,24,768]{3,2,1,0:T(8,128)} %negate_add_fusion) | copy-start | bytes 2654212
  94.9 1.0 copy-start.2

commit v11 on v10

--- a/solution.py
+++ b/solution.py
@@ -184,7 +184,7 @@
     mix = interpolation_matrix(recycle_rows, weight_index, weight_table, rows)
     mix, halo_source = lax.optimization_barrier((mix, velocity))
     behind, ahead = halo_planes(halo_source)
-    cols, mix, span_source = lax.optimization_barrier((cols, mix, velocity))
+    cols, mix, span_source, behind, ahead = lax.optimization_barrier((cols, mix, velocity, behind, ahead))
 
     source_slab, source_plane = divmod(RECYCLE_PLANE, planes)
     plane = jnp.concatenate(

time: 100 us -> 107 us (1.070)
  the two profiles are of different devices: /device:TPU:30 before, /device:TPU:31 now
where the time goes in v11:
time: 107 us; the launch traced here: 106 us
  waiting for transfers between devices  46.5 us (43%)
  starting transfers between devices  26.1 us (24%)
  Pallas kernels  16 us (15%)
  matrix products  8.32 us (8%)
  other arithmetic  5.61 us (5%)
  local copies, waits for them, and re-layouts  3.08 us (3%)
    all_to_all x1, waiting for transfers between devices, shards(): lax.all_to_all(wall.reshape(parts, rows_here, width), 'ga', 0, 0, tiled=T...  22.2 us
    ppermute x1, waiting for transfers between devices, halo_planes(): behind = lax.ppermute(field, 'gx', [(i, i + 1) for i in range(count - 1)])  17 us
    all_to_all x1, starting transfers between devices, shards(): cols = lax.all_to_all(send, 'ga', 0, 0, tiled=True).reshape(rows, width)  11 us
    all_to_all x1, starting transfers between devices, shards(): lax.all_to_all(wall.reshape(parts, rows_here, width), 'ga', 0, 0, tiled=T...  8.16 us
    ppermute x1, waiting for transfers between devices, halo_planes(): ahead = lax.ppermute(field, 'gx', [(i + 1, i) for i in range(count - 1)])  7.22 us
    dot_general x1, matrix products, shards(): jnp.dot(lines, jnp.asarray(spanwise_table(span)), precision=HIGHEST, pref...  6.53 us
    pallas_call x1, Pallas kernels, wall_block(): pl.pallas_call(kernel, out_shape=jax.ShapeDtypeStruct((rows, width), jnp....  6.45 us
    ppermute x1, starting transfers between devices, halo_planes(): behind = lax.ppermute(field, 'gx', [(i, i + 1) for i in range(count - 1)])  4.35 us
  transfers between devices with their start and end apart: 5, of which 3 were waited for; matrix products, arithmetic and copies ran while one was open for 12% of the time, Pallas kernels for 6%

profile of v11, /device:TPU:31, one launch (start us, length us, event | category | flops | bytes accessed | tf_op | source)
XLA Modules:
  0.0 106.4 jit_solution(2385375344866339439)
XLA Ops:
  0.7 2.9 %shard_map.113 = f32[16,24,576]{2,1,0:T(8,128)} custom-call(f32[3,4,24,768]{3,2,1,0:T(8,128)} %v_ref.3), custom_call_target="tpu_custom_call" | custom-call | tf_op jit(solution)/shard_map/pallas_call | solution.py:94
  3.6 11.0 %all-to-all-start = ((f32[16,24,576]{2,1,0:T(8,128)}), f32[16,24,576]{2,1,0:T(8,128)S(1)}, u32[]{:S(2)}, u32[]{:S(2)}) async-start(f32[16,24,576]{2,1,0:T(8,128)} %shard_map.113), calls=%async_computation | async-start | bytes 1966080 | tf_op jit(solution)/shard_map/all_to_all | solution.py:183
  14.6 0.1 select_reduce_fusion
  14.7 0.3 select_add_fusion
  15.0 4.4 %collective-permute-start = (f32[3,4,24,768]{3,2,1,0:T(8,128)S(1)}, f32[3,4,24,768]{3,2,1,0:T(8,128)S(1)}, u32[]{:S(2)}, u32[]{:S(2)}) collective-permute-start(f32[3,4,24,768]{3,2,1,0:T(8,128)S(1)} %copy-done), channel_id=1, source_target_pairs={{0,16},{16,32},{32,48},{48,64},{64,80},{80,96},{96,112},{112,128},... | collective-permute-start | bytes 2654216 | tf_op jit(solution)/shard_map/ppermute | solution.py:51
  19.4 1.9 %collective-permute-start.1 = (f32[3,4,24,768]{3,2,1,0:T(8,128)S(1)}, f32[3,4,24,768]{3,2,1,0:T(8,128)}, u32[]{:S(2)}, u32[]{:S(2)}) collective-permute-start(f32[3,4,24,768]{3,2,1,0:T(8,128)S(1)} %copy-done), channel_id=1, source_target_pairs={{16,0},{32,16},{48,32},{64,48},{80,64},{96,80},{112,96},{128,112},... | collective-permute-start | bytes 2654216 | tf_op jit(solution)/shard_map/ppermute | solution.py:52
  21.3 17.0 %collective-permute-done = f32[3,4,24,768]{3,2,1,0:T(8,128)S(1)} collective-permute-done((f32[3,4,24,768]{3,2,1,0:T(8,128)S(1)}, f32[3,4,24,768]{3,2,1,0:T(8,128)S(1)}, u32[]{:S(2)}, u32[]{:S(2)}) %collective-permute-start) | collective-permute-done | bytes 884768 | tf_op jit(solution)/shard_map/ppermute | solution.py:51
  38.4 7.2 %collective-permute-done.1 = f32[3,4,24,768]{3,2,1,0:T(8,128)} collective-permute-done((f32[3,4,24,768]{3,2,1,0:T(8,128)S(1)}, f32[3,4,24,768]{3,2,1,0:T(8,128)}, u32[]{:S(2)}, u32[]{:S(2)}) %collective-permute-start.1) | collective-permute-done | bytes 884768 | tf_op jit(solution)/shard_map/ppermute | solution.py:52
  45.6 0.1 fusion.10
  45.7 1.8 %fusion.2 = f32[384,144]{1,0:T(8,128)} fusion(f32[384,384]{1,0:T(8,128)S(1)} %select_add_fusion, f32[384,48]{1,0:T(8,128)S(1)} %get-tuple-element.25, f32[384,48]{1,0:T(8,128)S(1)} %get-tuple-element.26, f32[384,48]{1,0:T(8,128)S(1)} %get-tuple-element.24), kind=kOutput, calls=%fused_computation.14 | convolution fusion | flops 254914560 | bytes 1032192 | tf_op jit(solution)/shard_map/dot_general | solution.py:194
  47.5 0.7 collective-permute-start.2
  48.2 6.5 %fusion.11 = f32[288,1536]{1,0:T(8,128)S(1)} fusion(f32[288,768]{1,0:T(8,128)S(1)} %bitcast.15, f32[768,1536]{1,0:T(8,128)} %constant.40.clone), kind=kOutput, calls=%fused_computation.32 | convolution fusion | flops 4076863488 | bytes 7372800 | tf_op jit(solution)/shard_map/dot_general | solution.py:199
  54.8 1.0 fusion.9
  55.8 6.4 %shard_map.114.w_ref = f32[384,576]{1,0:T(8,128)} custom-call(f32[384,576]{1,0:T(8,128)} %bitcast.17, f32[384,384]{1,0:T(8,128)} %f_ref.1, f32[384,384]{1,0:T(8,128)} %s_ref.1), custom_call_target="tpu_custom_call" | custom-call | tf_op jit(solution)/shard_map/pallas_call | solution.py:114
  62.2 1.0 negate_add_fusion
  63.3 0.8 copy-done.7
  64.0 2.6 %shard_map.115 = f32[384,576]{1,0:T(8,128)} custom-call(s32[1]{0:T(128)} %bitcast.7.inlet_ref, f32[384,576]{1,0:T(8,128)} %shard_map.114.w_ref, f32[384,576]{1,0:T(8,128)} %bitcast.18, f32[384,144]{1,0:T(8,128)} %copy-done.7, f32[1,576]{1,0:T(1,128)} %constant.41.clone.g_ref, f32[1,576]{1,0:T(1,128)} %constant.42.clone.b_ref), custom_call_target="tpu_custom_call", output_to_operand_aliasing={{}: (1, {})} | custom-call | tf_op jit(solution)/shard_map/pallas_call | solution.py:146
  66.7 8.2 %all-to-all-start.1 = ((f32[16,24,576]{2,1,0:T(8,128)}), f32[16,24,576]{2,1,0:T(8,128)S(1)}, u32[]{:S(2)}, u32[]{:S(2)}) async-start(f32[16,24,576]{2,1,0:T(8,128)} %bitcast.19), calls=%async_computation.1 | async-start | bytes 1966080 | tf_op jit(solution)/shard_map/all_to_all | solution.py:212
  74.9 1.3 %broadcast_select_fusion = (f32[3,4,24,768]{3,2,1,0:T(8,128)S(1)}, f32[3,8,24,768]{3,2,1,0:T(8,128)S(1)}) fusion(f32[3,4,24,768]{3,2,1,0:T(8,128)} %collective-permute-done.1, f32[3,24,768]{2,1,0:T(8,128)S(1)} %slice_bitcast_fusion.2, pred[]{:T(512)S(6)} %eq.54, f32[3,4,24,768]{3,2,1,0:T(8,128)S(1)} %copy-done.6), kind=kLoop, calls=%fused_computation.13 | loop fusion | flops 221183 | bytes 3760129 | tf_op jit(solution)/shard_map/jit(_where)/select_n | solution.py:60
  76.3 1.1 %copy-done.4 = f32[3,4,24,768]{3,2,1,0:T(8,128)S(1)} copy-done((f32[3,4,24,768]{3,2,1,0:T(8,128)S(1)}, f32[3,4,24,768]{3,2,1,0:T(8,128)}, u32[]{:S(2)}) %copy-start.4) | copy-done | bytes 884760
  77.4 1.9 %add_add_fusion.t_ref = f32[3,4,24,768]{3,2,1,0:T(8,128)} fusion(f32[3,4,24,768]{3,2,1,0:T(8,128)S(1)} %copy-done.4, f32[3,4,24,768]{3,2,1,0:T(8,128)S(1)} %get-tuple-element.27, f32[3,4,24,768]{3,2,1,0:T(8,128)S(1)} %copy-done.6, f32[3,4,24,768]{3,2,1,0:T(8,128)S(1)} %copy-done, f32[3,8,24,768]{3,2,1,0:T(8,128)S(1)} %constant_dynamic-update-slice_fusion, ...), kind=kLoop, calls=%fused_computation.8 | loop fusion | flops 7077888 | bytes 7372800 | tf_op jit(solution)/shard_map/add | solution.py:214
  79.3 22.2 %all-to-all-done.1.b_ref = f32[16,24,576]{2,1,0:T(8,128)S(1)} async-done(((f32[16,24,576]{2,1,0:T(8,128)}), f32[16,24,576]{2,1,0:T(8,128)S(1)}, u32[]{:S(2)}, u32[]{:S(2)}) %all-to-all-start.1) | async-done | bytes 884768 | tf_op jit(solution)/shard_map/all_to_all | solution.py:212
  101.5 1.0 copy-done.2
  102.4 3.9 %shard_map.116 = (f32[3,4,24,768]{3,2,1,0:T(8,128)}, f32[3,4,24,768]{3,2,1,0:T(8,128)}) custom-call(f32[3,4,24,768]{3,2,1,0:T(8,128)} %v_ref.3, f32[3,4,24,768]{3,2,1,0:T(8,128)} %a_ref.1, f32[3,4,24,768]{3,2,1,0:T(8,128)} %add_add_fusion.t_ref, f32[16,24,576]{2,1,0:T(8,128)} %copy-done.2), custom_call_target="tpu_custom_call" | custom-call | tf_op jit(solution)/shard_map/pallas_call | solution.py:170
  (27 shorter events, 0.2 us)
Async XLA Ops:
  0.6 14.4 %copy-start = (f32[3,4,24,768]{3,2,1,0:T(8,128)S(1)}, f32[3,4,24,768]{3,2,1,0:T(8,128)}, u32[]{:S(2)}) copy-start(f32[3,4,24,768]{3,2,1,0:T(8,128)} %v_ref.3) | copy-start | bytes 2654212
  0.6 14.0 %copy-start.9 = (s32[384]{0:T(512)S(1)}, s32[384]{0:T(512)}, u32[]{:S(2)}) copy-start(s32[384]{0:T(512)} %param.15) | copy-start | bytes 4612
  0.7 14.0 %copy-start.10 = (f32[64]{0:T(128)S(1)}, f32[64]{0:T(128)}, u32[]{:S(2)}) copy-start(f32[64]{0:T(128)} %param.16) | copy-start | bytes 772
  0.7 14.1 %copy-start.8 = (s32[384]{0:T(512)S(1)}, s32[384]{0:T(512)}, u32[]{:S(2)}) copy-start(s32[384]{0:T(512)} %param.14) | copy-start | bytes 4612
  3.6 42.0 %all-to-all-start = ((f32[16,24,576]{2,1,0:T(8,128)}), f32[16,24,576]{2,1,0:T(8,128)S(1)}, u32[]{:S(2)}, u32[]{:S(2)}) async-start(f32[16,24,576]{2,1,0:T(8,128)} %shard_map.113), calls=%async_computation | async-start | bytes 1966080 | tf_op jit(solution)/shard_map/all_to_all | solution.py:183
  15.0 23.3 %collective-permute-start = (f32[3,4,24,768]{3,2,1,0:T(8,128)S(1)}, f32[3,4,24,768]{3,2,1,0:T(8,128)S(1)}, u32[]{:S(2)}, u32[]{:S(2)}) collective-permute-start(f32[3,4,24,768]{3,2,1,0:T(8,128)S(1)} %copy-done), channel_id=1, source_target_pairs={{0,16},{16,32},{32,48},{48,64},{64,80},{80,96},{96,112},{112,128},... | collective-permute-start | bytes 2654216 | tf_op jit(solution)/shard_map/ppermute | solution.py:51
  19.4 26.2 %collective-permute-start.1 = (f32[3,4,24,768]{3,2,1,0:T(8,128)S(1)}, f32[3,4,24,768]{3,2,1,0:T(8,128)}, u32[]{:S(2)}, u32[]{:S(2)}) collective-permute-start(f32[3,4,24,768]{3,2,1,0:T(8,128)S(1)} %copy-done), channel_id=1, source_target_pairs={{16,0},{32,16},{48,32},{64,48},{80,64},{96,80},{112,96},{128,112},... | collective-permute-start | bytes 2654216 | tf_op jit(solution)/shard_map/ppermute | solution.py:52
  38.4 9.8 %copy-start.5 = (f32[3,4,24,768]{3,2,1,0:T(8,128)}, f32[3,4,24,768]{3,2,1,0:T(8,128)S(1)}, u32[]{:S(2)}) copy-start(f32[3,4,24,768]{3,2,1,0:T(8,128)S(1)} %collective-permute-done) | copy-start | bytes 2654212
  45.6 9.2 %copy-start.1 = (f32[16,24,576]{2,1,0:T(8,128)}, f32[16,24,576]{2,1,0:T(8,128)S(1)}, u32[]{:S(2)}) copy-start(f32[16,24,576]{2,1,0:T(8,128)S(1)} %all-to-all-done) | copy-start | bytes 2654212
  47.5 15.8 %collective-permute-start.2 = (f32[384,144]{1,0:T(8,128)}, f32[384,144]{1,0:T(8,128)S(1)}, u32[]{:S(2)}, u32[]{:S(2)}) collective-permute-start(f32[384,144]{1,0:T(8,128)} %fusion.2), channel_id=1, source_target_pairs={{496,0},{497,1},{498,2},{499,3},{500,4},{501,5},{502,6},{503,7},{5... | collective-permute-start | bytes 663560 | tf_op jit(solution)/shard_map/ppermute | solution.py:195
  55.8 6.5 %copy-start.3 = (f32[288,768]{1,0:T(8,128)S(1)}, f32[288,768]{1,0:T(8,128)}, u32[]{:S(2)}) copy-start(f32[288,768]{1,0:T(8,128)} %get-tuple-element.23) | copy-start | bytes 2654212
  63.3 0.8 copy-start.7
  66.7 8.2 %copy-start.6 = (f32[3,4,24,768]{3,2,1,0:T(8,128)S(1)}, f32[3,4,24,768]{3,2,1,0:T(8,128)}, u32[]{:S(2)}) copy-start(f32[3,4,24,768]{3,2,1,0:T(8,128)} %copy-done.5) | copy-start | bytes 2654212
  66.7 34.8 %all-to-all-start.1 = ((f32[16,24,576]{2,1,0:T(8,128)}), f32[16,24,576]{2,1,0:T(8,128)S(1)}, u32[]{:S(2)}, u32[]{:S(2)}) async-start(f32[16,24,576]{2,1,0:T(8,128)} %bitcast.19), calls=%async_computation.1 | async-start | bytes 1966080 | tf_op jit(solution)/shard_map/all_to_all | solution.py:212
  76.2 1.2 %copy-start.4 = (f32[3,4,24,768]{3,2,1,0:T(8,128)S(1)}, f32[3,4,24,768]{3,2,1,0:T(8,128)}, u32[]{:S(2)}) copy-start(f32[3,4,24,768]{3,2,1,0:T(8,128)} %negate_add_fusion) | copy-start | bytes 2654212
  101.5 1.0 copy-start.2

commit v12 on v10

--- a/solution.py
+++ b/solution.py
@@ -156,18 +156,19 @@
     parts = back.shape[0]
     share = span // parts
 
-    def kernel(v_ref, a_ref, t_ref, b_ref, nv_ref, na_ref):
+    partial = keep_rate * accumulated + step_size * local_terms
+
+    def kernel(v_ref, p_ref, b_ref, nv_ref, na_ref):
         for c in range(comps):
             for x in range(planes):
                 k = (c * planes + x) * share
                 wall = jnp.concatenate([b_ref[d, :, k : k + share] for d in range(parts)], axis=1)
-                tendency = t_ref[c, x] + wall
-                acc = keep_rate * a_ref[c, x] + step_size * tendency
+                acc = p_ref[c, x] + step_size * wall
                 na_ref[c, x] = acc
                 nv_ref[c, x] = v_ref[c, x] + update_rate * acc
 
     shape = jax.ShapeDtypeStruct(velocity.shape, jnp.float32)
-    return pl.pallas_call(kernel, out_shape=(shape, shape))(velocity, accumulated, local_terms, back)
+    return pl.pallas_call(kernel, out_shape=(shape, shape))(velocity, partial, back)
 
 
 def shards(

time: 100 us -> 100 us (level)
    unnamed x17 -> x19, local copies, waits for them, and re-layouts: 2.22 us -> 2.21 us
where the time goes in v12:
time: 100 us; the launch traced here: 99.6 us
  waiting for transfers between devices  43.3 us (43%)
  starting transfers between devices  24.1 us (24%)
  Pallas kernels  15.8 us (16%)
  matrix products  7.55 us (8%)
  other arithmetic  5.56 us (6%)
  local copies, waits for them, and re-layouts  2.45 us (2%)
    ppermute x1, waiting for transfers between devices, halo_planes(): ahead = lax.ppermute(field, 'gx', [(i + 1, i) for i in range(count - 1)])  23.1 us
    all_to_all x1, waiting for transfers between devices, shards(): cols = lax.all_to_all(send, 'ga', 0, 0, tiled=True).reshape(rows, width)  20.1 us
    all_to_all x1, starting transfers between devices, shards(): cols = lax.all_to_all(send, 'ga', 0, 0, tiled=True).reshape(rows, width)  10.4 us
    dot_general x1, matrix products, shards(): jnp.dot(lines, jnp.asarray(spanwise_table(span)), precision=HIGHEST, pref...  6.53 us
    pallas_call x1, Pallas kernels, wall_block(): pl.pallas_call(kernel, out_shape=jax.ShapeDtypeStruct((rows, width), jnp....  6.47 us
    all_to_all x1, starting transfers between devices, shards(): lax.all_to_all(wall.reshape(parts, rows_here, width), 'ga', 0, 0, tiled=T...  4.86 us
    ppermute x1, starting transfers between devices, halo_planes(): behind = lax.ppermute(field, 'gx', [(i, i + 1) for i in range(count - 1)])  4.61 us
    pallas_call x1, Pallas kernels, combine(): pl.pallas_call(kernel, out_shape=(shape, shape))(velocity, partial, back)  3.67 us
  transfers between devices with their start and end apart: 5, of which 2 were waited for; matrix products, arithmetic and copies ran while one was open for 15% of the time, Pallas kernels for 9%

profile of v12, /device:TPU:30, one launch (start us, length us, event | category | flops | bytes accessed | tf_op | source)
XLA Modules:
  0.0 99.6 jit_solution(4533620827002709960)
XLA Ops:
  0.6 0.0 copy-start
  0.7 3.0 %shard_map.113 = f32[16,24,576]{2,1,0:T(8,128)} custom-call(f32[3,4,24,768]{3,2,1,0:T(8,128)} %v_ref.3), custom_call_target="tpu_custom_call" | custom-call | tf_op jit(solution)/shard_map/pallas_call | solution.py:94
  3.6 10.4 %all-to-all-start = ((f32[16,24,576]{2,1,0:T(8,128)}), f32[16,24,576]{2,1,0:T(8,128)S(1)}, u32[]{:S(2)}, u32[]{:S(2)}) async-start(f32[16,24,576]{2,1,0:T(8,128)} %shard_map.113), calls=%async_computation | async-start | bytes 1966080 | tf_op jit(solution)/shard_map/all_to_all | solution.py:184
  14.1 0.1 select_reduce_fusion
  14.2 0.3 select_add_fusion
  14.5 4.6 %collective-permute-start.2 = (f32[3,4,24,768]{3,2,1,0:T(8,128)S(1)}, f32[3,4,24,768]{3,2,1,0:T(8,128)}, u32[]{:S(2)}, u32[]{:S(2)}) collective-permute-start(f32[3,4,24,768]{3,2,1,0:T(8,128)S(1)} %copy-done), channel_id=1, source_target_pairs={{0,16},{16,32},{32,48},{48,64},{64,80},{80,96},{96,112},{112,128},... | collective-permute-start | bytes 2654216 | tf_op jit(solution)/shard_map/ppermute | solution.py:51
  19.1 20.1 %all-to-all-done = f32[16,24,576]{2,1,0:T(8,128)S(1)} async-done(((f32[16,24,576]{2,1,0:T(8,128)}), f32[16,24,576]{2,1,0:T(8,128)S(1)}, u32[]{:S(2)}, u32[]{:S(2)}) %all-to-all-start) | async-done | bytes 884768 | tf_op jit(solution)/shard_map/all_to_all | solution.py:184
  39.3 0.1 fusion.10
  39.4 1.0 %fusion.2 = f32[384,144]{1,0:T(8,128)S(1)} fusion(f32[384,384]{1,0:T(8,128)S(1)} %select_add_fusion, f32[384,48]{1,0:T(8,128)S(1)} %get-tuple-element.21, f32[384,48]{1,0:T(8,128)S(1)} %get-tuple-element.22, f32[384,48]{1,0:T(8,128)S(1)} %get-tuple-element.20), kind=kOutput, calls=%fused_computation.14 | convolution fusion | flops 254914560 | bytes 1032192 | tf_op jit(solution)/shard_map/dot_general | solution.py:195
  40.4 1.4 %collective-permute-start = (f32[384,144]{1,0:T(8,128)S(1)}, f32[384,144]{1,0:T(8,128)}, u32[]{:S(2)}, u32[]{:S(2)}) collective-permute-start(f32[384,144]{1,0:T(8,128)S(1)} %fusion.2), channel_id=1, source_target_pairs={{496,0},{497,1},{498,2},{499,3},{500,4},{501,5},{502,6},{503,7},{5... | collective-permute-start | bytes 663560 | tf_op jit(solution)/shard_map/ppermute | solution.py:196
  41.9 6.5 %fusion.11 = f32[288,1536]{1,0:T(8,128)S(1)} fusion(f32[288,768]{1,0:T(8,128)S(1)} %bitcast.15, f32[768,1536]{1,0:T(8,128)} %constant.42.clone), kind=kOutput, calls=%fused_computation.32 | convolution fusion | flops 4076863488 | bytes 7372800 | tf_op jit(solution)/shard_map/dot_general | solution.py:200
  48.4 1.0 %fusion.9 = (f32[288,768]{1,0:T(8,128)S(1)}, f32[288,768]{1,0:T(8,128)}) fusion(f32[288,1536]{1,0:T(8,128)S(1)} %fusion.11), kind=kLoop, calls=%fused_computation.30 | loop fusion | flops 221184 | bytes 3538944 | tf_op jit(solution)/shard_map/slice | solution.py:206
  49.4 6.5 %shard_map.114.w_ref = f32[384,576]{1,0:T(8,128)} custom-call(f32[384,576]{1,0:T(8,128)} %bitcast.17, f32[384,384]{1,0:T(8,128)} %f_ref.1, f32[384,384]{1,0:T(8,128)} %s_ref.1), custom_call_target="tpu_custom_call" | custom-call | tf_op jit(solution)/shard_map/pallas_call | solution.py:114
  55.9 1.0 %negate_add_fusion = f32[3,4,24,768]{3,2,1,0:T(8,128)} fusion(f32[3,4,24,768]{3,2,1,0:T(8,128)S(1)} %bitcast.21, f32[3,4,24,768]{3,2,1,0:T(8,128)S(1)} %bitcast.20, f32[4,24,768]{2,1,0:T(8,128)S(1)} %slice_bitcast_fusion.1), kind=kLoop, calls=%fused_computation.9 | loop fusion | flops 663552 | bytes 2949120 | tf_op jit(solution)/shard_map/add | solution.py:208
  57.0 2.7 %shard_map.115 = f32[384,576]{1,0:T(8,128)} custom-call(s32[1]{0:T(128)} %bitcast.7.inlet_ref, f32[384,576]{1,0:T(8,128)} %shard_map.114.w_ref, f32[384,576]{1,0:T(8,128)} %bitcast.18, f32[384,144]{1,0:T(8,128)} %collective-permute-done.f_ref, f32[1,576]{1,0:T(1,128)} %constant.43.clone.g_ref, ...), custom_call_target="tpu_custom_call", output_to_operand_aliasing={{}: (1, {})} | custom-call | tf_op jit(solution)/shard_map/pallas_call | solution.py:146
  59.6 4.9 %all-to-all-start.1 = ((f32[16,24,576]{2,1,0:T(8,128)}), f32[16,24,576]{2,1,0:T(8,128)S(1)}, u32[]{:S(2)}, u32[]{:S(2)}) async-start(f32[16,24,576]{2,1,0:T(8,128)} %bitcast.19), calls=%async_computation.1 | async-start | bytes 1966080 | tf_op jit(solution)/shard_map/all_to_all | solution.py:213
  64.5 2.7 %collective-permute-start.1 = (f32[3,4,24,768]{3,2,1,0:T(8,128)S(1)}, f32[3,4,24,768]{3,2,1,0:T(8,128)S(1)}, u32[]{:S(2)}, u32[]{:S(2)}) collective-permute-start(f32[3,4,24,768]{3,2,1,0:T(8,128)S(1)} %copy-done), channel_id=1, source_target_pairs={{16,0},{32,16},{48,32},{64,48},{80,64},{96,80},{112,96},{128,112},... | collective-permute-start | bytes 2654216 | tf_op jit(solution)/shard_map/ppermute | solution.py:52
  67.3 1.2 %constant_dynamic-update-slice_fusion.1 = f32[3,8,24,768]{3,2,1,0:T(8,128)S(1)} fusion(f32[3,4,24,768]{3,2,1,0:T(8,128)} %collective-permute-done.2), kind=kLoop, calls=%fused_computation.26 | loop fusion | bytes 1769472
  68.6 0.1 constant_dynamic-update-slice_fusion
  68.6 23.1 %collective-permute-done.1 = f32[3,4,24,768]{3,2,1,0:T(8,128)S(1)} collective-permute-done((f32[3,4,24,768]{3,2,1,0:T(8,128)S(1)}, f32[3,4,24,768]{3,2,1,0:T(8,128)S(1)}, u32[]{:S(2)}, u32[]{:S(2)}) %collective-permute-start.1) | collective-permute-done | bytes 884768 | tf_op jit(solution)/shard_map/ppermute | solution.py:52
  91.8 0.1 broadcast_select_fusion
  91.9 3.1 %multiply_add_fusion.p_ref = f32[3,4,24,768]{3,2,1,0:T(8,128)} fusion(f32[3,4,24,768]{3,2,1,0:T(8,128)S(1)} %copy-done.4, f32[3,4,24,768]{3,2,1,0:T(8,128)S(1)} %broadcast_select_fusion, f32[3,4,24,768]{3,2,1,0:T(8,128)} %collective-permute-done.2, f32[3,4,24,768]{3,2,1,0:T(8,128)S(1)} %copy-done, f32[3,8,24,768]{3,2,1,0:T(8,128)S(1)} %constant_dynamic-update-slice_fusion, ...), kind=kLoop, calls=%fused_computation.8 | loop fusion | flops 7741440 | bytes 8257536 | tf_op jit(solution)/shard_map/add | solution.py:159
  94.9 0.9 copy-done.2
  95.9 3.7 %shard_map.116 = (f32[3,4,24,768]{3,2,1,0:T(8,128)}, f32[3,4,24,768]{3,2,1,0:T(8,128)}) custom-call(f32[3,4,24,768]{3,2,1,0:T(8,128)} %v_ref.3, f32[3,4,24,768]{3,2,1,0:T(8,128)} %multiply_add_fusion.p_ref, f32[16,24,576]{2,1,0:T(8,128)} %copy-done.2), custom_call_target="tpu_custom_call" | custom-call | tf_op jit(solution)/shard_map/pallas_call | solution.py:171
  (24 shorter events, 0.1 us)
Async XLA Ops:
  0.6 13.9 %copy-start = (f32[3,4,24,768]{3,2,1,0:T(8,128)S(1)}, f32[3,4,24,768]{3,2,1,0:T(8,128)}, u32[]{:S(2)}) copy-start(f32[3,4,24,768]{3,2,1,0:T(8,128)} %v_ref.3) | copy-start | bytes 2654212
  0.6 13.4 %copy-start.7 = (s32[384]{0:T(512)S(1)}, s32[384]{0:T(512)}, u32[]{:S(2)}) copy-start(s32[384]{0:T(512)} %param.15) | copy-start | bytes 4612
  0.7 13.4 %copy-start.8 = (f32[64]{0:T(128)S(1)}, f32[64]{0:T(128)}, u32[]{:S(2)}) copy-start(f32[64]{0:T(128)} %param.16) | copy-start | bytes 772
  0.7 13.5 %copy-start.6 = (s32[384]{0:T(512)S(1)}, s32[384]{0:T(512)}, u32[]{:S(2)}) copy-start(s32[384]{0:T(512)} %param.14) | copy-start | bytes 4612
  3.6 35.6 %all-to-all-start = ((f32[16,24,576]{2,1,0:T(8,128)}), f32[16,24,576]{2,1,0:T(8,128)S(1)}, u32[]{:S(2)}, u32[]{:S(2)}) async-start(f32[16,24,576]{2,1,0:T(8,128)} %shard_map.113), calls=%async_computation | async-start | bytes 1966080 | tf_op jit(solution)/shard_map/all_to_all | solution.py:184
  14.5 52.8 %collective-permute-start.2 = (f32[3,4,24,768]{3,2,1,0:T(8,128)S(1)}, f32[3,4,24,768]{3,2,1,0:T(8,128)}, u32[]{:S(2)}, u32[]{:S(2)}) collective-permute-start(f32[3,4,24,768]{3,2,1,0:T(8,128)S(1)} %copy-done), channel_id=1, source_target_pairs={{0,16},{16,32},{32,48},{48,64},{64,80},{80,96},{96,112},{112,128},... | collective-permute-start | bytes 2654216 | tf_op jit(solution)/shard_map/ppermute | solution.py:51
  39.3 9.1 %copy-start.1 = (f32[16,24,576]{2,1,0:T(8,128)}, f32[16,24,576]{2,1,0:T(8,128)S(1)}, u32[]{:S(2)}) copy-start(f32[16,24,576]{2,1,0:T(8,128)S(1)} %all-to-all-done) | copy-start | bytes 2654212
  40.4 16.5 %collective-permute-start = (f32[384,144]{1,0:T(8,128)S(1)}, f32[384,144]{1,0:T(8,128)}, u32[]{:S(2)}, u32[]{:S(2)}) collective-permute-start(f32[384,144]{1,0:T(8,128)S(1)} %fusion.2), channel_id=1, source_target_pairs={{496,0},{497,1},{498,2},{499,3},{500,4},{501,5},{502,6},{503,7},{5... | collective-permute-start | bytes 663560 | tf_op jit(solution)/shard_map/ppermute | solution.py:196
  49.4 6.5 %copy-start.3 = (f32[288,768]{1,0:T(8,128)S(1)}, f32[288,768]{1,0:T(8,128)}, u32[]{:S(2)}) copy-start(f32[288,768]{1,0:T(8,128)} %get-tuple-element.19) | copy-start | bytes 2654212
  59.6 35.3 %all-to-all-start.1 = ((f32[16,24,576]{2,1,0:T(8,128)}), f32[16,24,576]{2,1,0:T(8,128)S(1)}, u32[]{:S(2)}, u32[]{:S(2)}) async-start(f32[16,24,576]{2,1,0:T(8,128)} %bitcast.19), calls=%async_computation.1 | async-start | bytes 1966080 | tf_op jit(solution)/shard_map/all_to_all | solution.py:213
  64.5 27.3 %collective-permute-start.1 = (f32[3,4,24,768]{3,2,1,0:T(8,128)S(1)}, f32[3,4,24,768]{3,2,1,0:T(8,128)S(1)}, u32[]{:S(2)}, u32[]{:S(2)}) collective-permute-start(f32[3,4,24,768]{3,2,1,0:T(8,128)S(1)} %copy-done), channel_id=1, source_target_pairs={{16,0},{32,16},{48,32},{64,48},{80,64},{96,80},{112,96},{128,112},... | collective-permute-start | bytes 2654216 | tf_op jit(solution)/shard_map/ppermute | solution.py:52
  68.5 23.3 %copy-start.4 = (f32[3,4,24,768]{3,2,1,0:T(8,128)S(1)}, f32[3,4,24,768]{3,2,1,0:T(8,128)}, u32[]{:S(2)}) copy-start(f32[3,4,24,768]{3,2,1,0:T(8,128)} %negate_add_fusion) | copy-start | bytes 2654212
  68.6 23.3 %copy-start.5 = (f32[3,4,24,768]{3,2,1,0:T(8,128)S(1)}, f32[3,4,24,768]{3,2,1,0:T(8,128)}, u32[]{:S(2)}) copy-start(f32[3,4,24,768]{3,2,1,0:T(8,128)} %param.11) | copy-start | bytes 2654212
  94.9 0.9 copy-start.2

commit v13 on v12

--- a/solution.py
+++ b/solution.py
@@ -200,7 +200,7 @@
     spectral = jnp.dot(
         lines,
         jnp.asarray(spanwise_table(span)),
-        precision=HIGHEST,
+        precision=lax.Precision.HIGH,
         preferred_element_type=jnp.float32,
     )
     span_first = spectral[:, :span].reshape(velocity.shape)

time: 100 us -> 98.4 us (0.984)
  the two profiles are of different devices: /device:TPU:30 before, /device:TPU:1 now
where the time goes in v13:
time: 98.4 us; the launch traced here: 97.8 us
  waiting for transfers between devices  43.5 us (44%)
  starting transfers between devices  23.2 us (24%)
  Pallas kernels  16.4 us (17%)
  matrix products  5.86 us (6%)
  other arithmetic  5.56 us (6%)
  local copies, waits for them, and re-layouts  2.45 us (2%)
    all_to_all x1, waiting for transfers between devices, shards(): cols = lax.all_to_all(send, 'ga', 0, 0, tiled=True).reshape(rows, width)  22.1 us
    ppermute x1, waiting for transfers between devices, halo_planes(): ahead = lax.ppermute(field, 'gx', [(i + 1, i) for i in range(count - 1)])  20.4 us
    all_to_all x1, starting transfers between devices, shards(): cols = lax.all_to_all(send, 'ga', 0, 0, tiled=True).reshape(rows, width)  11.8 us
    pallas_call x1, Pallas kernels, wall_block(): pl.pallas_call(kernel, out_shape=jax.ShapeDtypeStruct((rows, width), jnp....  6.48 us
    dot_general x1, matrix products, shards(): jnp.dot(lines, jnp.asarray(spanwise_table(span)), precision=lax.Precision...  4.84 us
    all_to_all x1, starting transfers between devices, shards(): lax.all_to_all(wall.reshape(parts, rows_here, width), 'ga', 0, 0, tiled=T...  4.73 us
    ppermute x1, starting transfers between devices, halo_planes(): behind = lax.ppermute(field, 'gx', [(i, i + 1) for i in range(count - 1)])  4.06 us
    pallas_call x1, Pallas kernels, combine(): pl.pallas_call(kernel, out_shape=(shape, shape))(velocity, partial, back)  3.67 us
  transfers between devices with their start and end apart: 5, of which 4 were waited for; matrix products, arithmetic and copies ran while one was open for 13% of the time, Pallas kernels for 10%

profile of v13, /device:TPU:1, one launch (start us, length us, event | category | flops | bytes accessed | tf_op | source)
XLA Modules:
  0.0 97.8 jit_solution(1795812623803529377)
XLA Ops:
  0.7 3.0 %shard_map.113 = f32[16,24,576]{2,1,0:T(8,128)} custom-call(f32[3,4,24,768]{3,2,1,0:T(8,128)} %v_ref.3), custom_call_target="tpu_custom_call" | custom-call | tf_op jit(solution)/shard_map/pallas_call | solution.py:94
  3.6 11.8 %all-to-all-start = ((f32[16,24,576]{2,1,0:T(8,128)}), f32[16,24,576]{2,1,0:T(8,128)S(1)}, u32[]{:S(2)}, u32[]{:S(2)}) async-start(f32[16,24,576]{2,1,0:T(8,128)} %shard_map.113), calls=%async_computation | async-start | bytes 1966080 | tf_op jit(solution)/shard_map/all_to_all | solution.py:184
  15.5 0.1 select_reduce_fusion
  15.6 0.3 select_add_fusion
  15.9 4.1 %collective-permute-start.2 = (f32[3,4,24,768]{3,2,1,0:T(8,128)S(1)}, f32[3,4,24,768]{3,2,1,0:T(8,128)}, u32[]{:S(2)}, u32[]{:S(2)}) collective-permute-start(f32[3,4,24,768]{3,2,1,0:T(8,128)S(1)} %copy-done), channel_id=1, source_target_pairs={{0,16},{16,32},{32,48},{48,64},{64,80},{80,96},{96,112},{112,128},... | collective-permute-start | bytes 2654216 | tf_op jit(solution)/shard_map/ppermute | solution.py:51
  20.0 22.1 %all-to-all-done = f32[16,24,576]{2,1,0:T(8,128)S(1)} async-done(((f32[16,24,576]{2,1,0:T(8,128)}), f32[16,24,576]{2,1,0:T(8,128)S(1)}, u32[]{:S(2)}, u32[]{:S(2)}) %all-to-all-start) | async-done | bytes 884768 | tf_op jit(solution)/shard_map/all_to_all | solution.py:184
  42.1 0.1 fusion.10
  42.2 1.0 %fusion.2 = f32[384,144]{1,0:T(8,128)S(1)} fusion(f32[384,384]{1,0:T(8,128)S(1)} %select_add_fusion, f32[384,48]{1,0:T(8,128)S(1)} %get-tuple-element.21, f32[384,48]{1,0:T(8,128)S(1)} %get-tuple-element.22, f32[384,48]{1,0:T(8,128)S(1)} %get-tuple-element.20), kind=kOutput, calls=%fused_computation.14 | convolution fusion | flops 254914560 | bytes 1032192 | tf_op jit(solution)/shard_map/dot_general | solution.py:195
  43.2 1.3 %collective-permute-start = (f32[384,144]{1,0:T(8,128)S(1)}, f32[384,144]{1,0:T(8,128)}, u32[]{:S(2)}, u32[]{:S(2)}) collective-permute-start(f32[384,144]{1,0:T(8,128)S(1)} %fusion.2), channel_id=1, source_target_pairs={{496,0},{497,1},{498,2},{499,3},{500,4},{501,5},{502,6},{503,7},{5... | collective-permute-start | bytes 663560 | tf_op jit(solution)/shard_map/ppermute | solution.py:196
  44.6 4.8 %fusion.11 = f32[288,1536]{1,0:T(8,128)S(1)} fusion(f32[288,768]{1,0:T(8,128)S(1)} %bitcast.15, f32[768,1536]{1,0:T(8,128)} %constant.42.clone), kind=kOutput, calls=%fused_computation.32 | convolution fusion | flops 2038431744 | bytes 7372800 | tf_op jit(solution)/shard_map/dot_general | solution.py:200
  49.4 1.0 %fusion.9 = (f32[288,768]{1,0:T(8,128)S(1)}, f32[288,768]{1,0:T(8,128)}) fusion(f32[288,1536]{1,0:T(8,128)S(1)} %fusion.11), kind=kLoop, calls=%fused_computation.30 | loop fusion | flops 221184 | bytes 3538944 | tf_op jit(solution)/shard_map/slice | solution.py:206
  50.5 6.5 %shard_map.114.w_ref = f32[384,576]{1,0:T(8,128)} custom-call(f32[384,576]{1,0:T(8,128)} %bitcast.17, f32[384,384]{1,0:T(8,128)} %f_ref.1, f32[384,384]{1,0:T(8,128)} %s_ref.1), custom_call_target="tpu_custom_call" | custom-call | tf_op jit(solution)/shard_map/pallas_call | solution.py:114
  56.9 1.0 %negate_add_fusion = f32[3,4,24,768]{3,2,1,0:T(8,128)} fusion(f32[3,4,24,768]{3,2,1,0:T(8,128)S(1)} %bitcast.21, f32[3,4,24,768]{3,2,1,0:T(8,128)S(1)} %bitcast.20, f32[4,24,768]{2,1,0:T(8,128)S(1)} %slice_bitcast_fusion.1), kind=kLoop, calls=%fused_computation.9 | loop fusion | flops 663552 | bytes 2949120 | tf_op jit(solution)/shard_map/add | solution.py:208
  58.0 0.6 collective-permute-done.f_ref
  58.6 3.3 %shard_map.115 = f32[384,576]{1,0:T(8,128)} custom-call(s32[1]{0:T(128)} %bitcast.7.inlet_ref, f32[384,576]{1,0:T(8,128)} %shard_map.114.w_ref, f32[384,576]{1,0:T(8,128)} %bitcast.18, f32[384,144]{1,0:T(8,128)} %collective-permute-done.f_ref, f32[1,576]{1,0:T(1,128)} %constant.43.clone.g_ref, ...), custom_call_target="tpu_custom_call", output_to_operand_aliasing={{}: (1, {})} | custom-call | tf_op jit(solution)/shard_map/pallas_call | solution.py:146
  61.8 4.7 %all-to-all-start.1 = ((f32[16,24,576]{2,1,0:T(8,128)}), f32[16,24,576]{2,1,0:T(8,128)S(1)}, u32[]{:S(2)}, u32[]{:S(2)}) async-start(f32[16,24,576]{2,1,0:T(8,128)} %bitcast.19), calls=%async_computation.1 | async-start | bytes 1966080 | tf_op jit(solution)/shard_map/all_to_all | solution.py:213
  66.6 1.3 %collective-permute-start.1 = (f32[3,4,24,768]{3,2,1,0:T(8,128)S(1)}, f32[3,4,24,768]{3,2,1,0:T(8,128)S(1)}, u32[]{:S(2)}, u32[]{:S(2)}) collective-permute-start(f32[3,4,24,768]{3,2,1,0:T(8,128)S(1)} %copy-done), channel_id=1, source_target_pairs={{16,0},{32,16},{48,32},{64,48},{80,64},{96,80},{112,96},{128,112},... | collective-permute-start | bytes 2654216 | tf_op jit(solution)/shard_map/ppermute | solution.py:52
  67.9 1.2 %constant_dynamic-update-slice_fusion.1 = f32[3,8,24,768]{3,2,1,0:T(8,128)S(1)} fusion(f32[3,4,24,768]{3,2,1,0:T(8,128)} %collective-permute-done.2), kind=kLoop, calls=%fused_computation.26 | loop fusion | bytes 1769472
  69.3 20.4 %collective-permute-done.1 = f32[3,4,24,768]{3,2,1,0:T(8,128)S(1)} collective-permute-done((f32[3,4,24,768]{3,2,1,0:T(8,128)S(1)}, f32[3,4,24,768]{3,2,1,0:T(8,128)S(1)}, u32[]{:S(2)}, u32[]{:S(2)}) %collective-permute-start.1) | collective-permute-done | bytes 884768 | tf_op jit(solution)/shard_map/ppermute | solution.py:52
  89.7 0.1 broadcast_select_fusion
  89.8 3.1 %multiply_add_fusion.p_ref = f32[3,4,24,768]{3,2,1,0:T(8,128)} fusion(f32[3,4,24,768]{3,2,1,0:T(8,128)S(1)} %copy-done.4, f32[3,4,24,768]{3,2,1,0:T(8,128)S(1)} %broadcast_select_fusion, f32[3,4,24,768]{3,2,1,0:T(8,128)} %collective-permute-done.2, f32[3,4,24,768]{3,2,1,0:T(8,128)S(1)} %copy-done, f32[3,8,24,768]{3,2,1,0:T(8,128)S(1)} %constant_dynamic-update-slice_fusion, ...), kind=kLoop, calls=%fused_computation.8 | loop fusion | flops 7741440 | bytes 8257536 | tf_op jit(solution)/shard_map/add | solution.py:159
  92.8 0.3 all-to-all-done.1.b_ref
  93.2 0.9 copy-done.2
  94.1 3.7 %shard_map.116 = (f32[3,4,24,768]{3,2,1,0:T(8,128)}, f32[3,4,24,768]{3,2,1,0:T(8,128)}) custom-call(f32[3,4,24,768]{3,2,1,0:T(8,128)} %v_ref.3, f32[3,4,24,768]{3,2,1,0:T(8,128)} %multiply_add_fusion.p_ref, f32[16,24,576]{2,1,0:T(8,128)} %copy-done.2), custom_call_target="tpu_custom_call" | custom-call | tf_op jit(solution)/shard_map/pallas_call | solution.py:171
  (24 shorter events, 0.2 us)
Async XLA Ops:
  0.6 15.3 %copy-start = (f32[3,4,24,768]{3,2,1,0:T(8,128)S(1)}, f32[3,4,24,768]{3,2,1,0:T(8,128)}, u32[]{:S(2)}) copy-start(f32[3,4,24,768]{3,2,1,0:T(8,128)} %v_ref.3) | copy-start | bytes 2654212
  0.6 14.8 %copy-start.7 = (s32[384]{0:T(512)S(1)}, s32[384]{0:T(512)}, u32[]{:S(2)}) copy-start(s32[384]{0:T(512)} %param.15) | copy-start | bytes 4612
  0.7 14.8 %copy-start.8 = (f32[64]{0:T(128)S(1)}, f32[64]{0:T(128)}, u32[]{:S(2)}) copy-start(f32[64]{0:T(128)} %param.16) | copy-start | bytes 772
  0.7 14.9 %copy-start.6 = (s32[384]{0:T(512)S(1)}, s32[384]{0:T(512)}, u32[]{:S(2)}) copy-start(s32[384]{0:T(512)} %param.14) | copy-start | bytes 4612
  3.6 38.4 %all-to-all-start = ((f32[16,24,576]{2,1,0:T(8,128)}), f32[16,24,576]{2,1,0:T(8,128)S(1)}, u32[]{:S(2)}, u32[]{:S(2)}) async-start(f32[16,24,576]{2,1,0:T(8,128)} %shard_map.113), calls=%async_computation | async-start | bytes 1966080 | tf_op jit(solution)/shard_map/all_to_all | solution.py:184
  15.9 52.0 %collective-permute-start.2 = (f32[3,4,24,768]{3,2,1,0:T(8,128)S(1)}, f32[3,4,24,768]{3,2,1,0:T(8,128)}, u32[]{:S(2)}, u32[]{:S(2)}) collective-permute-start(f32[3,4,24,768]{3,2,1,0:T(8,128)S(1)} %copy-done), channel_id=1, source_target_pairs={{0,16},{16,32},{32,48},{48,64},{64,80},{80,96},{96,112},{112,128},... | collective-permute-start | bytes 2654216 | tf_op jit(solution)/shard_map/ppermute | solution.py:51
  42.1 7.3 %copy-start.1 = (f32[16,24,576]{2,1,0:T(8,128)}, f32[16,24,576]{2,1,0:T(8,128)S(1)}, u32[]{:S(2)}) copy-start(f32[16,24,576]{2,1,0:T(8,128)S(1)} %all-to-all-done) | copy-start | bytes 2654212
  43.2 15.3 %collective-permute-start = (f32[384,144]{1,0:T(8,128)S(1)}, f32[384,144]{1,0:T(8,128)}, u32[]{:S(2)}, u32[]{:S(2)}) collective-permute-start(f32[384,144]{1,0:T(8,128)S(1)} %fusion.2), channel_id=1, source_target_pairs={{496,0},{497,1},{498,2},{499,3},{500,4},{501,5},{502,6},{503,7},{5... | collective-permute-start | bytes 663560 | tf_op jit(solution)/shard_map/ppermute | solution.py:196
  50.5 6.5 %copy-start.3 = (f32[288,768]{1,0:T(8,128)S(1)}, f32[288,768]{1,0:T(8,128)}, u32[]{:S(2)}) copy-start(f32[288,768]{1,0:T(8,128)} %get-tuple-element.19) | copy-start | bytes 2654212
  61.8 31.3 %all-to-all-start.1 = ((f32[16,24,576]{2,1,0:T(8,128)}), f32[16,24,576]{2,1,0:T(8,128)S(1)}, u32[]{:S(2)}, u32[]{:S(2)}) async-start(f32[16,24,576]{2,1,0:T(8,128)} %bitcast.19), calls=%async_computation.1 | async-start | bytes 1966080 | tf_op jit(solution)/shard_map/all_to_all | solution.py:213
  66.6 23.1 %collective-permute-start.1 = (f32[3,4,24,768]{3,2,1,0:T(8,128)S(1)}, f32[3,4,24,768]{3,2,1,0:T(8,128)S(1)}, u32[]{:S(2)}, u32[]{:S(2)}) collective-permute-start(f32[3,4,24,768]{3,2,1,0:T(8,128)S(1)} %copy-done), channel_id=1, source_target_pairs={{16,0},{32,16},{48,32},{64,48},{80,64},{96,80},{112,96},{128,112},... | collective-permute-start | bytes 2654216 | tf_op jit(solution)/shard_map/ppermute | solution.py:52
  69.2 20.6 %copy-start.4 = (f32[3,4,24,768]{3,2,1,0:T(8,128)S(1)}, f32[3,4,24,768]{3,2,1,0:T(8,128)}, u32[]{:S(2)}) copy-start(f32[3,4,24,768]{3,2,1,0:T(8,128)} %negate_add_fusion) | copy-start | bytes 2654212
  69.2 20.6 %copy-start.5 = (f32[3,4,24,768]{3,2,1,0:T(8,128)S(1)}, f32[3,4,24,768]{3,2,1,0:T(8,128)}, u32[]{:S(2)}) copy-start(f32[3,4,24,768]{3,2,1,0:T(8,128)} %param.11) | copy-start | bytes 2654212
  93.2 0.9 copy-start.2

commit v14 on v13

--- a/solution.py
+++ b/solution.py
@@ -209,7 +209,14 @@
     inflow, wall, span_terms = lax.optimization_barrier((inflow, wall, span_terms))
 
     inlet = (lax.axis_index("gx") == 0).astype(jnp.int32).reshape(1)
-    wall = add_ghost(wall, cols, inflow, inlet, planes)
+    lower, upper = ghost_weights(planes)
+    gain = jnp.asarray(np.tile(np.repeat(lower, share), comps)[None, :])
+    bias = jnp.asarray(np.tile(np.repeat(viscosity * upper, share), comps)[None, :])
+    flow = jnp.concatenate(
+        [inflow[:, c * share : (c + 1) * share] for c in range(comps) for x in range(planes)], axis=1
+    )
+    spread = jnp.concatenate([cols[:, 0 : planes * share]] * comps, axis=1)
+    wall = wall + jnp.where(inlet[0] > 0, flow * (spread * gain + bias), 0.0)
     back = lax.all_to_all(wall.reshape(parts, rows_here, width), "ga", 0, 0, tiled=True)
 
     local_terms = span_terms + streamwise(velocity, behind, ahead)

time: 98.4 us -> 104 us (1.057)
  local copies, waits for them, and re-layouts: 2.45 us -> 8.38 us
  Pallas kernels: 16.4 us -> 13 us
  other arithmetic: 5.56 us -> 7.2 us
    slice x0 -> x3, local copies, waits for them, and re-layouts: none -> 4.18 us  [the longest x2 3.26 us: shards(): inflow[:, c * share:(c + 1) * share]]
    pallas_call x1 -> x0, Pallas kernels: 3.29 us -> none  [add_ghost(): pl.pallas_call(kernel, out_shape=jax.ShapeDtypeStruct((rows, width), jnp....]
    add x0 -> x1, other arithmetic: none -> 2.5 us  [shards(): wall = wall + jnp.where(inlet[0] > 0, flow * (spread * gain + bias), 0.0)]
    concatenate x0 -> x1, local copies, waits for them, and re-layouts: none -> 1.72 us  [shards(): jnp.concatenate([inflow[:, c * share:(c + 1) * share] for c in range(comp...]
    unnamed x19 -> x23, local copies, waits for them, and re-layouts: 2.21 us -> 2.24 us
  transfers between devices with their start and end apart: 5 -> 5, of which waited for: 4 -> 4; matrix products, arithmetic and copies ran while one was open for 13% -> 20% of each run, Pallas kernels for 10% -> 6%
where the time goes in v14:
time: 104 us; the launch traced here: 103 us
  waiting for transfers between devices  44.5 us (43%)
  starting transfers between devices  23.2 us (22%)
  Pallas kernels  13 us (12%)
  local copies, waits for them, and re-layouts  8.38 us (8%)
  other arithmetic  7.2 us (7%)
  matrix products  5.86 us (6%)
    all_to_all x1, waiting for transfers between devices, shards(): cols = lax.all_to_all(send, 'ga', 0, 0, tiled=True).reshape(rows, width)  22.1 us
    ppermute x1, waiting for transfers between devices, halo_planes(): ahead = lax.ppermute(field, 'gx', [(i + 1, i) for i in range(count - 1)])  20.4 us
    all_to_all x1, starting transfers between devices, shards(): cols = lax.all_to_all(send, 'ga', 0, 0, tiled=True).reshape(rows, width)  11.8 us
    pallas_call x1, Pallas kernels, wall_block(): pl.pallas_call(kernel, out_shape=jax.ShapeDtypeStruct((rows, width), jnp....  6.35 us
    dot_general x1, matrix products, shards(): jnp.dot(lines, jnp.asarray(spanwise_table(span)), precision=lax.Precision...  4.84 us
    all_to_all x1, starting transfers between devices, shards(): lax.all_to_all(wall.reshape(parts, rows_here, width), 'ga', 0, 0, tiled=T...  4.73 us
    ppermute x1, starting transfers between devices, halo_planes(): behind = lax.ppermute(field, 'gx', [(i, i + 1) for i in range(count - 1)])  4.08 us
    pallas_call x1, Pallas kernels, combine(): pl.pallas_call(kernel, out_shape=(shape, shape))(velocity, partial, back)  3.67 us
  transfers between devices with their start and end apart: 5, of which 4 were waited for; matrix products, arithmetic and copies ran while one was open for 20% of the time, Pallas kernels for 6%

profile of v14, /device:TPU:1, one launch (start us, length us, event | category | flops | bytes accessed | tf_op | source)
XLA Modules:
  0.0 103.0 jit_solution(12727032472979004390)
XLA Ops:
  0.7 2.9 %shard_map.113 = f32[16,24,576]{2,1,0:T(8,128)} custom-call(f32[3,4,24,768]{3,2,1,0:T(8,128)} %v_ref.3), custom_call_target="tpu_custom_call" | custom-call | tf_op jit(solution)/shard_map/pallas_call | solution.py:94
  3.6 11.8 %all-to-all-start = ((f32[16,24,576]{2,1,0:T(8,128)}), f32[16,24,576]{2,1,0:T(8,128)S(1)}, u32[]{:S(2)}, u32[]{:S(2)}) async-start(f32[16,24,576]{2,1,0:T(8,128)} %shard_map.113), calls=%async_computation | async-start | bytes 1966080 | tf_op jit(solution)/shard_map/all_to_all | solution.py:184
  15.6 0.3 select_add_fusion
  15.9 4.1 %collective-permute-start.2 = (f32[3,4,24,768]{3,2,1,0:T(8,128)S(1)}, f32[3,4,24,768]{3,2,1,0:T(8,128)}, u32[]{:S(2)}, u32[]{:S(2)}) collective-permute-start(f32[3,4,24,768]{3,2,1,0:T(8,128)S(1)} %copy-done), channel_id=1, source_target_pairs={{0,16},{16,32},{32,48},{48,64},{64,80},{80,96},{96,112},{112,128},... | collective-permute-start | bytes 2654216 | tf_op jit(solution)/shard_map/ppermute | solution.py:51
  19.9 22.1 %all-to-all-done = f32[16,24,576]{2,1,0:T(8,128)S(1)} async-done(((f32[16,24,576]{2,1,0:T(8,128)}), f32[16,24,576]{2,1,0:T(8,128)S(1)}, u32[]{:S(2)}, u32[]{:S(2)}) %all-to-all-start) | async-done | bytes 884768 | tf_op jit(solution)/shard_map/all_to_all | solution.py:184
  42.2 0.9 slice.94
  43.1 1.0 fusion.6
  44.1 1.3 %collective-permute-start = (f32[384,144]{1,0:T(8,128)S(1)}, f32[384,144]{1,0:T(8,128)}, u32[]{:S(2)}, u32[]{:S(2)}) collective-permute-start(f32[384,144]{1,0:T(8,128)S(1)} %fusion.6), channel_id=1, source_target_pairs={{496,0},{497,1},{498,2},{499,3},{500,4},{501,5},{502,6},{503,7},{5... | collective-permute-start | bytes 663560 | tf_op jit(solution)/shard_map/ppermute | solution.py:196
  45.5 4.8 %fusion.17 = f32[288,1536]{1,0:T(8,128)S(1)} fusion(f32[288,768]{1,0:T(8,128)S(1)} %bitcast.14, f32[768,1536]{1,0:T(8,128)} %constant.42.clone), kind=kOutput, calls=%fused_computation.39 | convolution fusion | flops 2038431744 | bytes 7372800 | tf_op jit(solution)/shard_map/dot_general | solution.py:200
  50.4 6.4 %shard_map.114 = f32[384,576]{1,0:T(8,128)} custom-call(f32[384,576]{1,0:T(8,128)} %bitcast.17, f32[384,384]{1,0:T(8,128)} %f_ref.1, f32[384,384]{1,0:T(8,128)} %s_ref.1), custom_call_target="tpu_custom_call" | custom-call | tf_op jit(solution)/shard_map/pallas_call | solution.py:114
  56.8 1.0 negate_add_fusion
  57.8 1.6 %collective-permute-done = f32[384,144]{1,0:T(8,128)} collective-permute-done((f32[384,144]{1,0:T(8,128)S(1)}, f32[384,144]{1,0:T(8,128)}, u32[]{:S(2)}, u32[]{:S(2)}) %collective-permute-start) | collective-permute-done | bytes 221216 | tf_op jit(solution)/shard_map/ppermute | solution.py:196
  59.4 1.3 %fusion.15 = (f32[384,48]{1,0:T(8,128)S(1)}, f32[384,48]{1,0:T(8,128)S(1)}, f32[384,48]{1,0:T(8,128)S(1)}) fusion(f32[384,144]{1,0:T(8,128)} %collective-permute-done), kind=kLoop, calls=%fused_computation.37 | loop fusion | bytes 442368 | tf_op jit(solution)/shard_map/slice | solution.py:216
  60.8 1.9 %fusion.16 = (f32[384,96]{1,0:T(8,128)}, f32[384,96]{1,0:T(8,128)}) fusion(f32[384,144]{1,0:T(8,128)} %collective-permute-done), kind=kLoop, calls=%fused_computation.38 | loop fusion | bytes 589824 | tf_op jit(solution)/shard_map/slice | solution.py:216
  62.7 1.7 %concatenate.24 = f32[384,576]{1,0:T(8,128)S(1)} concatenate(f32[384,48]{1,0:T(8,128)S(1)} %get-tuple-element.25, f32[384,48]{1,0:T(8,128)S(1)} %get-tuple-element.25, f32[384,48]{1,0:T(8,128)S(1)} %get-tuple-element.25, f32[384,96]{1,0:T(8,128)} %get-tuple-element.27, f32[384,48]{1,0:T(8,128)S(1)} %get-tuple-element.24, f32[384,48]{1,0:T(8,128)S(1)} %get-tuple-element.24, ...), dimensions={1} | concatenate | bytes 1769472 | tf_op jit(solution)/shard_map/concatenate | solution.py:215
  64.5 2.5 %fusion.3 = f32[384,576]{1,0:T(8,128)} fusion(f32[384,576]{1,0:T(8,128)S(1)} %copy-done.2, f32[384,576]{1,0:T(8,128)S(1)} %concatenate.24, f32[384,192]{1,0:T(8,128)} %slice.94, f32[576]{0:T(1024)S(1)} %copy-done.8, f32[576]{0:T(1024)S(1)} %copy-done.7, pred[]{:T(512)S(6)} %gt.3), kind=kLoop, calls=%fused_computation.8 | loop fusion | flops 1548288 | bytes 2953729 | tf_op jit(solution)/shard_map/add | solution.py:219
  67.0 4.7 %all-to-all-start.1 = ((f32[16,24,576]{2,1,0:T(8,128)}), f32[16,24,576]{2,1,0:T(8,128)S(1)}, u32[]{:S(2)}, u32[]{:S(2)}) async-start(f32[16,24,576]{2,1,0:T(8,128)} %bitcast.7), calls=%async_computation.1 | async-start | bytes 1966080 | tf_op jit(solution)/shard_map/all_to_all | solution.py:220
  71.7 1.3 %collective-permute-start.1 = (f32[3,4,24,768]{3,2,1,0:T(8,128)S(1)}, f32[3,4,24,768]{3,2,1,0:T(8,128)S(1)}, u32[]{:S(2)}, u32[]{:S(2)}) collective-permute-start(f32[3,4,24,768]{3,2,1,0:T(8,128)S(1)} %copy-done), channel_id=1, source_target_pairs={{16,0},{32,16},{48,32},{64,48},{80,64},{96,80},{112,96},{128,112},... | collective-permute-start | bytes 2654216 | tf_op jit(solution)/shard_map/ppermute | solution.py:52
  73.1 1.2 %constant_dynamic-update-slice_fusion.1 = f32[3,8,24,768]{3,2,1,0:T(8,128)S(1)} fusion(f32[3,4,24,768]{3,2,1,0:T(8,128)} %collective-permute-done.2), kind=kLoop, calls=%fused_computation.31 | loop fusion | bytes 1769472
  74.4 20.4 %collective-permute-done.1 = f32[3,4,24,768]{3,2,1,0:T(8,128)S(1)} collective-permute-done((f32[3,4,24,768]{3,2,1,0:T(8,128)S(1)}, f32[3,4,24,768]{3,2,1,0:T(8,128)S(1)}, u32[]{:S(2)}, u32[]{:S(2)}) %collective-permute-start.1) | collective-permute-done | bytes 884768 | tf_op jit(solution)/shard_map/ppermute | solution.py:52
  94.9 3.1 %multiply_add_fusion.p_ref = f32[3,4,24,768]{3,2,1,0:T(8,128)} fusion(f32[3,4,24,768]{3,2,1,0:T(8,128)S(1)} %copy-done.4, f32[3,4,24,768]{3,2,1,0:T(8,128)S(1)} %broadcast_select_fusion, f32[3,4,24,768]{3,2,1,0:T(8,128)} %collective-permute-done.2, f32[3,4,24,768]{3,2,1,0:T(8,128)S(1)} %copy-done, ...), kind=kLoop, calls=%fused_computation.13 | loop fusion | flops 7741440 | bytes 8257536 | tf_op jit(solution)/shard_map/add | solution.py:159
  98.0 0.3 all-to-all-done.1.b_ref
  98.3 1.0 copy-done.3
  99.3 3.7 %shard_map.115 = (f32[3,4,24,768]{3,2,1,0:T(8,128)}, f32[3,4,24,768]{3,2,1,0:T(8,128)}) custom-call(f32[3,4,24,768]{3,2,1,0:T(8,128)} %v_ref.3, f32[3,4,24,768]{3,2,1,0:T(8,128)} %multiply_add_fusion.p_ref, f32[16,24,576]{2,1,0:T(8,128)} %copy-done.3), custom_call_target="tpu_custom_call" | custom-call | tf_op jit(solution)/shard_map/pallas_call | solution.py:171
  (32 shorter events, 0.6 us)
Async XLA Ops:
  0.6 15.2 %copy-start = (f32[3,4,24,768]{3,2,1,0:T(8,128)S(1)}, f32[3,4,24,768]{3,2,1,0:T(8,128)}, u32[]{:S(2)}) copy-start(f32[3,4,24,768]{3,2,1,0:T(8,128)} %v_ref.3) | copy-start | bytes 2654212
  0.6 14.8 %copy-start.9 = (s32[384]{0:T(512)S(1)}, s32[384]{0:T(512)}, u32[]{:S(2)}) copy-start(s32[384]{0:T(512)} %param.15) | copy-start | bytes 4612
  0.7 14.8 %copy-start.10 = (f32[64]{0:T(128)S(1)}, f32[64]{0:T(128)}, u32[]{:S(2)}) copy-start(f32[64]{0:T(128)} %param.16) | copy-start | bytes 772
  0.7 14.9 %copy-start.6 = (s32[384]{0:T(512)S(1)}, s32[384]{0:T(512)}, u32[]{:S(2)}) copy-start(s32[384]{0:T(512)} %param.14) | copy-start | bytes 4612
  3.6 38.4 %all-to-all-start = ((f32[16,24,576]{2,1,0:T(8,128)}), f32[16,24,576]{2,1,0:T(8,128)S(1)}, u32[]{:S(2)}, u32[]{:S(2)}) async-start(f32[16,24,576]{2,1,0:T(8,128)} %shard_map.113), calls=%async_computation | async-start | bytes 1966080 | tf_op jit(solution)/shard_map/all_to_all | solution.py:184
  15.9 57.2 %collective-permute-start.2 = (f32[3,4,24,768]{3,2,1,0:T(8,128)S(1)}, f32[3,4,24,768]{3,2,1,0:T(8,128)}, u32[]{:S(2)}, u32[]{:S(2)}) collective-permute-start(f32[3,4,24,768]{3,2,1,0:T(8,128)S(1)} %copy-done), channel_id=1, source_target_pairs={{0,16},{16,32},{32,48},{48,64},{64,80},{80,96},{96,112},{112,128},... | collective-permute-start | bytes 2654216 | tf_op jit(solution)/shard_map/ppermute | solution.py:51
  42.0 2.1 %copy-start.1 = (f32[16,24,576]{2,1,0:T(8,128)}, f32[16,24,576]{2,1,0:T(8,128)S(1)}, u32[]{:S(2)}) copy-start(f32[16,24,576]{2,1,0:T(8,128)S(1)} %all-to-all-done) | copy-start | bytes 2654212
  44.1 15.3 %collective-permute-start = (f32[384,144]{1,0:T(8,128)S(1)}, f32[384,144]{1,0:T(8,128)}, u32[]{:S(2)}, u32[]{:S(2)}) collective-permute-start(f32[384,144]{1,0:T(8,128)S(1)} %fusion.6), channel_id=1, source_target_pairs={{496,0},{497,1},{498,2},{499,3},{500,4},{501,5},{502,6},{503,7},{5... | collective-permute-start | bytes 663560 | tf_op jit(solution)/shard_map/ppermute | solution.py:196
  60.8 3.7 %copy-start.2 = (f32[384,576]{1,0:T(8,128)S(1)}, f32[384,576]{1,0:T(8,128)}, u32[]{:S(2)}) copy-start(f32[384,576]{1,0:T(8,128)} %shard_map.114) | copy-start | bytes 2654212
  60.8 3.7 %copy-start.7 = (f32[576]{0:T(1024)S(1)}, f32[576]{0:T(1024)}, u32[]{:S(2)}) copy-start(f32[576]{0:T(1024)} %constant.47) | copy-start | bytes 6916
  60.8 3.7 %copy-start.8 = (f32[576]{0:T(1024)S(1)}, f32[576]{0:T(1024)}, u32[]{:S(2)}) copy-start(f32[576]{0:T(1024)} %constant.48) | copy-start | bytes 6916
  67.0 31.3 %all-to-all-start.1 = ((f32[16,24,576]{2,1,0:T(8,128)}), f32[16,24,576]{2,1,0:T(8,128)S(1)}, u32[]{:S(2)}, u32[]{:S(2)}) async-start(f32[16,24,576]{2,1,0:T(8,128)} %bitcast.7), calls=%async_computation.1 | async-start | bytes 1966080 | tf_op jit(solution)/shard_map/all_to_all | solution.py:220
  71.7 23.1 %collective-permute-start.1 = (f32[3,4,24,768]{3,2,1,0:T(8,128)S(1)}, f32[3,4,24,768]{3,2,1,0:T(8,128)S(1)}, u32[]{:S(2)}, u32[]{:S(2)}) collective-permute-start(f32[3,4,24,768]{3,2,1,0:T(8,128)S(1)} %copy-done), channel_id=1, source_target_pairs={{16,0},{32,16},{48,32},{64,48},{80,64},{96,80},{112,96},{128,112},... | collective-permute-start | bytes 2654216 | tf_op jit(solution)/shard_map/ppermute | solution.py:52
  74.3 20.6 %copy-start.4 = (f32[3,4,24,768]{3,2,1,0:T(8,128)S(1)}, f32[3,4,24,768]{3,2,1,0:T(8,128)}, u32[]{:S(2)}) copy-start(f32[3,4,24,768]{3,2,1,0:T(8,128)} %negate_add_fusion) | copy-start | bytes 2654212
  74.3 20.6 %copy-start.5 = (f32[3,4,24,768]{3,2,1,0:T(8,128)S(1)}, f32[3,4,24,768]{3,2,1,0:T(8,128)}, u32[]{:S(2)}) copy-start(f32[3,4,24,768]{3,2,1,0:T(8,128)} %param.11) | copy-start | bytes 2654212
  98.3 1.0 copy-start.3

commit v15 on v13

--- a/solution.py
+++ b/solution.py
@@ -146,7 +146,9 @@
     return pl.pallas_call(
         kernel,
         out_shape=jax.ShapeDtypeStruct((rows, width), jnp.float32),
-        in_specs=[pl.BlockSpec(memory_space=pltpu.SMEM)] + [vmem] * 5,
+        in_specs=[pl.BlockSpec(memory_space=pltpu.SMEM), vmem, pl.BlockSpec((rows, 256), lambda i: (0, 0))]
+        + [vmem] * 3,
+        grid=(1,),
         input_output_aliases={1: 0},
     )(inlet, wall, cols, inflow, jnp.asarray(gain, jnp.float32), jnp.asarray(bias, jnp.float32))
 
@@ -192,7 +194,7 @@
         [cols[:, (c * planes + source_plane) * share : (c * planes + source_plane + 1) * share] for c in range(comps)],
         axis=1,
     )
-    inflow = jnp.dot(mix, plane, precision=HIGHEST, preferred_element_type=jnp.float32)
+    inflow = jnp.dot(mix, plane, precision=lax.Precision.HIGH, preferred_element_type=jnp.float32)
     inflow = lax.ppermute(inflow, "gx", [(source_slab, 0)])
 
     wall = wall_block(cols, wall_first, wall_second, planes)

time: 98.4 us -> 97.9 us (level)
  no operation moved by 1% of the time
where the time goes in v15:
time: 97.9 us; the launch traced here: 97.3 us
  waiting for transfers between devices  43.5 us (44%)
  starting transfers between devices  23.2 us (24%)
  Pallas kernels  16.2 us (17%)
  other arithmetic  5.56 us (6%)
  matrix products  5.53 us (6%)
  local copies, waits for them, and re-layouts  2.45 us (3%)
    all_to_all x1, waiting for transfers between devices, shards(): cols = lax.all_to_all(send, 'ga', 0, 0, tiled=True).reshape(rows, width)  22.1 us
    ppermute x1, waiting for transfers between devices, halo_planes(): ahead = lax.ppermute(field, 'gx', [(i + 1, i) for i in range(count - 1)])  20.4 us
    all_to_all x1, starting transfers between devices, shards(): cols = lax.all_to_all(send, 'ga', 0, 0, tiled=True).reshape(rows, width)  11.8 us
    pallas_call x1, Pallas kernels, wall_block(): pl.pallas_call(kernel, out_shape=jax.ShapeDtypeStruct((rows, width), jnp....  6.48 us
    dot_general x1, matrix products, shards(): jnp.dot(lines, jnp.asarray(spanwise_table(span)), precision=lax.Precision...  4.84 us
    all_to_all x1, starting transfers between devices, shards(): lax.all_to_all(wall.reshape(parts, rows_here, width), 'ga', 0, 0, tiled=T...  4.73 us
    ppermute x1, starting transfers between devices, halo_planes(): behind = lax.ppermute(field, 'gx', [(i, i + 1) for i in range(count - 1)])  4.06 us
    pallas_call x1, Pallas kernels, combine(): pl.pallas_call(kernel, out_shape=(shape, shape))(velocity, partial, back)  3.67 us
  transfers between devices with their start and end apart: 5, of which 4 were waited for; matrix products, arithmetic and copies ran while one was open for 13% of the time, Pallas kernels for 10%

profile of v15, /device:TPU:1, one launch (start us, length us, event | category | flops | bytes accessed | tf_op | source)
XLA Modules:
  0.0 97.3 jit_solution(9695797788916373705)
XLA Ops:
  0.7 3.0 %shard_map.113 = f32[16,24,576]{2,1,0:T(8,128)} custom-call(f32[3,4,24,768]{3,2,1,0:T(8,128)} %v_ref.3), custom_call_target="tpu_custom_call" | custom-call | tf_op jit(solution)/shard_map/pallas_call | solution.py:94
  3.6 11.8 %all-to-all-start = ((f32[16,24,576]{2,1,0:T(8,128)}), f32[16,24,576]{2,1,0:T(8,128)S(1)}, u32[]{:S(2)}, u32[]{:S(2)}) async-start(f32[16,24,576]{2,1,0:T(8,128)} %shard_map.113), calls=%async_computation | async-start | bytes 1966080 | tf_op jit(solution)/shard_map/all_to_all | solution.py:186
  15.5 0.1 select_reduce_fusion
  15.6 0.3 select_add_fusion
  15.9 4.1 %collective-permute-start.2 = (f32[3,4,24,768]{3,2,1,0:T(8,128)S(1)}, f32[3,4,24,768]{3,2,1,0:T(8,128)}, u32[]{:S(2)}, u32[]{:S(2)}) collective-permute-start(f32[3,4,24,768]{3,2,1,0:T(8,128)S(1)} %copy-done), channel_id=1, source_target_pairs={{0,16},{16,32},{32,48},{48,64},{64,80},{80,96},{96,112},{112,128},... | collective-permute-start | bytes 2654216 | tf_op jit(solution)/shard_map/ppermute | solution.py:51
  20.0 22.1 %all-to-all-done = f32[16,24,576]{2,1,0:T(8,128)S(1)} async-done(((f32[16,24,576]{2,1,0:T(8,128)}), f32[16,24,576]{2,1,0:T(8,128)S(1)}, u32[]{:S(2)}, u32[]{:S(2)}) %all-to-all-start) | async-done | bytes 884768 | tf_op jit(solution)/shard_map/all_to_all | solution.py:186
  42.1 0.1 fusion.10
  42.2 0.7 fusion.2
  42.9 1.3 %collective-permute-start = (f32[384,144]{1,0:T(8,128)S(1)}, f32[384,144]{1,0:T(8,128)}, u32[]{:S(2)}, u32[]{:S(2)}) collective-permute-start(f32[384,144]{1,0:T(8,128)S(1)} %fusion.2), channel_id=1, source_target_pairs={{496,0},{497,1},{498,2},{499,3},{500,4},{501,5},{502,6},{503,7},{5... | collective-permute-start | bytes 663560 | tf_op jit(solution)/shard_map/ppermute | solution.py:198
  44.2 4.8 %fusion.11 = f32[288,1536]{1,0:T(8,128)S(1)} fusion(f32[288,768]{1,0:T(8,128)S(1)} %bitcast.15, f32[768,1536]{1,0:T(8,128)} %constant.42.clone), kind=kOutput, calls=%fused_computation.32 | convolution fusion | flops 2038431744 | bytes 7372800 | tf_op jit(solution)/shard_map/dot_general | solution.py:202
  49.1 1.0 %fusion.9 = (f32[288,768]{1,0:T(8,128)S(1)}, f32[288,768]{1,0:T(8,128)}) fusion(f32[288,1536]{1,0:T(8,128)S(1)} %fusion.11), kind=kLoop, calls=%fused_computation.30 | loop fusion | flops 221184 | bytes 3538944 | tf_op jit(solution)/shard_map/slice | solution.py:208
  50.1 6.5 %shard_map.114.w_ref = f32[384,576]{1,0:T(8,128)} custom-call(f32[384,576]{1,0:T(8,128)} %bitcast.17, f32[384,384]{1,0:T(8,128)} %f_ref.1, f32[384,384]{1,0:T(8,128)} %s_ref.1), custom_call_target="tpu_custom_call" | custom-call | tf_op jit(solution)/shard_map/pallas_call | solution.py:114
  56.6 1.0 %negate_add_fusion = f32[3,4,24,768]{3,2,1,0:T(8,128)} fusion(f32[3,4,24,768]{3,2,1,0:T(8,128)S(1)} %bitcast.21, f32[3,4,24,768]{3,2,1,0:T(8,128)S(1)} %bitcast.20, f32[4,24,768]{2,1,0:T(8,128)S(1)} %slice_bitcast_fusion.1), kind=kLoop, calls=%fused_computation.9 | loop fusion | flops 663552 | bytes 2949120 | tf_op jit(solution)/shard_map/add | solution.py:210
  57.6 0.6 collective-permute-done.f_ref
  58.2 3.1 %shard_map.115 = f32[384,576]{1,0:T(8,128)} custom-call(s32[1]{0:T(128)} %bitcast.7.inlet_ref, f32[384,576]{1,0:T(8,128)} %shard_map.114.w_ref, f32[384,576]{1,0:T(8,128)} %bitcast.18, f32[384,144]{1,0:T(8,128)} %collective-permute-done.f_ref, f32[1,576]{1,0:T(1,128)} %constant.43.clone.g_ref, ...), custom_call_target="tpu_custom_call", output_to_operand_aliasing={{}: (1, {})} | custom-call | tf_op jit(solution)/shard_map/pallas_call | solution.py:146
  61.3 4.7 %all-to-all-start.1 = ((f32[16,24,576]{2,1,0:T(8,128)}), f32[16,24,576]{2,1,0:T(8,128)S(1)}, u32[]{:S(2)}, u32[]{:S(2)}) async-start(f32[16,24,576]{2,1,0:T(8,128)} %bitcast.19), calls=%async_computation.1 | async-start | bytes 1966080 | tf_op jit(solution)/shard_map/all_to_all | solution.py:215
  66.1 1.3 %collective-permute-start.1 = (f32[3,4,24,768]{3,2,1,0:T(8,128)S(1)}, f32[3,4,24,768]{3,2,1,0:T(8,128)S(1)}, u32[]{:S(2)}, u32[]{:S(2)}) collective-permute-start(f32[3,4,24,768]{3,2,1,0:T(8,128)S(1)} %copy-done), channel_id=1, source_target_pairs={{16,0},{32,16},{48,32},{64,48},{80,64},{96,80},{112,96},{128,112},... | collective-permute-start | bytes 2654216 | tf_op jit(solution)/shard_map/ppermute | solution.py:52
  67.4 1.2 %constant_dynamic-update-slice_fusion.1 = f32[3,8,24,768]{3,2,1,0:T(8,128)S(1)} fusion(f32[3,4,24,768]{3,2,1,0:T(8,128)} %collective-permute-done.2), kind=kLoop, calls=%fused_computation.26 | loop fusion | bytes 1769472
  68.8 20.4 %collective-permute-done.1 = f32[3,4,24,768]{3,2,1,0:T(8,128)S(1)} collective-permute-done((f32[3,4,24,768]{3,2,1,0:T(8,128)S(1)}, f32[3,4,24,768]{3,2,1,0:T(8,128)S(1)}, u32[]{:S(2)}, u32[]{:S(2)}) %collective-permute-start.1) | collective-permute-done | bytes 884768 | tf_op jit(solution)/shard_map/ppermute | solution.py:52
  89.2 0.1 broadcast_select_fusion
  89.3 3.1 %multiply_add_fusion.p_ref = f32[3,4,24,768]{3,2,1,0:T(8,128)} fusion(f32[3,4,24,768]{3,2,1,0:T(8,128)S(1)} %copy-done.4, f32[3,4,24,768]{3,2,1,0:T(8,128)S(1)} %broadcast_select_fusion, f32[3,4,24,768]{3,2,1,0:T(8,128)} %collective-permute-done.2, f32[3,4,24,768]{3,2,1,0:T(8,128)S(1)} %copy-done, f32[3,8,24,768]{3,2,1,0:T(8,128)S(1)} %constant_dynamic-update-slice_fusion, ...), kind=kLoop, calls=%fused_computation.8 | loop fusion | flops 7741440 | bytes 8257536 | tf_op jit(solution)/shard_map/add | solution.py:161
  92.3 0.3 all-to-all-done.1.b_ref
  92.7 0.9 copy-done.2
  93.6 3.7 %shard_map.116 = (f32[3,4,24,768]{3,2,1,0:T(8,128)}, f32[3,4,24,768]{3,2,1,0:T(8,128)}) custom-call(f32[3,4,24,768]{3,2,1,0:T(8,128)} %v_ref.3, f32[3,4,24,768]{3,2,1,0:T(8,128)} %multiply_add_fusion.p_ref, f32[16,24,576]{2,1,0:T(8,128)} %copy-done.2), custom_call_target="tpu_custom_call" | custom-call | tf_op jit(solution)/shard_map/pallas_call | solution.py:173
  (24 shorter events, 0.2 us)
Async XLA Ops:
  0.6 15.3 %copy-start = (f32[3,4,24,768]{3,2,1,0:T(8,128)S(1)}, f32[3,4,24,768]{3,2,1,0:T(8,128)}, u32[]{:S(2)}) copy-start(f32[3,4,24,768]{3,2,1,0:T(8,128)} %v_ref.3) | copy-start | bytes 2654212
  0.6 14.8 %copy-start.7 = (s32[384]{0:T(512)S(1)}, s32[384]{0:T(512)}, u32[]{:S(2)}) copy-start(s32[384]{0:T(512)} %param.15) | copy-start | bytes 4612
  0.7 14.8 %copy-start.8 = (f32[64]{0:T(128)S(1)}, f32[64]{0:T(128)}, u32[]{:S(2)}) copy-start(f32[64]{0:T(128)} %param.16) | copy-start | bytes 772
  0.7 14.9 %copy-start.6 = (s32[384]{0:T(512)S(1)}, s32[384]{0:T(512)}, u32[]{:S(2)}) copy-start(s32[384]{0:T(512)} %param.14) | copy-start | bytes 4612
  3.6 38.4 %all-to-all-start = ((f32[16,24,576]{2,1,0:T(8,128)}), f32[16,24,576]{2,1,0:T(8,128)S(1)}, u32[]{:S(2)}, u32[]{:S(2)}) async-start(f32[16,24,576]{2,1,0:T(8,128)} %shard_map.113), calls=%async_computation | async-start | bytes 1966080 | tf_op jit(solution)/shard_map/all_to_all | solution.py:186
  15.9 51.5 %collective-permute-start.2 = (f32[3,4,24,768]{3,2,1,0:T(8,128)S(1)}, f32[3,4,24,768]{3,2,1,0:T(8,128)}, u32[]{:S(2)}, u32[]{:S(2)}) collective-permute-start(f32[3,4,24,768]{3,2,1,0:T(8,128)S(1)} %copy-done), channel_id=1, source_target_pairs={{0,16},{16,32},{32,48},{48,64},{64,80},{80,96},{96,112},{112,128},... | collective-permute-start | bytes 2654216 | tf_op jit(solution)/shard_map/ppermute | solution.py:51
  42.1 7.0 %copy-start.1 = (f32[16,24,576]{2,1,0:T(8,128)}, f32[16,24,576]{2,1,0:T(8,128)S(1)}, u32[]{:S(2)}) copy-start(f32[16,24,576]{2,1,0:T(8,128)S(1)} %all-to-all-done) | copy-start | bytes 2654212
  42.9 15.3 %collective-permute-start = (f32[384,144]{1,0:T(8,128)S(1)}, f32[384,144]{1,0:T(8,128)}, u32[]{:S(2)}, u32[]{:S(2)}) collective-permute-start(f32[384,144]{1,0:T(8,128)S(1)} %fusion.2), channel_id=1, source_target_pairs={{496,0},{497,1},{498,2},{499,3},{500,4},{501,5},{502,6},{503,7},{5... | collective-permute-start | bytes 663560 | tf_op jit(solution)/shard_map/ppermute | solution.py:198
  50.1 6.5 %copy-start.3 = (f32[288,768]{1,0:T(8,128)S(1)}, f32[288,768]{1,0:T(8,128)}, u32[]{:S(2)}) copy-start(f32[288,768]{1,0:T(8,128)} %get-tuple-element.19) | copy-start | bytes 2654212
  61.3 31.3 %all-to-all-start.1 = ((f32[16,24,576]{2,1,0:T(8,128)}), f32[16,24,576]{2,1,0:T(8,128)S(1)}, u32[]{:S(2)}, u32[]{:S(2)}) async-start(f32[16,24,576]{2,1,0:T(8,128)} %bitcast.19), calls=%async_computation.1 | async-start | bytes 1966080 | tf_op jit(solution)/shard_map/all_to_all | solution.py:215
  66.1 23.1 %collective-permute-start.1 = (f32[3,4,24,768]{3,2,1,0:T(8,128)S(1)}, f32[3,4,24,768]{3,2,1,0:T(8,128)S(1)}, u32[]{:S(2)}, u32[]{:S(2)}) collective-permute-start(f32[3,4,24,768]{3,2,1,0:T(8,128)S(1)} %copy-done), channel_id=1, source_target_pairs={{16,0},{32,16},{48,32},{64,48},{80,64},{96,80},{112,96},{128,112},... | collective-permute-start | bytes 2654216 | tf_op jit(solution)/shard_map/ppermute | solution.py:52
  68.7 20.6 %copy-start.4 = (f32[3,4,24,768]{3,2,1,0:T(8,128)S(1)}, f32[3,4,24,768]{3,2,1,0:T(8,128)}, u32[]{:S(2)}) copy-start(f32[3,4,24,768]{3,2,1,0:T(8,128)} %negate_add_fusion) | copy-start | bytes 2654212
  68.7 20.6 %copy-start.5 = (f32[3,4,24,768]{3,2,1,0:T(8,128)S(1)}, f32[3,4,24,768]{3,2,1,0:T(8,128)}, u32[]{:S(2)}) copy-start(f32[3,4,24,768]{3,2,1,0:T(8,128)} %param.11) | copy-start | bytes 2654212
  92.7 0.9 copy-start.2
